TPU v7x, 512 devices: a whole 4x4x16 slice. The times are simulated.
512 devices in a mesh: ctx: 64 (over x_hi, z, core), head: 8 (over x_lo, y).
Axes of the slice: x: 4 (x_hi: 2, x_lo: 2; x = x_hi * 2 + x_lo), y: 4, z: 16, core: 2. Of those that a mesh axis runs over, the one named last changes fastest.
Arguments:
- q_latent: bfloat16 [8192, 64, 512], P('ctx', 'head'), may hold values from -1.25 to 1.25
- q_rope: bfloat16 [8192, 4096], P('ctx', 'head'), may hold values from -1.25 to 1.25
- attn_out: bfloat16 [8192, 64, 512], P('ctx', 'head'), may hold values from -4 to 4
- grad_out: bfloat16 [8192, 64, 512], P('ctx', 'head'), may hold values from -1 to 1
- log_total: float32 [8192, 64], P('ctx', 'head'), may hold values from 4 to 6
- latent: bfloat16 [8192, 512], P('ctx'), may hold values from -2.5 to 2.5
- key_rope: bfloat16 [8192, 64], P('ctx'), may hold values from -2.5 to 2.5
- doc_start: int32 [8192], P('ctx'), may hold values from 0 to 8191, as said below
Outputs:
- grad_q_latent: bfloat16 [8192, 64, 512], P('ctx', 'head')
- grad_q_rope: bfloat16 [8192, 4096], P('ctx', 'head')
- grad_latent: bfloat16 [8192, 512], P(('ctx', 'head'))
- grad_key_rope: bfloat16 [8192, 64], P(('ctx', 'head'))
Inputs may be any that keep to these rules, and one draw needn't show every extreme that they name: doc_start[t] is the first token of the document that holds token t. Documents are runs of 1 to 897 tokens laid end to end from token 0; one document has exactly 897 tokens, and the last token of the sequence is a document of its own.
All inputs are finite; a program needn't handle non-finite values.
Results may differ from a plain program's by a relative error of at most 0.0056.
Values may be sent and summed in bfloat16 or wider, within the bound.
No kernel may reach another device: no remote copies, remote signals or barrier semaphores. Data moves between devices by JAX's collectives and lax.ppermute only.
A program may use at most 64 MiB of HBM per device.

v0:
```python
import jax
import jax.numpy as jnp
from jax import lax
from jax.sharding import PartitionSpec as P

ROPE = 64
NOPE = 128
LEVELS = 3


def shifted(x, axis, by):
    count = lax.axis_size(axis)
    pairs = [(i, i + by) for i in range(count) if 0 <= i + by < count]
    return lax.ppermute(x, axis, pairs)


def shifted_2(x, axis, by):
    count = lax.axis_size(axis)
    return lax.ppermute(x, axis, [(i, (i + by) % count) for i in range(count)])


def tile_terms(
    q_latent,
    q_rot,
    grad_out,
    row_delta,
    log_total,
    doc_start,
    query_pos,
    earliest,
    latent_blk,
    rope_blk,
    key_tile,
):
    tok_rows = latent_blk.shape[0]
    head_count = q_latent.shape[1]
    key_first = key_tile * tok_rows
    softmax_scale = (NOPE + ROPE) ** (-0.5)

    def compute(unused):
        key_pos = key_first + jnp.arange(tok_rows, dtype=jnp.int32)
        visible = (
            (key_pos[None, :] >= doc_start[:, None]) & (key_pos[None, :] <= query_pos[:, None])
        )[:, None, :]
        scores = (
            jnp.einsum("thc,kc->thk", q_latent, latent_blk, preferred_element_type=jnp.float32)
            + jnp.einsum("thr,kr->thk", q_rot, rope_blk, preferred_element_type=jnp.float32)
        ) * softmax_scale
        probs = jnp.where(
            visible, jnp.exp(jnp.where(visible, scores, 0.0) - log_total[:, :, None]), 0.0
        )
        grad_probs = jnp.einsum(
            "thc,kc->thk", grad_out, latent_blk, preferred_element_type=jnp.float32
        )
        grad_scores = probs * (grad_probs - row_delta[:, :, None])
        probs_b = probs.astype(jnp.bfloat16)
        grad_b = grad_scores.astype(jnp.bfloat16)
        grad_qlat = softmax_scale * jnp.einsum(
            "thk,kc->thc", grad_b, latent_blk, preferred_element_type=jnp.float32
        )
        grad_qrot = softmax_scale * jnp.einsum(
            "thk,kr->thr", grad_b, rope_blk, preferred_element_type=jnp.float32
        )
        grad_lat = softmax_scale * jnp.einsum(
            "thk,thc->kc", grad_b, q_latent, preferred_element_type=jnp.float32
        ) + jnp.einsum("thk,thc->kc", probs_b, grad_out, preferred_element_type=jnp.float32)
        grad_rot = softmax_scale * jnp.einsum(
            "thk,thr->kr", grad_b, q_rot, preferred_element_type=jnp.float32
        )
        return (grad_qlat, grad_qrot, grad_lat, grad_rot)

    def skipped(unused):
        return (
            jnp.zeros((tok_rows, head_count, latent_blk.shape[1]), jnp.float32),
            jnp.zeros((tok_rows, head_count, rope_blk.shape[1]), jnp.float32),
            jnp.zeros(latent_blk.shape, jnp.float32),
            jnp.zeros(rope_blk.shape, jnp.float32),
        )

    return lax.cond(earliest <= key_first + tok_rows - 1, compute, skipped, 0)


def share_groups(pair):
    return lax.psum_scatter(pair, "head", scatter_dimension=1, tiled=True)


def local(q_latent, q_rope, attn_out, grad_out, log_total, latent, key_rope, doc_start):
    tok_rows, head_count, lat_width = q_latent.shape
    rope_width = key_rope.shape[1]
    span = 2**LEVELS
    q_rot = q_rope.reshape(tok_rows, head_count, rope_width)
    row_delta = jnp.einsum("thc,thc->th", grad_out, attn_out, preferred_element_type=jnp.float32)
    own_tile = lax.axis_index("ctx")
    query_pos = own_tile * tok_rows + jnp.arange(tok_rows, dtype=jnp.int32)
    earliest = jnp.min(doc_start)

    def terms_for(latent_blk, rope_blk, key_tile):
        return tile_terms(
            q_latent,
            q_rot,
            grad_out,
            row_delta,
            log_total,
            doc_start,
            query_pos,
            earliest,
            latent_blk,
            rope_blk,
            key_tile,
        )

    first = terms_for(latent, key_rope, own_tile)

    def cycle_turn(step_index, state):
        latent_blk, rope_blk, sum_latent, sum_rope, grad_qlat, grad_qrot = state
        latent_blk, rope_blk = shifted((latent_blk, rope_blk), "ctx", 1)
        sum_latent, sum_rope = shifted_2((sum_latent, sum_rope), "ctx", 1)
        terms = terms_for(latent_blk, rope_blk, own_tile - step_index)
        return (
            latent_blk,
            rope_blk,
            sum_latent + terms[2][None],
            sum_rope + terms[3][None],
            grad_qlat + terms[0],
            grad_qrot + terms[1],
        )

    state = (latent, key_rope, first[2][None], first[3][None], first[0], first[1])
    state = lax.fori_loop(1, span, cycle_turn, state)
    grad_qlat, grad_qrot = (state[4], state[5])
    owned = (state[2], state[3])
    owned = shifted_2(owned, "ctx", 1 - span)
    owned = share_groups(owned)
    return (
        grad_qlat.astype(jnp.bfloat16),
        grad_qrot.reshape(tok_rows, head_count * rope_width).astype(jnp.bfloat16),
        owned[0][0].astype(jnp.bfloat16),
        owned[1][0].astype(jnp.bfloat16),
    )


def solution(mesh):
    in_specs = (
        P("ctx", "head", None),
        P("ctx", "head"),
        P("ctx", "head", None),
        P("ctx", "head", None),
        P("ctx", "head"),
        P("ctx", None),
        P("ctx", None),
        P("ctx"),
    )
    out_specs = (
        P("ctx", "head", None),
        P("ctx", "head"),
        P(("ctx", "head"), None),
        P(("ctx", "head"), None),
    )
    return jax.shard_map(local, mesh=mesh, in_specs=in_specs, out_specs=out_specs, check_vma=False)
```

profile of v0, /device:TPU:6, one launch (start us, length us, event | category | flops | bytes accessed | tf_op | source)
XLA Modules:
  0.0 353.9 jit_solution(18413513900037086746)
XLA Ops:
  18.2 10.1 %conditional.2 = (f32[128,8,512]{2,0,1:T(8,128)S(1)}, f32[128,8,64]{0,2,1:T(8,128)S(1)}, f32[1,128,512]{2,1,0:T(8,128)}, f32[1,128,64]{1,2,0:T(8,128)}) conditional(s32[]{:T(128)} %convert_element_type.49, () %tuple.62, (s32[]{:T(128)}, s32[128]{0:T(128)}, s32[]{:T(128)}, bf16[128,8,512]{2,1,0:T(8,128)(2,1)S(1)}, bf16[128,512]{1,0:T(8,128)(2,1)S(1)}, ...), branch_computations={%region_1.0_spmd, %region_2.3_spmd} | conditional | flops 723378432 | bytes 12037160 | solution.py:80
  29.8 194.1 %while.28 = (s32[]{:T(128)}, bf16[128,512]{1,0:T(8,128)(2,1)S(1)}, bf16[128,64]{0,1:T(8,128)(2,1)}, f32[1,128,512]{2,1,0:T(8,128)}, f32[1,128,64]{1,2,0:T(8,128)...) while((s32[]{:T(128)}, bf16[128,512]{1,0:T(8,128)(2,1)S(1)}, ...), condition=%wide.region_6.7_spmd.clone, body=%wide.region_3.6_spmd.clone.sunk | while | flops 724041984 | bytes 28618892 | solution.py:129
  31.7 3.9 %collective-permute-start = (bf16[128,512]{1,0:T(8,128)(2,1)S(1)}, bf16[128,512]{1,0:T(8,128)(2,1)S(1)}, u32[]{:S(2)}, u32[]{:S(2)}) collective-permute-start(bf16[128,512]{1,0:T(8,128)(2,1)S(1)} %get-tuple-element.864), channel_id=1, source_target_pairs={{0,8},{8,16},{16,24},{24,32},{32,40},{40,48},{48,56},{56,64},{64,7... | collective-permute-start | bytes 393224 | tf_op jit(solution)/shard_map/while/body/eval_jaxpr/ppermute | solution.py:14
  37.5 3.9 %collective-permute-start.1 = (bf16[128,64]{0,1:T(8,128)(2,1)}, bf16[128,64]{0,1:T(8,128)(2,1)S(1)}, u32[]{:S(2)}, u32[]{:S(2)}) collective-permute-start(bf16[128,64]{0,1:T(8,128)(2,1)} %get-tuple-element.865), channel_id=1, source_target_pairs={{0,8},{8,16},{16,24},{24,32},{32,40},{40,48},{48,56},{56,64},{64,7... | collective-permute-start | bytes 49160 | tf_op jit(solution)/shard_map/while/body/eval_jaxpr/ppermute | solution.py:14
  42.0 6.8 %collective-permute-done.1 = bf16[128,64]{0,1:T(8,128)(2,1)S(1)} collective-permute-done((bf16[128,64]{0,1:T(8,128)(2,1)}, bf16[128,64]{0,1:T(8,128)(2,1)S(1)}, u32[]{:S(2)}, u32[]{:S(2)}) %collective-permute-start.1) | collective-permute-done | bytes 16416 | tf_op jit(solution)/shard_map/while/body/eval_jaxpr/ppermute | solution.py:14
  49.5 7.9 %conditional.5 = (f32[128,8,512]{2,0,1:T(8,128)S(1)}, f32[128,8,64]{0,2,1:T(8,128)S(1)}, f32[1,128,512]{2,1,0:T(8,128)}, f32[1,128,64]{1,2,0:T(8,128)S(1)}) conditional(s32[]{:T(128)} %convert_element_type.68, () %tuple.88, (s32[]{:T(128)}, s32[128]{0:T(128)}, s32[]{:T(128)}, bf16[128,8,512]{2,0,1:T(8,128)(2,1)}, bf16[128,512]{1,0:T(8,128)(2,1)S(1)}, ...), branch_computations={%region_4.4_spmd, %region_5.5_spmd} | conditional | flops 723378432 | bytes 16231492 | solution.py:80
  73.0 6.4 %collective-permute-done.1 = bf16[128,64]{0,1:T(8,128)(2,1)S(1)} collective-permute-done((bf16[128,64]{0,1:T(8,128)(2,1)}, bf16[128,64]{0,1:T(8,128)(2,1)S(1)}, u32[]{:S(2)}, u32[]{:S(2)}) %collective-permute-start.1) | collective-permute-done | bytes 16416 | tf_op jit(solution)/shard_map/while/body/eval_jaxpr/ppermute | solution.py:14
  90.4 4.5 %collective-permute-start = (bf16[128,512]{1,0:T(8,128)(2,1)S(1)}, bf16[128,512]{1,0:T(8,128)(2,1)S(1)}, u32[]{:S(2)}, u32[]{:S(2)}) collective-permute-start(bf16[128,512]{1,0:T(8,128)(2,1)S(1)} %get-tuple-element.864), channel_id=1, source_target_pairs={{0,8},{8,16},{16,24},{24,32},{32,40},{40,48},{48,56},{56,64},{64,7... | collective-permute-start | bytes 393224 | tf_op jit(solution)/shard_map/while/body/eval_jaxpr/ppermute | solution.py:14
  96.8 4.8 %collective-permute-start.1 = (bf16[128,64]{0,1:T(8,128)(2,1)}, bf16[128,64]{0,1:T(8,128)(2,1)S(1)}, u32[]{:S(2)}, u32[]{:S(2)}) collective-permute-start(bf16[128,64]{0,1:T(8,128)(2,1)} %get-tuple-element.865), channel_id=1, source_target_pairs={{0,8},{8,16},{16,24},{24,32},{32,40},{40,48},{48,56},{56,64},{64,7... | collective-permute-start | bytes 49160 | tf_op jit(solution)/shard_map/while/body/eval_jaxpr/ppermute | solution.py:14
  118.5 8.5 %collective-permute-start.3 = (f32[1,128,64]{1,2,0:T(8,128)}, f32[1,128,64]{1,2,0:T(8,128)}, u32[]{:S(2)}, u32[]{:S(2)}) collective-permute-start(f32[1,128,64]{1,2,0:T(8,128)} %get-tuple-element.867), channel_id=1, source_target_pairs={{0,8},{8,16},{16,24},{24,32},{32,40},{40,48},{48,56},{56,64},{64,7... | collective-permute-start | bytes 98312 | tf_op jit(solution)/shard_map/while/body/eval_jaxpr/ppermute | solution.py:19
  127.0 3.9 %collective-permute-start.1 = (bf16[128,64]{0,1:T(8,128)(2,1)}, bf16[128,64]{0,1:T(8,128)(2,1)S(1)}, u32[]{:S(2)}, u32[]{:S(2)}) collective-permute-start(bf16[128,64]{0,1:T(8,128)(2,1)} %get-tuple-element.865), channel_id=1, source_target_pairs={{0,8},{8,16},{16,24},{24,32},{32,40},{40,48},{48,56},{56,64},{64,7... | collective-permute-start | bytes 49160 | tf_op jit(solution)/shard_map/while/body/eval_jaxpr/ppermute | solution.py:14
  131.4 4.4 %collective-permute-done.1 = bf16[128,64]{0,1:T(8,128)(2,1)S(1)} collective-permute-done((bf16[128,64]{0,1:T(8,128)(2,1)}, bf16[128,64]{0,1:T(8,128)(2,1)S(1)}, u32[]{:S(2)}, u32[]{:S(2)}) %collective-permute-start.1) | collective-permute-done | bytes 16416 | tf_op jit(solution)/shard_map/while/body/eval_jaxpr/ppermute | solution.py:14
  150.6 9.3 %collective-permute-start.1 = (bf16[128,64]{0,1:T(8,128)(2,1)}, bf16[128,64]{0,1:T(8,128)(2,1)S(1)}, u32[]{:S(2)}, u32[]{:S(2)}) collective-permute-start(bf16[128,64]{0,1:T(8,128)(2,1)} %get-tuple-element.865), channel_id=1, source_target_pairs={{0,8},{8,16},{16,24},{24,32},{32,40},{40,48},{48,56},{56,64},{64,7... | collective-permute-start | bytes 49160 | tf_op jit(solution)/shard_map/while/body/eval_jaxpr/ppermute | solution.py:14
  172.2 3.9 %collective-permute-start = (bf16[128,512]{1,0:T(8,128)(2,1)S(1)}, bf16[128,512]{1,0:T(8,128)(2,1)S(1)}, u32[]{:S(2)}, u32[]{:S(2)}) collective-permute-start(bf16[128,512]{1,0:T(8,128)(2,1)S(1)} %get-tuple-element.864), channel_id=1, source_target_pairs={{0,8},{8,16},{16,24},{24,32},{32,40},{40,48},{48,56},{56,64},{64,7... | collective-permute-start | bytes 393224 | tf_op jit(solution)/shard_map/while/body/eval_jaxpr/ppermute | solution.py:14
  178.1 4.2 %collective-permute-start.1 = (bf16[128,64]{0,1:T(8,128)(2,1)}, bf16[128,64]{0,1:T(8,128)(2,1)S(1)}, u32[]{:S(2)}, u32[]{:S(2)}) collective-permute-start(bf16[128,64]{0,1:T(8,128)(2,1)} %get-tuple-element.865), channel_id=1, source_target_pairs={{0,8},{8,16},{16,24},{24,32},{32,40},{40,48},{48,56},{56,64},{64,7... | collective-permute-start | bytes 49160 | tf_op jit(solution)/shard_map/while/body/eval_jaxpr/ppermute | solution.py:14
  182.9 4.1 %collective-permute-done.1 = bf16[128,64]{0,1:T(8,128)(2,1)S(1)} collective-permute-done((bf16[128,64]{0,1:T(8,128)(2,1)}, bf16[128,64]{0,1:T(8,128)(2,1)S(1)}, u32[]{:S(2)}, u32[]{:S(2)}) %collective-permute-start.1) | collective-permute-done | bytes 16416 | tf_op jit(solution)/shard_map/while/body/eval_jaxpr/ppermute | solution.py:14
  199.3 4.2 %collective-permute-start = (bf16[128,512]{1,0:T(8,128)(2,1)S(1)}, bf16[128,512]{1,0:T(8,128)(2,1)S(1)}, u32[]{:S(2)}, u32[]{:S(2)}) collective-permute-start(bf16[128,512]{1,0:T(8,128)(2,1)S(1)} %get-tuple-element.864), channel_id=1, source_target_pairs={{0,8},{8,16},{16,24},{24,32},{32,40},{40,48},{48,56},{56,64},{64,7... | collective-permute-start | bytes 393224 | tf_op jit(solution)/shard_map/while/body/eval_jaxpr/ppermute | solution.py:14
  206.0 4.2 %collective-permute-start.1 = (bf16[128,64]{0,1:T(8,128)(2,1)}, bf16[128,64]{0,1:T(8,128)(2,1)S(1)}, u32[]{:S(2)}, u32[]{:S(2)}) collective-permute-start(bf16[128,64]{0,1:T(8,128)(2,1)} %get-tuple-element.865), channel_id=1, source_target_pairs={{0,8},{8,16},{16,24},{24,32},{32,40},{40,48},{48,56},{56,64},{64,7... | collective-permute-start | bytes 49160 | tf_op jit(solution)/shard_map/while/body/eval_jaxpr/ppermute | solution.py:14
  210.8 4.1 %collective-permute-done.1 = bf16[128,64]{0,1:T(8,128)(2,1)S(1)} collective-permute-done((bf16[128,64]{0,1:T(8,128)(2,1)}, bf16[128,64]{0,1:T(8,128)(2,1)S(1)}, u32[]{:S(2)}, u32[]{:S(2)}) %collective-permute-start.1) | collective-permute-done | bytes 16416 | tf_op jit(solution)/shard_map/while/body/eval_jaxpr/ppermute | solution.py:14
  223.9 4.0 %collective-permute-start.4 = (f32[1,128,512]{2,1,0:T(8,128)}, f32[1,128,512]{2,1,0:T(8,128)S(1)}, u32[]{:S(2)}, u32[]{:S(2)}) collective-permute-start(f32[1,128,512]{2,1,0:T(8,128)} %get-tuple-element.584), channel_id=1, source_target_pairs={{0,456},{8,464},{16,472},{24,480},{32,488},{40,496},{48,504},{56,0... | collective-permute-start | bytes 786440 | tf_op jit(solution)/shard_map/ppermute | solution.py:19
  228.7 9.3 %collective-permute-start.5 = (f32[1,128,64]{2,1,0:T(8,128)S(1)}, f32[1,128,64]{2,1,0:T(8,128)S(1)}, u32[]{:S(2)}, u32[]{:S(2)}) collective-permute-start(f32[1,128,64]{2,1,0:T(8,128)S(1)} %copy.34), channel_id=1, source_target_pairs={{0,456},{8,464},{16,472},{24,480},{32,488},{40,496},{48,504},{56,0... | collective-permute-start | bytes 98312 | tf_op jit(solution)/shard_map/ppermute | solution.py:19
  238.1 13.3 %collective-permute-done.5 = f32[1,128,64]{2,1,0:T(8,128)S(1)} collective-permute-done((f32[1,128,64]{2,1,0:T(8,128)S(1)}, f32[1,128,64]{2,1,0:T(8,128)S(1)}, u32[]{:S(2)}, u32[]{:S(2)}) %collective-permute-start.5) | collective-permute-done | bytes 32800 | tf_op jit(solution)/shard_map/ppermute | solution.py:19
  257.3 41.4 %reduce-scatter.5.cloned.1.call-done = f32[1,16,64]{2,1,0:T(8,128)} async-done(((f32[1,128,64]{2,1,0:T(8,128)}), f32[1,16,64]{2,1,0:T(8,128)}) %reduce-scatter.5.cloned.1.call-update) | async-done | bytes 4112 | tf_op jit(solution)/shard_map/reduce_scatter | solution.py:84
  300.0 45.8 %reduce-scatter.3.cloned.1.call-done = f32[1,16,512]{2,1,0:T(8,128)} async-done(((f32[1,128,512]{2,1,0:T(8,128)}), f32[1,16,512]{2,1,0:T(8,128)}) %reduce-scatter.3.cloned.1.call-update) | async-done | bytes 32784 | tf_op jit(solution)/shard_map/reduce_scatter | solution.py:84
  (231 shorter events, 145.7 us)
Async XLA Ops:
  7.2 291.5 %reduce-scatter.5.cloned.1.call-start = ((), (), s32[]{:S(2)}) async-start(), calls=%async_computation.3 | async-start | bytes 73728 | tf_op jit(solution)/shard_map/reduce_scatter | solution.py:84
  29.8 33.2 %collective-permute-start.2 = (f32[1,128,512]{2,1,0:T(8,128)}, f32[1,128,512]{2,1,0:T(8,128)}, u32[]{:S(2)}, u32[]{:S(2)}) collective-permute-start(f32[1,128,512]{2,1,0:T(8,128)} %get-tuple-element.866), channel_id=1, source_target_pairs={{0,8},{8,16},{16,24},{24,32},{32,40},{40,48},{48,56},{56,64},{64,7... | collective-permute-start | bytes 786440 | tf_op jit(solution)/shard_map/while/body/eval_jaxpr/ppermute | solution.py:19
  31.7 17.8 %collective-permute-start = (bf16[128,512]{1,0:T(8,128)(2,1)S(1)}, bf16[128,512]{1,0:T(8,128)(2,1)S(1)}, u32[]{:S(2)}, u32[]{:S(2)}) collective-permute-start(bf16[128,512]{1,0:T(8,128)(2,1)S(1)} %get-tuple-element.864), channel_id=1, source_target_pairs={{0,8},{8,16},{16,24},{24,32},{32,40},{40,48},{48,56},{56,64},{64,7... | collective-permute-start | bytes 393224 | tf_op jit(solution)/shard_map/while/body/eval_jaxpr/ppermute | solution.py:14
  35.6 26.0 %collective-permute-start.3 = (f32[1,128,64]{1,2,0:T(8,128)}, f32[1,128,64]{1,2,0:T(8,128)}, u32[]{:S(2)}, u32[]{:S(2)}) collective-permute-start(f32[1,128,64]{1,2,0:T(8,128)} %get-tuple-element.867), channel_id=1, source_target_pairs={{0,8},{8,16},{16,24},{24,32},{32,40},{40,48},{48,56},{56,64},{64,7... | collective-permute-start | bytes 98312 | tf_op jit(solution)/shard_map/while/body/eval_jaxpr/ppermute | solution.py:19
  64.8 21.9 %collective-permute-start.2 = (f32[1,128,512]{2,1,0:T(8,128)}, f32[1,128,512]{2,1,0:T(8,128)}, u32[]{:S(2)}, u32[]{:S(2)}) collective-permute-start(f32[1,128,512]{2,1,0:T(8,128)} %get-tuple-element.866), channel_id=1, source_target_pairs={{0,8},{8,16},{16,24},{24,32},{32,40},{40,48},{48,56},{56,64},{64,7... | collective-permute-start | bytes 786440 | tf_op jit(solution)/shard_map/while/body/eval_jaxpr/ppermute | solution.py:19
  68.6 16.6 %collective-permute-start.3 = (f32[1,128,64]{1,2,0:T(8,128)}, f32[1,128,64]{1,2,0:T(8,128)}, u32[]{:S(2)}, u32[]{:S(2)}) collective-permute-start(f32[1,128,64]{1,2,0:T(8,128)} %get-tuple-element.867), channel_id=1, source_target_pairs={{0,8},{8,16},{16,24},{24,32},{32,40},{40,48},{48,56},{56,64},{64,7... | collective-permute-start | bytes 98312 | tf_op jit(solution)/shard_map/while/body/eval_jaxpr/ppermute | solution.py:19
  88.4 24.4 %collective-permute-start.2 = (f32[1,128,512]{2,1,0:T(8,128)}, f32[1,128,512]{2,1,0:T(8,128)}, u32[]{:S(2)}, u32[]{:S(2)}) collective-permute-start(f32[1,128,512]{2,1,0:T(8,128)} %get-tuple-element.866), channel_id=1, source_target_pairs={{0,8},{8,16},{16,24},{24,32},{32,40},{40,48},{48,56},{56,64},{64,7... | collective-permute-start | bytes 786440 | tf_op jit(solution)/shard_map/while/body/eval_jaxpr/ppermute | solution.py:19
  90.4 15.9 %collective-permute-start = (bf16[128,512]{1,0:T(8,128)(2,1)S(1)}, bf16[128,512]{1,0:T(8,128)(2,1)S(1)}, u32[]{:S(2)}, u32[]{:S(2)}) collective-permute-start(bf16[128,512]{1,0:T(8,128)(2,1)S(1)} %get-tuple-element.864), channel_id=1, source_target_pairs={{0,8},{8,16},{16,24},{24,32},{32,40},{40,48},{48,56},{56,64},{64,7... | collective-permute-start | bytes 393224 | tf_op jit(solution)/shard_map/while/body/eval_jaxpr/ppermute | solution.py:14
  94.8 16.6 %collective-permute-start.3 = (f32[1,128,64]{1,2,0:T(8,128)}, f32[1,128,64]{1,2,0:T(8,128)}, u32[]{:S(2)}, u32[]{:S(2)}) collective-permute-start(f32[1,128,64]{1,2,0:T(8,128)} %get-tuple-element.867), channel_id=1, source_target_pairs={{0,8},{8,16},{16,24},{24,32},{32,40},{40,48},{48,56},{56,64},{64,7... | collective-permute-start | bytes 98312 | tf_op jit(solution)/shard_map/while/body/eval_jaxpr/ppermute | solution.py:19
  114.7 28.4 %collective-permute-start.2 = (f32[1,128,512]{2,1,0:T(8,128)}, f32[1,128,512]{2,1,0:T(8,128)}, u32[]{:S(2)}, u32[]{:S(2)}) collective-permute-start(f32[1,128,512]{2,1,0:T(8,128)} %get-tuple-element.866), channel_id=1, source_target_pairs={{0,8},{8,16},{16,24},{24,32},{32,40},{40,48},{48,56},{56,64},{64,7... | collective-permute-start | bytes 786440 | tf_op jit(solution)/shard_map/while/body/eval_jaxpr/ppermute | solution.py:19
  116.6 19.9 %collective-permute-start = (bf16[128,512]{1,0:T(8,128)(2,1)S(1)}, bf16[128,512]{1,0:T(8,128)(2,1)S(1)}, u32[]{:S(2)}, u32[]{:S(2)}) collective-permute-start(bf16[128,512]{1,0:T(8,128)(2,1)S(1)} %get-tuple-element.864), channel_id=1, source_target_pairs={{0,8},{8,16},{16,24},{24,32},{32,40},{40,48},{48,56},{56,64},{64,7... | collective-permute-start | bytes 393224 | tf_op jit(solution)/shard_map/while/body/eval_jaxpr/ppermute | solution.py:14
  118.5 23.1 %collective-permute-start.3 = (f32[1,128,64]{1,2,0:T(8,128)}, f32[1,128,64]{1,2,0:T(8,128)}, u32[]{:S(2)}, u32[]{:S(2)}) collective-permute-start(f32[1,128,64]{1,2,0:T(8,128)} %get-tuple-element.867), channel_id=1, source_target_pairs={{0,8},{8,16},{16,24},{24,32},{32,40},{40,48},{48,56},{56,64},{64,7... | collective-permute-start | bytes 98312 | tf_op jit(solution)/shard_map/while/body/eval_jaxpr/ppermute | solution.py:19
  144.9 23.3 %collective-permute-start.2 = (f32[1,128,512]{2,1,0:T(8,128)}, f32[1,128,512]{2,1,0:T(8,128)}, u32[]{:S(2)}, u32[]{:S(2)}) collective-permute-start(f32[1,128,512]{2,1,0:T(8,128)} %get-tuple-element.866), channel_id=1, source_target_pairs={{0,8},{8,16},{16,24},{24,32},{32,40},{40,48},{48,56},{56,64},{64,7... | collective-permute-start | bytes 786440 | tf_op jit(solution)/shard_map/while/body/eval_jaxpr/ppermute | solution.py:19
  146.8 14.8 %collective-permute-start = (bf16[128,512]{1,0:T(8,128)(2,1)S(1)}, bf16[128,512]{1,0:T(8,128)(2,1)S(1)}, u32[]{:S(2)}, u32[]{:S(2)}) collective-permute-start(bf16[128,512]{1,0:T(8,128)(2,1)S(1)} %get-tuple-element.864), channel_id=1, source_target_pairs={{0,8},{8,16},{16,24},{24,32},{32,40},{40,48},{48,56},{56,64},{64,7... | collective-permute-start | bytes 393224 | tf_op jit(solution)/shard_map/while/body/eval_jaxpr/ppermute | solution.py:14
  148.7 18.1 %collective-permute-start.3 = (f32[1,128,64]{1,2,0:T(8,128)}, f32[1,128,64]{1,2,0:T(8,128)}, u32[]{:S(2)}, u32[]{:S(2)}) collective-permute-start(f32[1,128,64]{1,2,0:T(8,128)} %get-tuple-element.867), channel_id=1, source_target_pairs={{0,8},{8,16},{16,24},{24,32},{32,40},{40,48},{48,56},{56,64},{64,7... | collective-permute-start | bytes 98312 | tf_op jit(solution)/shard_map/while/body/eval_jaxpr/ppermute | solution.py:19
  170.0 24.2 %collective-permute-start.2 = (f32[1,128,512]{2,1,0:T(8,128)}, f32[1,128,512]{2,1,0:T(8,128)}, u32[]{:S(2)}, u32[]{:S(2)}) collective-permute-start(f32[1,128,512]{2,1,0:T(8,128)} %get-tuple-element.866), channel_id=1, source_target_pairs={{0,8},{8,16},{16,24},{24,32},{32,40},{40,48},{48,56},{56,64},{64,7... | collective-permute-start | bytes 786440 | tf_op jit(solution)/shard_map/while/body/eval_jaxpr/ppermute | solution.py:19
  172.2 15.4 %collective-permute-start = (bf16[128,512]{1,0:T(8,128)(2,1)S(1)}, bf16[128,512]{1,0:T(8,128)(2,1)S(1)}, u32[]{:S(2)}, u32[]{:S(2)}) collective-permute-start(bf16[128,512]{1,0:T(8,128)(2,1)S(1)} %get-tuple-element.864), channel_id=1, source_target_pairs={{0,8},{8,16},{16,24},{24,32},{32,40},{40,48},{48,56},{56,64},{64,7... | collective-permute-start | bytes 393224 | tf_op jit(solution)/shard_map/while/body/eval_jaxpr/ppermute | solution.py:14
  176.2 16.6 %collective-permute-start.3 = (f32[1,128,64]{1,2,0:T(8,128)}, f32[1,128,64]{1,2,0:T(8,128)}, u32[]{:S(2)}, u32[]{:S(2)}) collective-permute-start(f32[1,128,64]{1,2,0:T(8,128)} %get-tuple-element.867), channel_id=1, source_target_pairs={{0,8},{8,16},{16,24},{24,32},{32,40},{40,48},{48,56},{56,64},{64,7... | collective-permute-start | bytes 98312 | tf_op jit(solution)/shard_map/while/body/eval_jaxpr/ppermute | solution.py:19
  196.0 26.1 %collective-permute-start.2 = (f32[1,128,512]{2,1,0:T(8,128)}, f32[1,128,512]{2,1,0:T(8,128)}, u32[]{:S(2)}, u32[]{:S(2)}) collective-permute-start(f32[1,128,512]{2,1,0:T(8,128)} %get-tuple-element.866), channel_id=1, source_target_pairs={{0,8},{8,16},{16,24},{24,32},{32,40},{40,48},{48,56},{56,64},{64,7... | collective-permute-start | bytes 786440 | tf_op jit(solution)/shard_map/while/body/eval_jaxpr/ppermute | solution.py:19
  199.3 16.2 %collective-permute-start = (bf16[128,512]{1,0:T(8,128)(2,1)S(1)}, bf16[128,512]{1,0:T(8,128)(2,1)S(1)}, u32[]{:S(2)}, u32[]{:S(2)}) collective-permute-start(bf16[128,512]{1,0:T(8,128)(2,1)S(1)} %get-tuple-element.864), channel_id=1, source_target_pairs={{0,8},{8,16},{16,24},{24,32},{32,40},{40,48},{48,56},{56,64},{64,7... | collective-permute-start | bytes 393224 | tf_op jit(solution)/shard_map/while/body/eval_jaxpr/ppermute | solution.py:14
  203.5 17.2 %collective-permute-start.3 = (f32[1,128,64]{1,2,0:T(8,128)}, f32[1,128,64]{1,2,0:T(8,128)}, u32[]{:S(2)}, u32[]{:S(2)}) collective-permute-start(f32[1,128,64]{1,2,0:T(8,128)} %get-tuple-element.867), channel_id=1, source_target_pairs={{0,8},{8,16},{16,24},{24,32},{32,40},{40,48},{48,56},{56,64},{64,7... | collective-permute-start | bytes 98312 | tf_op jit(solution)/shard_map/while/body/eval_jaxpr/ppermute | solution.py:19
  223.9 28.2 %collective-permute-start.4 = (f32[1,128,512]{2,1,0:T(8,128)}, f32[1,128,512]{2,1,0:T(8,128)S(1)}, u32[]{:S(2)}, u32[]{:S(2)}) collective-permute-start(f32[1,128,512]{2,1,0:T(8,128)} %get-tuple-element.584), channel_id=1, source_target_pairs={{0,456},{8,464},{16,472},{24,480},{32,488},{40,496},{48,504},{56,0... | collective-permute-start | bytes 786440 | tf_op jit(solution)/shard_map/ppermute | solution.py:19
  228.7 22.6 %collective-permute-start.5 = (f32[1,128,64]{2,1,0:T(8,128)S(1)}, f32[1,128,64]{2,1,0:T(8,128)S(1)}, u32[]{:S(2)}, u32[]{:S(2)}) collective-permute-start(f32[1,128,64]{2,1,0:T(8,128)S(1)} %copy.34), channel_id=1, source_target_pairs={{0,456},{8,464},{16,472},{24,480},{32,488},{40,496},{48,504},{56,0... | collective-permute-start | bytes 98312 | tf_op jit(solution)/shard_map/ppermute | solution.py:19
  252.0 93.7 %reduce-scatter.3.cloned.1.call-start = ((), (), s32[]{:S(2)}) async-start(), calls=%async_computation.2 | async-start | bytes 294912 | tf_op jit(solution)/shard_map/reduce_scatter | solution.py:84
  (44 other events, 205.2 us)
Sparse Core Ops, SparseCore 0:
  252.1 46.4 reduce-scatter.4
  301.4 44.2 reduce-scatter.2
where the time goes:
time: 357 us; the launch traced here: 354 us
  waiting for transfers between devices  130 us (36%)
  starting transfers between devices  104 us (29%)
  other arithmetic  54 us (15%)
  local copies, waits for them, and re-layouts  30.2 us (8%)
  matrix products  16.4 us (5%)
  between operations  14.7 us (4%)
  loops' own time  4.63 us (1%)
    reduce_scatter x2, waiting for transfers between devices, share_groups(): return lax.psum_scatter(pair, 'head', scatter_dimension=1, tiled=True)  87.2 us
    ppermute x14, starting transfers between devices, shifted(): return lax.ppermute(x, axis, pairs)  54.5 us
    ppermute x16, starting transfers between devices, shifted_2(): return lax.ppermute(x, axis, [(i, (i + by) % count) for i in range(count)])  49 us
    ppermute x14, waiting for transfers between devices, shifted(): return lax.ppermute(x, axis, pairs)  29.9 us
    add x7, other arithmetic, cycle_turn(): grad_qlat + terms[0]  24.2 us
    ppermute x16, waiting for transfers between devices, shifted_2(): return lax.ppermute(x, axis, [(i, (i + by) % count) for i in range(count)])  13.4 us
    add x7, other arithmetic, cycle_turn(): sum_latent + terms[2][None]  12.5 us
    unnamed x20, local copies, waits for them, and re-layouts  10.4 us
  transfers between devices with their start and end apart: 32, of which 10 were waited for; matrix products, arithmetic and copies ran while one was open for 17% of the time, Pallas kernels for 0%

commit v1 on v0

v1 whole, which is shorter than its diff:
```python
import jax
import jax.numpy as jnp
from jax import lax
from jax.sharding import PartitionSpec as P

ROPE = 64
NOPE = 128
LEVELS = 3


def shifted(x, axis, by):
    count = lax.axis_size(axis)
    pairs = [(i, i + by) for i in range(count) if 0 <= i + by < count]
    return lax.ppermute(x, axis, pairs)


def local(q_latent, q_rope, attn_out, grad_out, log_total, latent, key_rope, doc_start):
    tok_rows, head_count, lat_width = q_latent.shape
    rope_width = key_rope.shape[1]
    span = 2**LEVELS
    groups = lax.axis_size("head")
    softmax_scale = (NOPE + ROPE) ** (-0.5)
    q_rot = q_rope.reshape(tok_rows, head_count, rope_width)
    row_delta = jnp.einsum("thc,thc->th", grad_out, attn_out, preferred_element_type=jnp.float32)
    own_tile = lax.axis_index("ctx")
    query_pos = own_tile * tok_rows + jnp.arange(tok_rows, dtype=jnp.int32)

    keys = jnp.concatenate([latent, key_rope], axis=1)[None]
    width = 1
    while width < span:
        keys = jnp.concatenate([shifted(keys, "ctx", width), keys], axis=0)
        width *= 2
    keys = keys.reshape(span * tok_rows, lat_width + rope_width)
    lat_all = keys[:, :lat_width]
    rot_all = keys[:, lat_width:]

    key_pos = (own_tile - span + 1) * tok_rows + jnp.arange(span * tok_rows, dtype=jnp.int32)
    visible = (
        (key_pos[None, :] >= doc_start[:, None]) & (key_pos[None, :] <= query_pos[:, None])
    )[:, None, :]
    scores = (
        jnp.einsum("thc,kc->thk", q_latent, lat_all, preferred_element_type=jnp.float32)
        + jnp.einsum("thr,kr->thk", q_rot, rot_all, preferred_element_type=jnp.float32)
    ) * softmax_scale
    probs = jnp.where(
        visible, jnp.exp(jnp.where(visible, scores, 0.0) - log_total[:, :, None]), 0.0
    )
    grad_probs = jnp.einsum("thc,kc->thk", grad_out, lat_all, preferred_element_type=jnp.float32)
    grad_scores = probs * (grad_probs - row_delta[:, :, None])
    probs_b = probs.astype(jnp.bfloat16)
    grad_b = grad_scores.astype(jnp.bfloat16)
    grad_qlat = softmax_scale * jnp.einsum(
        "thk,kc->thc", grad_b, lat_all, preferred_element_type=jnp.float32
    )
    grad_qrot = softmax_scale * jnp.einsum(
        "thk,kr->thr", grad_b, rot_all, preferred_element_type=jnp.float32
    )
    grad_lat = softmax_scale * jnp.einsum(
        "thk,thc->kc", grad_b, q_latent, preferred_element_type=jnp.float32
    ) + jnp.einsum("thk,thc->kc", probs_b, grad_out, preferred_element_type=jnp.float32)
    grad_rot = softmax_scale * jnp.einsum(
        "thk,thr->kr", grad_b, q_rot, preferred_element_type=jnp.float32
    )

    part = jnp.concatenate([grad_lat, grad_rot], axis=1)
    block = tok_rows // groups
    part = part.reshape(span, groups, block, lat_width + rope_width)
    part = lax.all_to_all(part, "head", 1, 1, tiled=True).sum(axis=1)

    width = span
    while width > 1:
        half = width // 2
        part = part[half:] + shifted(part[:half], "ctx", -half)
        width = half
    owned = part[0]
    return (
        grad_qlat.astype(jnp.bfloat16),
        grad_qrot.reshape(tok_rows, head_count * rope_width).astype(jnp.bfloat16),
        owned[:, :lat_width].astype(jnp.bfloat16),
        owned[:, lat_width:].astype(jnp.bfloat16),
    )


def solution(mesh):
    in_specs = (
        P("ctx", "head", None),
        P("ctx", "head"),
        P("ctx", "head", None),
        P("ctx", "head", None),
        P("ctx", "head"),
        P("ctx", None),
        P("ctx", None),
        P("ctx"),
    )
    out_specs = (
        P("ctx", "head", None),
        P("ctx", "head"),
        P(("ctx", "head"), None),
        P(("ctx", "head"), None),
    )
    return jax.shard_map(local, mesh=mesh, in_specs=in_specs, out_specs=out_specs, check_vma=False)
```

time: 357 us -> 140 us (0.39)
  the two profiles are of different devices: /device:TPU:6 before, /device:TPU:69 now
where the time goes in v1:
time: 140 us; the launch traced here: 139 us
  waiting for transfers between devices  39.3 us (28%)
  blocking collectives  32.7 us (23%)
  starting transfers between devices  26.7 us (19%)
  local copies, waits for them, and re-layouts  17.5 us (12%)
  matrix products  11.1 us (8%)
  other arithmetic  10.7 us (8%)
    ppermute x6, waiting for transfers between devices, shifted(): return lax.ppermute(x, axis, pairs)  39.3 us
    all_to_all x1, blocking collectives, local(): part = lax.all_to_all(part, 'head', 1, 1, tiled=True).sum(axis=1)  32.7 us
    ppermute x6, starting transfers between devices, shifted(): return lax.ppermute(x, axis, pairs)  26.7 us
    unnamed x32, local copies, waits for them, and re-layouts  8.78 us
    concatenate x1, local copies, waits for them, and re-layouts, local(): part = jnp.concatenate([grad_lat, grad_rot], axis=1)  3.18 us
  transfers between devices with their start and end apart: 6, of which 6 were waited for; matrix products, arithmetic and copies ran while one was open for 9% of the time, Pallas kernels for 0%

profile of v1, /device:TPU:69, one launch (start us, length us, event | category | flops | bytes accessed | tf_op | source)
XLA Modules:
  0.0 138.8 jit_solution(6973941782515152101)
XLA Ops:
  2.5 4.1 %collective-permute-start = (bf16[1,128,576]{1,2,0:T(8,128)(2,1)S(1)}, bf16[1,128,576]{1,2,0:T(8,128)(2,1)S(1)}, u32[]{:S(2)}, u32[]{:S(2)}) collective-permute-start(bf16[1,128,576]{1,2,0:T(8,128)(2,1)S(1)} %maximum_bitcast_fusion), channel_id=1, source_target_pairs={{0,8},{8,16},{16,24},{24,32},{32,40},{40,48},{48,56},{56,64},{64,7... | collective-permute-start | bytes 442376 | tf_op jit(solution)/shard_map/ppermute | solution.py:14
  6.6 2.1 %collective-permute-done = bf16[1,128,576]{1,2,0:T(8,128)(2,1)S(1)} collective-permute-done((bf16[1,128,576]{1,2,0:T(8,128)(2,1)S(1)}, bf16[1,128,576]{1,2,0:T(8,128)(2,1)S(1)}, u32[]{:S(2)}, u32[]{:S(2)}) %collective-permute-start) | collective-permute-done | bytes 147488 | tf_op jit(solution)/shard_map/ppermute | solution.py:14
  8.7 4.8 %collective-permute-start.1 = (bf16[2,128,576]{1,2,0:T(8,128)(2,1)S(1)}, bf16[2,128,576]{1,2,0:T(8,128)(2,1)S(1)}, u32[]{:S(2)}, u32[]{:S(2)}) collective-permute-start(bf16[2,128,576]{1,2,0:T(8,128)(2,1)S(1)} %pad_maximum_fusion.3), channel_id=1, source_target_pairs={{0,16},{8,24},{16,32},{24,40},{32,48},{40,56},{48,64},{56,72},{64,... | collective-permute-start | bytes 884744 | tf_op jit(solution)/shard_map/ppermute | solution.py:14
  13.5 1.9 %copy.56 = bf16[128,8,512]{0,2,1:T(8,128)(2,1)S(1)} copy(bf16[128,8,512]{2,1,0:T(8,128)(2,1)} %param.11) | data formatting | bytes 2097152 | tf_op args[3]
  15.5 4.6 %collective-permute-done.1 = bf16[2,128,576]{1,2,0:T(8,128)(2,1)S(1)} collective-permute-done((bf16[2,128,576]{1,2,0:T(8,128)(2,1)S(1)}, bf16[2,128,576]{1,2,0:T(8,128)(2,1)S(1)}, u32[]{:S(2)}, u32[]{:S(2)}) %collective-permute-start.1) | collective-permute-done | bytes 294944 | tf_op jit(solution)/shard_map/ppermute | solution.py:14
  20.2 4.4 %collective-permute-start.2 = (bf16[4,128,576]{1,2,0:T(8,128)(2,1)S(1)}, bf16[4,128,576]{1,2,0:T(8,128)(2,1)}, u32[]{:S(2)}, u32[]{:S(2)}) collective-permute-start(bf16[4,128,576]{1,2,0:T(8,128)(2,1)S(1)} %pad_maximum_fusion.2), channel_id=1, source_target_pairs={{0,32},{8,40},{16,48},{24,56},{32,64},{40,72},{48,80},{56,88},{64,... | collective-permute-start | bytes 1769480 | tf_op jit(solution)/shard_map/ppermute | solution.py:14
  24.6 1.6 %fusion.4 = f32[128,8]{1,0:T(8,128)S(1)} fusion(bf16[128,8,512]{2,1,0:T(8,128)(2,1)S(1)} %copy-done.1, bf16[128,8,512]{2,1,0:T(8,128)(2,1)} %param.10), kind=kLoop, calls=%fused_computation.10 | loop fusion | flops 2096128 | bytes 2101248
  27.0 2.7 %copy.54 = bf16[128,8,512]{0,2,1:T(8,128)(2,1)} copy(bf16[128,8,512]{2,1,0:T(8,128)(2,1)} %param.8) | data formatting | bytes 2097152 | tf_op args[0]
  30.5 4.9 %collective-permute-done.2 = bf16[4,128,576]{1,2,0:T(8,128)(2,1)} collective-permute-done((bf16[4,128,576]{1,2,0:T(8,128)(2,1)S(1)}, bf16[4,128,576]{1,2,0:T(8,128)(2,1)}, u32[]{:S(2)}, u32[]{:S(2)}) %collective-permute-start.2) | collective-permute-done | bytes 589856 | tf_op jit(solution)/shard_map/ppermute | solution.py:14
  37.5 1.7 %fusion.9 = f32[1024,128,8]{1,0,2:T(8,128)S(1)} fusion(bf16[128,8,64]{0,2,1:T(8,128)(2,1)} %bitcast.56, bf16[1024,576]{1,0:T(8,128)(2,1)S(1)} %bitcast.51), kind=kOutput, calls=%fused_computation.24 | convolution fusion | flops 134217728 | bytes 4587520 | tf_op jit(solution)/shard_map/thr,kr->thk/dot_general | solution.py:43
  39.2 1.7 %fusion.3 = f32[128,8,1024]{0,2,1:T(8,128)S(1)} fusion(f32[1024,128,8]{1,0,2:T(8,128)S(1)} %fusion.9, bf16[128,8,512]{0,2,1:T(8,128)(2,1)S(1)} %copy-done.6, f32[128,8]{0,1:T(8,128)S(1)} %copy-done.12, pred[128,1024]{0,1:T(8,128)(4,1)S(1)} %copy-done.10, bf16[1024,576]{1,0:T(8,128)(2,1)S(1)} %bitcast.52), kind=kOutput, calls=%fused_computation.5 | convolution fusion | flops 1078984704 | bytes 10620928 | tf_op jit(solution)/shard_map/thc,kc->thk/dot_general | solution.py:42
  42.2 2.6 %fusion = bf16[128,8,1024]{0,2,1:T(8,128)(2,1)S(1)} fusion(f32[128,8,1024]{0,2,1:T(8,128)S(1)} %fusion.3, bf16[128,8,512]{0,2,1:T(8,128)(2,1)} %copy-done, f32[128,8]{0,1:T(8,128)S(1)} %copy.67, bf16[1024,576]{1,0:T(8,128)(2,1)S(1)} %bitcast.53), kind=kOutput, calls=%fused_computation.1 | convolution fusion | flops 1076887552 | bytes 8392704 | tf_op jit(solution)/shard_map/thc,kc->thk/dot_general | solution.py:48
  46.9 1.6 %pad_maximum_fusion = f32[1024,576]{0,1:T(8,128)} fusion(f32[1024,64]{0,1:T(8,128)S(1)} %fusion.7, f32[1024,512]{0,1:T(8,128)S(1)} %bitcast_add_fusion), kind=kLoop, calls=%fused_computation.6 | loop fusion | flops 589824 | bytes 4718592 | tf_op jit(solution)/shard_map/concatenate | solution.py:65
  48.5 3.2 %copy.58 = f32[1024,576]{1,0:T(8,128)} copy(f32[1024,576]{0,1:T(8,128)} %pad_maximum_fusion) | data formatting | bytes 4718592 | tf_op jit(solution)/shard_map/concatenate | solution.py:65
  51.7 2.0 %copy.59 = f32[8,8,16,576]{3,2,0,1:T(8,128)S(1)} copy(f32[8,8,16,576]{3,2,1,0:T(8,128)} %bitcast.50) | data formatting | bytes 4718592 | tf_op jit(solution)/shard_map/reshape | solution.py:67
  53.6 32.7 %all_to_all.5 = f32[8,8,16,576]{3,2,0,1:T(8,128)} all-to-all(f32[8,8,16,576]{3,2,0,1:T(8,128)S(1)} %copy.59), channel_id=1, replica_groups=mesh['ctx'=64,'head'=8] {'head'}, dimensions={1} | all-to-all | bytes 4718592 | tf_op jit(solution)/shard_map/all_to_all | solution.py:68
  86.3 2.6 %reduce_sum.9 = f32[8,16,576]{2,1,0:T(8,128)} reduce(f32[8,8,16,576]{3,2,0,1:T(8,128)} %all_to_all.5, f32[]{:T(128)} %constant.4.clone.1), dimensions={1}, to_apply=%region_0.1 | reduce | flops 516096 | bytes 2654212 | tf_op jit(solution)/shard_map/reduce_sum | solution.py:68
  89.9 1.9 %collective-permute-start.3 = (f32[4,16,576]{2,1,0:T(8,128)S(1)}, f32[4,16,576]{2,1,0:T(8,128)S(1)}, u32[]{:S(2)}, u32[]{:S(2)}) collective-permute-start(f32[4,16,576]{2,1,0:T(8,128)S(1)} %slice.45), channel_id=1, source_target_pairs={{32,0},{40,8},{48,16},{56,24},{64,32},{72,40},{80,48},{88,56},{96,... | collective-permute-start | bytes 442376 | tf_op jit(solution)/shard_map/ppermute | solution.py:14
  91.8 23.1 %collective-permute-done.3 = f32[4,16,576]{2,1,0:T(8,128)S(1)} collective-permute-done((f32[4,16,576]{2,1,0:T(8,128)S(1)}, f32[4,16,576]{2,1,0:T(8,128)S(1)}, u32[]{:S(2)}, u32[]{:S(2)}) %collective-permute-start.3) | collective-permute-done | bytes 147488 | tf_op jit(solution)/shard_map/ppermute | solution.py:14
  115.9 7.0 %collective-permute-start.4 = (f32[2,16,576]{2,1,0:T(8,128)S(1)}, f32[2,16,576]{2,1,0:T(8,128)S(1)}, u32[]{:S(2)}, u32[]{:S(2)}) collective-permute-start(f32[2,16,576]{2,1,0:T(8,128)S(1)} %slice.47), channel_id=1, source_target_pairs={{16,0},{24,8},{32,16},{40,24},{48,32},{56,40},{64,48},{72,56},{80,... | collective-permute-start | bytes 221192 | tf_op jit(solution)/shard_map/ppermute | solution.py:14
  124.2 2.7 %collective-permute-done.4 = f32[2,16,576]{2,1,0:T(8,128)S(1)} collective-permute-done((f32[2,16,576]{2,1,0:T(8,128)S(1)}, f32[2,16,576]{2,1,0:T(8,128)S(1)}, u32[]{:S(2)}, u32[]{:S(2)}) %collective-permute-start.4) | collective-permute-done | bytes 73760 | tf_op jit(solution)/shard_map/ppermute | solution.py:14
  127.5 4.5 %collective-permute-start.5 = (f32[1,16,576]{2,1,0:T(8,128)}, f32[1,16,576]{2,1,0:T(8,128)}, u32[]{:S(2)}, u32[]{:S(2)}) collective-permute-start(f32[1,16,576]{2,1,0:T(8,128)} %slice.49), channel_id=1, source_target_pairs={{8,0},{16,8},{24,16},{32,24},{40,32},{48,40},{56,48},{64,56},{72,6... | collective-permute-start | bytes 110600 | tf_op jit(solution)/shard_map/ppermute | solution.py:14
  132.6 1.5 %copy.60 = bf16[128,8,512]{2,1,0:T(8,128)(2,1)} copy(bf16[128,8,512]{2,0,1:T(8,128)(2,1)S(1)} %multiply_convert_fusion) | data formatting | bytes 2097152
  134.9 2.0 %collective-permute-done.5 = f32[1,16,576]{2,1,0:T(8,128)} collective-permute-done((f32[1,16,576]{2,1,0:T(8,128)}, f32[1,16,576]{2,1,0:T(8,128)}, u32[]{:S(2)}, u32[]{:S(2)}) %collective-permute-start.5) | collective-permute-done | bytes 36896 | tf_op jit(solution)/shard_map/ppermute | solution.py:14
  (51 shorter events, 16.2 us)
Async XLA Ops:
  1.7 22.9 %copy-start.1 = (bf16[128,8,512]{2,1,0:T(8,128)(2,1)S(1)}, bf16[128,8,512]{2,1,0:T(8,128)(2,1)}, u32[]{:S(2)}) copy-start(bf16[128,8,512]{2,1,0:T(8,128)(2,1)} %param.11) | copy-start | bytes 3145732
  2.5 6.2 %collective-permute-start = (bf16[1,128,576]{1,2,0:T(8,128)(2,1)S(1)}, bf16[1,128,576]{1,2,0:T(8,128)(2,1)S(1)}, u32[]{:S(2)}, u32[]{:S(2)}) collective-permute-start(bf16[1,128,576]{1,2,0:T(8,128)(2,1)S(1)} %maximum_bitcast_fusion), channel_id=1, source_target_pairs={{0,8},{8,16},{16,24},{24,32},{32,40},{40,48},{48,56},{56,64},{64,7... | collective-permute-start | bytes 442376 | tf_op jit(solution)/shard_map/ppermute | solution.py:14
  8.7 17.5 %copy-start.2 = (bf16[1,128,576]{1,2,0:T(8,128)(2,1)}, bf16[1,128,576]{1,2,0:T(8,128)(2,1)S(1)}, u32[]{:S(2)}) copy-start(bf16[1,128,576]{1,2,0:T(8,128)(2,1)S(1)} %collective-permute-done) | copy-start | bytes 442372
  8.7 11.4 %collective-permute-start.1 = (bf16[2,128,576]{1,2,0:T(8,128)(2,1)S(1)}, bf16[2,128,576]{1,2,0:T(8,128)(2,1)S(1)}, u32[]{:S(2)}, u32[]{:S(2)}) collective-permute-start(bf16[2,128,576]{1,2,0:T(8,128)(2,1)S(1)} %pad_maximum_fusion.3), channel_id=1, source_target_pairs={{0,16},{8,24},{16,32},{24,40},{32,48},{40,56},{48,64},{56,72},{64,... | collective-permute-start | bytes 884744 | tf_op jit(solution)/shard_map/ppermute | solution.py:14
  15.4 25.5 %copy-start = (bf16[128,8,512]{0,2,1:T(8,128)(2,1)}, bf16[128,8,512]{0,2,1:T(8,128)(2,1)S(1)}, u32[]{:S(2)}) copy-start(bf16[128,8,512]{0,2,1:T(8,128)(2,1)S(1)} %copy.56) | copy-start | bytes 3145732
  15.5 10.8 %copy-start.9 = (bf16[128,512]{1,0:T(8,128)(2,1)S(1)}, bf16[128,512]{1,0:T(8,128)(2,1)}, u32[]{:S(2)}) copy-start(bf16[128,512]{1,0:T(8,128)(2,1)} %param.9) | copy-start | bytes 393220
  20.1 9.6 %copy-start.4 = (bf16[2,128,576]{1,2,0:T(8,128)(2,1)}, bf16[2,128,576]{1,2,0:T(8,128)(2,1)S(1)}, u32[]{:S(2)}) copy-start(bf16[2,128,576]{1,2,0:T(8,128)(2,1)S(1)} %collective-permute-done.1) | copy-start | bytes 884740
  20.2 9.5 %copy-start.11 = (s32[128]{0:T(128)S(1)}, s32[128]{0:T(128)}, u32[]{:S(2)}) copy-start(s32[128]{0:T(128)} %param.15) | copy-start | bytes 1540
  20.2 15.2 %collective-permute-start.2 = (bf16[4,128,576]{1,2,0:T(8,128)(2,1)S(1)}, bf16[4,128,576]{1,2,0:T(8,128)(2,1)}, u32[]{:S(2)}, u32[]{:S(2)}) collective-permute-start(bf16[4,128,576]{1,2,0:T(8,128)(2,1)S(1)} %pad_maximum_fusion.2), channel_id=1, source_target_pairs={{0,32},{8,40},{16,48},{24,56},{32,64},{40,72},{48,80},{56,88},{64,... | collective-permute-start | bytes 1769480 | tf_op jit(solution)/shard_map/ppermute | solution.py:14
  26.2 9.2 %copy-start.3 = (bf16[1,128,576]{1,2,0:T(8,128)(2,1)S(1)}, bf16[1,128,576]{1,2,0:T(8,128)(2,1)}, u32[]{:S(2)}) copy-start(bf16[1,128,576]{1,2,0:T(8,128)(2,1)} %copy-done.2) | copy-start | bytes 442372
  37.4 1.7 %copy-start.6 = (bf16[128,8,512]{0,2,1:T(8,128)(2,1)S(1)}, bf16[128,8,512]{0,2,1:T(8,128)(2,1)}, u32[]{:S(2)}) copy-start(bf16[128,8,512]{0,2,1:T(8,128)(2,1)} %copy.54) | copy-start | bytes 3145732
  37.5 1.7 %copy-start.10 = (pred[128,1024]{0,1:T(8,128)(4,1)S(1)}, pred[128,1024]{0,1:T(8,128)(4,1)}, u32[]{:S(2)}) copy-start(pred[128,1024]{0,1:T(8,128)(4,1)} %compare_and_fusion) | copy-start | bytes 393220
  37.5 1.7 %copy-start.12 = (f32[128,8]{0,1:T(8,128)S(1)}, f32[128,8]{0,1:T(8,128)}, u32[]{:S(2)}) copy-start(f32[128,8]{0,1:T(8,128)} %param.12) | copy-start | bytes 12292
  42.2 2.6 %copy-start.5 = (bf16[128,512]{0,1:T(8,128)(2,1)S(1)}, bf16[128,512]{0,1:T(8,128)(2,1)}, u32[]{:S(2)}) copy-start(bf16[128,512]{0,1:T(8,128)(2,1)} %copy.47) | copy-start | bytes 393220
  89.9 25.1 %collective-permute-start.3 = (f32[4,16,576]{2,1,0:T(8,128)S(1)}, f32[4,16,576]{2,1,0:T(8,128)S(1)}, u32[]{:S(2)}, u32[]{:S(2)}) collective-permute-start(f32[4,16,576]{2,1,0:T(8,128)S(1)} %slice.45), channel_id=1, source_target_pairs={{32,0},{40,8},{48,16},{56,24},{64,32},{72,40},{80,48},{88,56},{96,... | collective-permute-start | bytes 442376 | tf_op jit(solution)/shard_map/ppermute | solution.py:14
  115.9 11.0 %collective-permute-start.4 = (f32[2,16,576]{2,1,0:T(8,128)S(1)}, f32[2,16,576]{2,1,0:T(8,128)S(1)}, u32[]{:S(2)}, u32[]{:S(2)}) collective-permute-start(f32[2,16,576]{2,1,0:T(8,128)S(1)} %slice.47), channel_id=1, source_target_pairs={{16,0},{24,8},{32,16},{40,24},{48,32},{56,40},{64,48},{72,56},{80,... | collective-permute-start | bytes 221192 | tf_op jit(solution)/shard_map/ppermute | solution.py:14
  126.9 0.6 copy-start.7
  127.5 9.3 %collective-permute-start.5 = (f32[1,16,576]{2,1,0:T(8,128)}, f32[1,16,576]{2,1,0:T(8,128)}, u32[]{:S(2)}, u32[]{:S(2)}) collective-permute-start(f32[1,16,576]{2,1,0:T(8,128)} %slice.49), channel_id=1, source_target_pairs={{8,0},{16,8},{24,16},{32,24},{40,32},{48,40},{56,48},{64,56},{72,6... | collective-permute-start | bytes 110600 | tf_op jit(solution)/shard_map/ppermute | solution.py:14
  132.6 4.3 %copy-start.8 = (f32[2,16,576]{2,1,0:T(8,128)S(1)}, f32[2,16,576]{2,1,0:T(8,128)}, u32[]{:S(2)}) copy-start(f32[2,16,576]{2,1,0:T(8,128)} %copy-done.7) | copy-start | bytes 221188

commit v2 on v1

v2 whole, which is shorter than its diff:
```python
import jax
import jax.numpy as jnp
from jax import lax
from jax.sharding import PartitionSpec as P

ROPE = 64
NOPE = 128
LEVELS = 3


def shifted(x, axis, by):
    count = lax.axis_size(axis)
    pairs = [(i, i + by) for i in range(count) if 0 <= i + by < count]
    return lax.ppermute(x, axis, pairs)


def window_terms(q_latent, q_rot, grad_out, row_delta, log_total, doc_start, query_pos, keys, key_first):
    lat_width = q_latent.shape[2]
    softmax_scale = (NOPE + ROPE) ** (-0.5)
    lat_all = keys[:, :lat_width]
    rot_all = keys[:, lat_width:]
    key_pos = key_first + jnp.arange(keys.shape[0], dtype=jnp.int32)
    visible = (
        (key_pos[None, :] >= doc_start[:, None]) & (key_pos[None, :] <= query_pos[:, None])
    )[:, None, :]
    scores = (
        jnp.einsum("thc,kc->thk", q_latent, lat_all, preferred_element_type=jnp.float32)
        + jnp.einsum("thr,kr->thk", q_rot, rot_all, preferred_element_type=jnp.float32)
    ) * softmax_scale
    probs = jnp.where(
        visible, jnp.exp(jnp.where(visible, scores, 0.0) - log_total[:, :, None]), 0.0
    )
    grad_probs = jnp.einsum("thc,kc->thk", grad_out, lat_all, preferred_element_type=jnp.float32)
    grad_scores = probs * (grad_probs - row_delta[:, :, None])
    probs_b = probs.astype(jnp.bfloat16)
    grad_b = grad_scores.astype(jnp.bfloat16)
    grad_qlat = jnp.einsum("thk,kc->thc", grad_b, lat_all, preferred_element_type=jnp.float32)
    grad_qrot = jnp.einsum("thk,kr->thr", grad_b, rot_all, preferred_element_type=jnp.float32)
    grad_lat = softmax_scale * jnp.einsum(
        "thk,thc->kc", grad_b, q_latent, preferred_element_type=jnp.float32
    ) + jnp.einsum("thk,thc->kc", probs_b, grad_out, preferred_element_type=jnp.float32)
    grad_rot = softmax_scale * jnp.einsum(
        "thk,thr->kr", grad_b, q_rot, preferred_element_type=jnp.float32
    )
    return grad_qlat, grad_qrot, jnp.concatenate([grad_lat, grad_rot], axis=1)


def local(q_latent, q_rope, attn_out, grad_out, log_total, latent, key_rope, doc_start):
    tok_rows, head_count, lat_width = q_latent.shape
    rope_width = key_rope.shape[1]
    span = 2**LEVELS
    half_span = span // 2
    groups = lax.axis_size("head")
    block = tok_rows // groups
    softmax_scale = (NOPE + ROPE) ** (-0.5)
    q_rot = q_rope.reshape(tok_rows, head_count, rope_width)
    row_delta = jnp.einsum("thc,thc->th", grad_out, attn_out, preferred_element_type=jnp.float32)
    own_tile = lax.axis_index("ctx")
    query_pos = own_tile * tok_rows + jnp.arange(tok_rows, dtype=jnp.int32)

    def terms(keys, first_tile):
        flat = keys.reshape(-1, lat_width + rope_width)
        return window_terms(
            q_latent, q_rot, grad_out, row_delta, log_total, doc_start, query_pos,
            flat, first_tile * tok_rows,
        )

    def group_sum(part):
        part = part.reshape(-1, groups, block, lat_width + rope_width)
        return lax.all_to_all(part, "head", 1, 1, tiled=True).sum(axis=1)

    near = jnp.concatenate([latent, key_rope], axis=1)[None]
    width = 1
    while width < half_span:
        near = jnp.concatenate([shifted(near, "ctx", width), near], axis=0)
        width *= 2
    far = shifted(near, "ctx", half_span)

    near_qlat, near_qrot, near_part = terms(near, own_tile - half_span + 1)
    far_qlat, far_qrot, far_part = terms(far, own_tile - span + 1)
    grad_qlat = softmax_scale * (near_qlat + far_qlat)
    grad_qrot = softmax_scale * (near_qrot + far_qrot)

    far_sum = shifted(group_sum(far_part), "ctx", -half_span)
    part = group_sum(near_part) + far_sum
    width = half_span
    while width > 1:
        half = width // 2
        part = part[half:] + shifted(part[:half], "ctx", -half)
        width = half
    owned = part[0]
    return (
        grad_qlat.astype(jnp.bfloat16),
        grad_qrot.reshape(tok_rows, head_count * rope_width).astype(jnp.bfloat16),
        owned[:, :lat_width].astype(jnp.bfloat16),
        owned[:, lat_width:].astype(jnp.bfloat16),
    )


def solution(mesh):
    in_specs = (
        P("ctx", "head", None),
        P("ctx", "head"),
        P("ctx", "head", None),
        P("ctx", "head", None),
        P("ctx", "head"),
        P("ctx", None),
        P("ctx", None),
        P("ctx"),
    )
    out_specs = (
        P("ctx", "head", None),
        P("ctx", "head"),
        P(("ctx", "head"), None),
        P(("ctx", "head"), None),
    )
    return jax.shard_map(local, mesh=mesh, in_specs=in_specs, out_specs=out_specs, check_vma=False)
```

time: 140 us -> 137 us (0.979)
  the two profiles are of different devices: /device:TPU:69 before, /device:TPU:6 now
where the time goes in v2:
time: 137 us; the launch traced here: 136 us
  waiting for transfers between devices  53.4 us (39%)
  starting transfers between devices  30.2 us (22%)
  local copies, waits for them, and re-layouts  21.6 us (16%)
  matrix products  18.7 us (14%)
  other arithmetic  11.2 us (8%)
    ppermute x6, waiting for transfers between devices, shifted(): return lax.ppermute(x, axis, pairs)  44.5 us
    ppermute x6, starting transfers between devices, shifted(): return lax.ppermute(x, axis, pairs)  19.6 us
    all_to_all x2, starting transfers between devices, group_sum(): return lax.all_to_all(part, 'head', 1, 1, tiled=True).sum(axis=1)  10.7 us
    all_to_all x2, waiting for transfers between devices, group_sum(): return lax.all_to_all(part, 'head', 1, 1, tiled=True).sum(axis=1)  8.87 us
    unnamed x30, local copies, waits for them, and re-layouts  7 us
    concatenate x2, local copies, waits for them, and re-layouts, window_terms(): return (grad_qlat, grad_qrot, jnp.concatenate([grad_lat, grad_rot], axis=1))  5.49 us
    reshape x2, local copies, waits for them, and re-layouts, group_sum(): part = part.reshape(-1, groups, block, lat_width + rope_width)  5.1 us
    dot_general x2, matrix products, window_terms(): jnp.einsum('thk,kc->thc', grad_b, lat_all, preferred_element_type=jnp.flo...  4.82 us
  transfers between devices with their start and end apart: 8, of which 6 were waited for; matrix products, arithmetic and copies ran while one was open for 24% of the time, Pallas kernels for 0%

profile of v2, /device:TPU:6, one launch (start us, length us, event | category | flops | bytes accessed | tf_op | source)
XLA Modules:
  0.0 136.1 jit_solution(4674753307504595613)
XLA Ops:
  2.5 2.1 %collective-permute-start = (bf16[1,128,576]{1,2,0:T(8,128)(2,1)S(1)}, bf16[1,128,576]{1,2,0:T(8,128)(2,1)S(1)}, u32[]{:S(2)}, u32[]{:S(2)}) collective-permute-start(bf16[1,128,576]{1,2,0:T(8,128)(2,1)S(1)} %maximum_bitcast_fusion), channel_id=1, source_target_pairs={{0,8},{8,16},{16,24},{24,32},{32,40},{40,48},{48,56},{56,64},{64,7... | collective-permute-start | bytes 442376 | tf_op jit(solution)/shard_map/ppermute | solution.py:14
  7.6 1.9 %copy.86 = bf16[128,8,512]{0,2,1:T(8,128)(2,1)S(1)} copy(bf16[128,8,512]{2,1,0:T(8,128)(2,1)} %param.8) | data formatting | bytes 2097152 | tf_op args[0]
  9.6 7.5 %collective-permute-done = bf16[1,128,576]{1,2,0:T(8,128)(2,1)S(1)} collective-permute-done((bf16[1,128,576]{1,2,0:T(8,128)(2,1)S(1)}, bf16[1,128,576]{1,2,0:T(8,128)(2,1)S(1)}, u32[]{:S(2)}, u32[]{:S(2)}) %collective-permute-start) | collective-permute-done | bytes 147488 | tf_op jit(solution)/shard_map/ppermute | solution.py:14
  17.2 1.9 %collective-permute-start.1 = (bf16[2,128,576]{1,2,0:T(8,128)(2,1)S(1)}, bf16[2,128,576]{1,2,0:T(8,128)(2,1)S(1)}, u32[]{:S(2)}, u32[]{:S(2)}) collective-permute-start(bf16[2,128,576]{1,2,0:T(8,128)(2,1)S(1)} %pad_maximum_fusion.3), channel_id=1, source_target_pairs={{0,16},{8,24},{16,32},{24,40},{32,48},{40,56},{48,64},{56,72},{64,... | collective-permute-start | bytes 884744 | tf_op jit(solution)/shard_map/ppermute | solution.py:14
  19.3 10.1 %collective-permute-done.1 = bf16[2,128,576]{1,2,0:T(8,128)(2,1)S(1)} collective-permute-done((bf16[2,128,576]{1,2,0:T(8,128)(2,1)S(1)}, bf16[2,128,576]{1,2,0:T(8,128)(2,1)S(1)}, u32[]{:S(2)}, u32[]{:S(2)}) %collective-permute-start.1) | collective-permute-done | bytes 294944 | tf_op jit(solution)/shard_map/ppermute | solution.py:14
  30.3 2.0 %collective-permute-start.2 = (bf16[4,128,576]{1,2,0:T(8,128)(2,1)}, bf16[4,128,576]{1,2,0:T(8,128)(2,1)}, u32[]{:S(2)}, u32[]{:S(2)}) collective-permute-start(bf16[4,128,576]{1,2,0:T(8,128)(2,1)} %pad_maximum_fusion.2), channel_id=1, source_target_pairs={{0,32},{8,40},{16,48},{24,56},{32,64},{40,72},{48,80},{56,88},{64,... | collective-permute-start | bytes 1769480 | tf_op jit(solution)/shard_map/ppermute | solution.py:14
  34.1 2.3 %fusion.8 = f32[128,8,512]{0,2,1:T(8,128)} fusion(f32[512,128,8]{1,0,2:T(8,128)S(1)} %fusion.21, bf16[128,8,512]{0,2,1:T(8,128)(2,1)S(1)} %copy.86, f32[128,8]{0,1:T(8,128)S(1)} %copy-done.11, pred[128,512]{0,1:T(8,128)(4,1)S(1)} %get-tuple-element.17, bf16[512,576]{1,0:T(8,128)(2,1)S(1)} %bitcast.104), kind=kOutput, calls=%fused_computation.13 | convolution fusion | flops 539492352 | bytes 5836800 | tf_op jit(solution)/shard_map/thc,kc->thk/dot_general | solution.py:27
  36.5 25.3 %collective-permute-done.2 = bf16[4,128,576]{1,2,0:T(8,128)(2,1)} collective-permute-done((bf16[4,128,576]{1,2,0:T(8,128)(2,1)}, bf16[4,128,576]{1,2,0:T(8,128)(2,1)}, u32[]{:S(2)}, u32[]{:S(2)}) %collective-permute-start.2) | collective-permute-done | bytes 589856 | tf_op jit(solution)/shard_map/ppermute | solution.py:14
  69.4 2.7 %copy.97 = f32[512,576]{1,0:T(8,128)} copy(f32[512,576]{0,1:T(8,128)} %pad_maximum_fusion.1) | data formatting | bytes 2359296 | tf_op jit(solution)/shard_map/concatenate | solution.py:45
  72.1 2.5 %copy.98 = f32[4,8,16,576]{3,2,0,1:T(8,128)} copy(f32[4,8,16,576]{3,2,1,0:T(8,128)} %bitcast.108) | data formatting | bytes 2359296 | tf_op jit(solution)/shard_map/reshape | solution.py:69
  74.6 5.9 %all-to-all-start.1 = ((f32[4,8,16,576]{3,2,0,1:T(8,128)}), f32[4,8,16,576]{3,2,0,1:T(8,128)}, u32[]{:S(2)}, u32[]{:S(2)}) async-start(f32[4,8,16,576]{3,2,0,1:T(8,128)} %copy.98), calls=%async_computation.1 | async-start | bytes 2621440 | tf_op jit(solution)/shard_map/all_to_all | solution.py:70
  80.6 2.6 %fusion.4 = bf16[128,8,512]{0,2,1:T(8,128)(2,1)S(1)} fusion(f32[128,8,512]{0,2,1:T(8,128)} %fusion.8, bf16[128,8,512]{0,2,1:T(8,128)(2,1)S(1)} %copy.88, f32[128,8]{0,1:T(8,128)S(1)} %copy.106, bf16[512,576]{1,0:T(8,128)(2,1)} %bitcast.105), kind=kOutput, calls=%fused_computation.7 | convolution fusion | flops 538443776 | bytes 4722688 | tf_op jit(solution)/shard_map/thc,kc->thk/dot_general | solution.py:33
  86.7 2.7 %copy.90 = f32[512,576]{1,0:T(8,128)} copy(f32[512,576]{0,1:T(8,128)} %pad_maximum_fusion) | data formatting | bytes 2359296 | tf_op jit(solution)/shard_map/concatenate | solution.py:45
  89.5 2.6 %copy.91 = f32[4,8,16,576]{3,2,0,1:T(8,128)} copy(f32[4,8,16,576]{3,2,1,0:T(8,128)} %bitcast.109) | data formatting | bytes 2359296 | tf_op jit(solution)/shard_map/reshape | solution.py:69
  92.0 3.2 %all-to-all-done.1 = f32[4,8,16,576]{3,2,0,1:T(8,128)} async-done(((f32[4,8,16,576]{3,2,0,1:T(8,128)}), f32[4,8,16,576]{3,2,0,1:T(8,128)}, u32[]{:S(2)}, u32[]{:S(2)}) %all-to-all-start.1) | async-done | bytes 1179680 | tf_op jit(solution)/shard_map/all_to_all | solution.py:70
  95.3 4.7 %all-to-all-start = ((f32[4,8,16,576]{3,2,0,1:T(8,128)}), f32[4,8,16,576]{3,2,0,1:T(8,128)}, u32[]{:S(2)}, u32[]{:S(2)}) async-start(f32[4,8,16,576]{3,2,0,1:T(8,128)} %copy.91), calls=%async_computation | async-start | bytes 2621440 | tf_op jit(solution)/shard_map/all_to_all | solution.py:70
  100.0 2.1 %fusion.19 = f32[128,8,512]{2,0,1:T(8,128)} fusion(bf16[128,8,512]{0,2,1:T(8,128)(2,1)S(1)} %fusion.4, bf16[512,576]{1,0:T(8,128)(2,1)S(1)} %bitcast.106), kind=kOutput, calls=%fused_computation.38 | convolution fusion | flops 536870912 | bytes 3670016 | tf_op jit(solution)/shard_map/thk,kc->thc/dot_general | solution.py:37
  102.1 2.1 %reduce_sum.19 = f32[4,16,576]{2,1,0:T(8,128)} reduce(f32[4,8,16,576]{3,2,0,1:T(8,128)} %all-to-all-done.1, f32[]{:T(128)} %constant.22.clone.1), dimensions={1}, to_apply=%region_1.2 | reduce | flops 258048 | bytes 1327108 | tf_op jit(solution)/shard_map/reduce_sum | solution.py:70
  104.1 6.4 %collective-permute-start.3 = (f32[4,16,576]{2,1,0:T(8,128)}, f32[4,16,576]{2,1,0:T(8,128)}, u32[]{:S(2)}, u32[]{:S(2)}) collective-permute-start(f32[4,16,576]{2,1,0:T(8,128)} %reduce_sum.19), channel_id=1, source_target_pairs={{32,0},{40,8},{48,16},{56,24},{64,32},{72,40},{80,48},{88,56},{96,... | collective-permute-start | bytes 442376 | tf_op jit(solution)/shard_map/ppermute | solution.py:14
  110.9 5.7 %all-to-all-done = f32[4,8,16,576]{3,2,0,1:T(8,128)} async-done(((f32[4,8,16,576]{3,2,0,1:T(8,128)}), f32[4,8,16,576]{3,2,0,1:T(8,128)}, u32[]{:S(2)}, u32[]{:S(2)}) %all-to-all-start) | async-done | bytes 1179680 | tf_op jit(solution)/shard_map/all_to_all | solution.py:70
  116.5 2.1 %reduce_sum.18 = f32[4,16,576]{2,1,0:T(8,128)} reduce(f32[4,8,16,576]{3,2,0,1:T(8,128)} %all-to-all-done, f32[]{:T(128)} %constant.22.clone.1), dimensions={1}, to_apply=%region_0.1 | reduce | flops 258048 | bytes 1327108 | tf_op jit(solution)/shard_map/reduce_sum | solution.py:70
  119.6 1.9 %collective-permute-start.4 = (f32[2,16,576]{2,1,0:T(8,128)S(1)}, f32[2,16,576]{2,1,0:T(8,128)S(1)}, u32[]{:S(2)}, u32[]{:S(2)}) collective-permute-start(f32[2,16,576]{2,1,0:T(8,128)S(1)} %slice.47), channel_id=1, source_target_pairs={{16,0},{24,8},{32,16},{40,24},{48,32},{56,40},{64,48},{72,56},{80,... | collective-permute-start | bytes 221192 | tf_op jit(solution)/shard_map/ppermute | solution.py:14
  121.5 2.8 %multiply_convert_fusion = bf16[128,8,512]{2,0,1:T(8,128)(2,1)} fusion(f32[128,8,512]{2,0,1:T(8,128)S(1)} %copy-done.2, bf16[128,8,512]{0,2,1:T(8,128)(2,1)S(1)} %fusion, bf16[512,576]{1,0:T(8,128)(2,1)} %bitcast.101), kind=kOutput, calls=%fused_computation.14 | convolution fusion | flops 538443776 | bytes 4718592 | tf_op jit(solution)/shard_map/thk,kc->thc/dot_general | solution.py:37
  126.0 5.3 %collective-permute-start.5 = (f32[1,16,576]{2,1,0:T(8,128)S(1)}, f32[1,16,576]{2,1,0:T(8,128)S(1)}, u32[]{:S(2)}, u32[]{:S(2)}) collective-permute-start(f32[1,16,576]{2,1,0:T(8,128)S(1)} %slice.49), channel_id=1, source_target_pairs={{8,0},{16,8},{24,16},{32,24},{40,32},{48,40},{56,48},{64,56},{72,6... | collective-permute-start | bytes 110600 | tf_op jit(solution)/shard_map/ppermute | solution.py:14
  (63 shorter events, 26.7 us)
Async XLA Ops:
  0.6 5.8 %copy-start.7 = (bf16[128,8,512]{2,1,0:T(8,128)(2,1)S(1)}, bf16[128,8,512]{2,1,0:T(8,128)(2,1)}, u32[]{:S(2)}) copy-start(bf16[128,8,512]{2,1,0:T(8,128)(2,1)} %param.11) | copy-start | bytes 3145732
  2.5 5.0 %copy-start.9 = (bf16[128,512]{1,0:T(8,128)(2,1)S(1)}, bf16[128,512]{1,0:T(8,128)(2,1)}, u32[]{:S(2)}) copy-start(bf16[128,512]{1,0:T(8,128)(2,1)} %param.9) | copy-start | bytes 393220
  2.5 14.6 %collective-permute-start = (bf16[1,128,576]{1,2,0:T(8,128)(2,1)S(1)}, bf16[1,128,576]{1,2,0:T(8,128)(2,1)S(1)}, u32[]{:S(2)}, u32[]{:S(2)}) collective-permute-start(bf16[1,128,576]{1,2,0:T(8,128)(2,1)S(1)} %maximum_bitcast_fusion), channel_id=1, source_target_pairs={{0,8},{8,16},{16,24},{24,32},{32,40},{40,48},{48,56},{56,64},{64,7... | collective-permute-start | bytes 442376 | tf_op jit(solution)/shard_map/ppermute | solution.py:14
  6.5 12.7 %copy-start.10 = (s32[128]{0:T(128)S(1)}, s32[128]{0:T(128)}, u32[]{:S(2)}) copy-start(s32[128]{0:T(128)} %param.15) | copy-start | bytes 1540
  9.6 57.9 %copy-start = (bf16[128,8,512]{0,2,1:T(8,128)(2,1)}, bf16[128,8,512]{0,2,1:T(8,128)(2,1)S(1)}, u32[]{:S(2)}) copy-start(bf16[128,8,512]{0,2,1:T(8,128)(2,1)S(1)} %copy.86) | copy-start | bytes 3145732
  17.2 12.2 %collective-permute-start.1 = (bf16[2,128,576]{1,2,0:T(8,128)(2,1)S(1)}, bf16[2,128,576]{1,2,0:T(8,128)(2,1)S(1)}, u32[]{:S(2)}, u32[]{:S(2)}) collective-permute-start(bf16[2,128,576]{1,2,0:T(8,128)(2,1)S(1)} %pad_maximum_fusion.3), channel_id=1, source_target_pairs={{0,16},{8,24},{16,32},{24,40},{32,48},{40,56},{48,64},{56,72},{64,... | collective-permute-start | bytes 884744 | tf_op jit(solution)/shard_map/ppermute | solution.py:14
  30.3 3.8 %copy-start.11 = (f32[128,8]{0,1:T(8,128)S(1)}, f32[128,8]{0,1:T(8,128)}, u32[]{:S(2)}) copy-start(f32[128,8]{0,1:T(8,128)} %param.12) | copy-start | bytes 12292
  30.3 31.5 %collective-permute-start.2 = (bf16[4,128,576]{1,2,0:T(8,128)(2,1)}, bf16[4,128,576]{1,2,0:T(8,128)(2,1)}, u32[]{:S(2)}, u32[]{:S(2)}) collective-permute-start(bf16[4,128,576]{1,2,0:T(8,128)(2,1)} %pad_maximum_fusion.2), channel_id=1, source_target_pairs={{0,32},{8,40},{16,48},{24,56},{32,64},{40,72},{48,80},{56,88},{64,... | collective-permute-start | bytes 1769480 | tf_op jit(solution)/shard_map/ppermute | solution.py:14
  33.7 2.7 %copy-start.5 = (bf16[4,128,576]{2,1,0:T(8,128)(2,1)}, bf16[4,128,576]{2,1,0:T(8,128)(2,1)S(1)}, u32[]{:S(2)}) copy-start(bf16[4,128,576]{2,1,0:T(8,128)(2,1)S(1)} %copy.70) | copy-start | bytes 1769476
  63.1 1.4 %copy-start.4 = (bf16[4,128,576]{2,1,0:T(8,128)(2,1)}, bf16[4,128,576]{2,1,0:T(8,128)(2,1)S(1)}, u32[]{:S(2)}) copy-start(bf16[4,128,576]{2,1,0:T(8,128)(2,1)S(1)} %copy.76) | copy-start | bytes 1769476
  74.6 20.6 %all-to-all-start.1 = ((f32[4,8,16,576]{3,2,0,1:T(8,128)}), f32[4,8,16,576]{3,2,0,1:T(8,128)}, u32[]{:S(2)}, u32[]{:S(2)}) async-start(f32[4,8,16,576]{3,2,0,1:T(8,128)} %copy.98), calls=%async_computation.1 | async-start | bytes 2621440 | tf_op jit(solution)/shard_map/all_to_all | solution.py:70
  80.6 3.1 %copy-start.3 = (f32[128,8,512]{0,2,1:T(8,128)S(1)}, f32[128,8,512]{0,2,1:T(8,128)}, u32[]{:S(2)}) copy-start(f32[128,8,512]{0,2,1:T(8,128)} %fusion.8) | copy-start | bytes 6291460
  83.6 1.2 copy-start.1
  89.5 10.5 %copy-start.6 = (bf16[4,128,576]{2,1,0:T(8,128)(2,1)S(1)}, bf16[4,128,576]{2,1,0:T(8,128)(2,1)}, u32[]{:S(2)}) copy-start(bf16[4,128,576]{2,1,0:T(8,128)(2,1)} %copy-done.5) | copy-start | bytes 1769476
  95.3 21.3 %all-to-all-start = ((f32[4,8,16,576]{3,2,0,1:T(8,128)}), f32[4,8,16,576]{3,2,0,1:T(8,128)}, u32[]{:S(2)}, u32[]{:S(2)}) async-start(f32[4,8,16,576]{3,2,0,1:T(8,128)} %copy.91), calls=%async_computation | async-start | bytes 2621440 | tf_op jit(solution)/shard_map/all_to_all | solution.py:70
  104.1 14.5 %collective-permute-start.3 = (f32[4,16,576]{2,1,0:T(8,128)}, f32[4,16,576]{2,1,0:T(8,128)}, u32[]{:S(2)}, u32[]{:S(2)}) collective-permute-start(f32[4,16,576]{2,1,0:T(8,128)} %reduce_sum.19), channel_id=1, source_target_pairs={{32,0},{40,8},{48,16},{56,24},{64,32},{72,40},{80,48},{88,56},{96,... | collective-permute-start | bytes 442376 | tf_op jit(solution)/shard_map/ppermute | solution.py:14
  110.8 10.7 %copy-start.2 = (f32[128,8,512]{2,0,1:T(8,128)S(1)}, f32[128,8,512]{2,0,1:T(8,128)}, u32[]{:S(2)}) copy-start(f32[128,8,512]{2,0,1:T(8,128)} %fusion.19) | copy-start | bytes 6291460
  119.6 6.3 %collective-permute-start.4 = (f32[2,16,576]{2,1,0:T(8,128)S(1)}, f32[2,16,576]{2,1,0:T(8,128)S(1)}, u32[]{:S(2)}, u32[]{:S(2)}) collective-permute-start(f32[2,16,576]{2,1,0:T(8,128)S(1)} %slice.47), channel_id=1, source_target_pairs={{16,0},{24,8},{32,16},{40,24},{48,32},{56,40},{64,48},{72,56},{80,... | collective-permute-start | bytes 221192 | tf_op jit(solution)/shard_map/ppermute | solution.py:14
  124.3 9.0 %copy-start.8 = (bf16[128,8,512]{2,0,1:T(8,128)(2,1)S(1)}, bf16[128,8,512]{2,0,1:T(8,128)(2,1)}, u32[]{:S(2)}) copy-start(bf16[128,8,512]{2,0,1:T(8,128)(2,1)} %multiply_convert_fusion) | copy-start | bytes 3145732
  126.0 8.9 %collective-permute-start.5 = (f32[1,16,576]{2,1,0:T(8,128)S(1)}, f32[1,16,576]{2,1,0:T(8,128)S(1)}, u32[]{:S(2)}, u32[]{:S(2)}) collective-permute-start(f32[1,16,576]{2,1,0:T(8,128)S(1)} %slice.49), channel_id=1, source_target_pairs={{8,0},{16,8},{24,16},{32,24},{40,32},{48,40},{56,48},{64,56},{72,6... | collective-permute-start | bytes 110600 | tf_op jit(solution)/shard_map/ppermute | solution.py:14

commit v3 on v2

--- a/solution.py
+++ b/solution.py
@@ -69,12 +69,21 @@
         part = part.reshape(-1, groups, block, lat_width + rope_width)
         return lax.all_to_all(part, "head", 1, 1, tiled=True).sum(axis=1)
 
-    near = jnp.concatenate([latent, key_rope], axis=1)[None]
+    keys = jnp.concatenate([latent, key_rope], axis=1)
+    rows = lax.dynamic_slice_in_dim(keys, lax.axis_index("head") * block, block, axis=0)[None]
     width = 1
     while width < half_span:
-        near = jnp.concatenate([shifted(near, "ctx", width), near], axis=0)
+        rows = jnp.concatenate([shifted(rows, "ctx", width), rows], axis=0)
         width *= 2
-    far = shifted(near, "ctx", half_span)
+    far_rows = shifted(rows, "ctx", half_span)
+
+    def assemble(part):
+        spread = jnp.broadcast_to(part[None], (groups,) + part.shape)
+        got = lax.all_to_all(spread, "head", 0, 0, tiled=True)
+        return got.transpose(1, 0, 2, 3)
+
+    near = assemble(rows)
+    far = assemble(far_rows)
 
     near_qlat, near_qrot, near_part = terms(near, own_tile - half_span + 1)
     far_qlat, far_qrot, far_part = terms(far, own_tile - span + 1)

time: 137 us -> 122 us (0.89)
  waiting for transfers between devices: 53.4 us -> 40.4 us
  starting transfers between devices: 30.2 us -> 32.5 us
  other arithmetic: 11.2 us -> 9.37 us
  local copies, waits for them, and re-layouts: 21.6 us -> 19.8 us
    ppermute x6, waiting for transfers between devices: 44.5 us -> 26 us  [shifted(): return lax.ppermute(x, axis, pairs)]
    all_to_all x0 -> x2, starting transfers between devices: none -> 11.6 us  [assemble(): got = lax.all_to_all(spread, 'head', 0, 0, tiled=True)]
    ppermute x6, starting transfers between devices: 19.6 us -> 11.6 us  [shifted(): return lax.ppermute(x, axis, pairs)]
    all_to_all x0 -> x2, waiting for transfers between devices: none -> 3.62 us  [assemble(): got = lax.all_to_all(spread, 'head', 0, 0, tiled=True)]
    all_to_all x2, waiting for transfers between devices: 8.87 us -> 10.7 us  [group_sum(): return lax.all_to_all(part, 'head', 1, 1, tiled=True).sum(axis=1)]
    broadcast_in_dim x0 -> x2, local copies, waits for them, and re-layouts: none -> 1.82 us  [assemble(): spread = jnp.broadcast_to(part[None], (groups,) + part.shape)]
    unnamed x1, other arithmetic: 1.89 us -> 0.34 us
    all_to_all x2, starting transfers between devices: 10.7 us -> 9.28 us  [group_sum(): return lax.all_to_all(part, 'head', 1, 1, tiled=True).sum(axis=1)]
  transfers between devices with their start and end apart: 8 -> 10, of which waited for: 6 -> 7; matrix products, arithmetic and copies ran while one was open for 24% -> 27% of each run, Pallas kernels for 0% -> 0%
where the time goes in v3:
time: 122 us; the launch traced here: 121 us
  waiting for transfers between devices  40.4 us (33%)
  starting transfers between devices  32.5 us (27%)
  local copies, waits for them, and re-layouts  19.8 us (16%)
  matrix products  17.6 us (14%)
  other arithmetic  9.37 us (8%)
    ppermute x6, waiting for transfers between devices, shifted(): return lax.ppermute(x, axis, pairs)  26 us
    all_to_all x2, starting transfers between devices, assemble(): got = lax.all_to_all(spread, 'head', 0, 0, tiled=True)  11.6 us
    ppermute x6, starting transfers between devices, shifted(): return lax.ppermute(x, axis, pairs)  11.6 us
    all_to_all x2, waiting for transfers between devices, group_sum(): return lax.all_to_all(part, 'head', 1, 1, tiled=True).sum(axis=1)  10.7 us
    all_to_all x2, starting transfers between devices, group_sum(): return lax.all_to_all(part, 'head', 1, 1, tiled=True).sum(axis=1)  9.28 us
    unnamed x36, local copies, waits for them, and re-layouts  7.27 us
    dot_general x2, matrix products, window_terms(): jnp.einsum('thk,kc->thc', grad_b, lat_all, preferred_element_type=jnp.flo...  4.82 us
    concatenate x2, local copies, waits for them, and re-layouts, window_terms(): return (grad_qlat, grad_qrot, jnp.concatenate([grad_lat, grad_rot], axis=1))  4.41 us
  transfers between devices with their start and end apart: 10, of which 7 were waited for; matrix products, arithmetic and copies ran while one was open for 27% of the time, Pallas kernels for 0%

profile of v3, /device:TPU:6, one launch (start us, length us, event | category | flops | bytes accessed | tf_op | source)
XLA Modules:
  0.0 120.7 jit_solution(10222554880206912561)
XLA Ops:
  4.3 11.2 %collective-permute-done = bf16[1,16,576]{2,1,0:T(8,128)(2,1)S(1)} collective-permute-done((bf16[1,16,576]{2,1,0:T(8,128)(2,1)S(1)}, bf16[1,16,576]{2,1,0:T(8,128)(2,1)S(1)}, u32[]{:S(2)}, u32[]{:S(2)}) %collective-permute-start) | collective-permute-done | bytes 18464 | tf_op jit(solution)/shard_map/ppermute | solution.py:14
  15.5 1.9 %collective-permute-start.1 = (bf16[2,16,576]{2,1,0:T(8,128)(2,1)S(1)}, bf16[2,16,576]{2,1,0:T(8,128)(2,1)S(1)}, u32[]{:S(2)}, u32[]{:S(2)}) collective-permute-start(bf16[2,16,576]{2,1,0:T(8,128)(2,1)S(1)} %pad_maximum_fusion.3), channel_id=1, source_target_pairs={{0,16},{8,24},{16,32},{24,40},{32,48},{40,56},{48,64},{56,72},{64,... | collective-permute-start | bytes 110600 | tf_op jit(solution)/shard_map/ppermute | solution.py:14
  17.5 7.7 %collective-permute-done.1 = bf16[2,16,576]{2,1,0:T(8,128)(2,1)S(1)} collective-permute-done((bf16[2,16,576]{2,1,0:T(8,128)(2,1)S(1)}, bf16[2,16,576]{2,1,0:T(8,128)(2,1)S(1)}, u32[]{:S(2)}, u32[]{:S(2)}) %collective-permute-start.1) | collective-permute-done | bytes 36896 | tf_op jit(solution)/shard_map/ppermute | solution.py:14
  26.1 5.9 %all-to-all-start = ((bf16[8,4,16,576]{3,2,1,0:T(8,128)(2,1)}), bf16[8,4,16,576]{3,2,1,0:T(8,128)(2,1)}, u32[]{:S(2)}, u32[]{:S(2)}) async-start(bf16[8,4,16,576]{3,2,1,0:T(8,128)(2,1)} %broadcast_in_dim.57), calls=%async_computation | async-start | bytes 1310720 | tf_op jit(solution)/shard_map/all_to_all | solution.py:82
  32.9 2.0 %collective-permute-start.2 = (bf16[4,16,576]{2,1,0:T(8,128)(2,1)S(1)}, bf16[4,16,576]{2,1,0:T(8,128)(2,1)S(1)}, u32[]{:S(2)}, u32[]{:S(2)}) collective-permute-start(bf16[4,16,576]{2,1,0:T(8,128)(2,1)S(1)} %pad_maximum_fusion.2), channel_id=1, source_target_pairs={{0,32},{8,40},{16,48},{24,56},{32,64},{40,72},{48,80},{56,88},{64,... | collective-permute-start | bytes 221192 | tf_op jit(solution)/shard_map/ppermute | solution.py:14
  36.4 1.9 %copy.86 = bf16[128,8,512]{0,2,1:T(8,128)(2,1)S(1)} copy(bf16[128,8,512]{2,1,0:T(8,128)(2,1)} %param.8) | data formatting | bytes 2097152 | tf_op args[0]
  38.4 5.5 %collective-permute-done.2 = bf16[4,16,576]{2,1,0:T(8,128)(2,1)S(1)} collective-permute-done((bf16[4,16,576]{2,1,0:T(8,128)(2,1)S(1)}, bf16[4,16,576]{2,1,0:T(8,128)(2,1)S(1)}, u32[]{:S(2)}, u32[]{:S(2)}) %collective-permute-start.2) | collective-permute-done | bytes 73760 | tf_op jit(solution)/shard_map/ppermute | solution.py:14
  44.9 5.7 %all-to-all-start.1 = ((bf16[8,4,16,576]{3,2,1,0:T(8,128)(2,1)}), bf16[8,4,16,576]{3,2,1,0:T(8,128)(2,1)S(1)}, u32[]{:S(2)}, u32[]{:S(2)}) async-start(bf16[8,4,16,576]{3,2,1,0:T(8,128)(2,1)} %broadcast_in_dim.60), calls=%async_computation.1 | async-start | bytes 1310720 | tf_op jit(solution)/shard_map/all_to_all | solution.py:82
  52.6 2.3 %fusion.8 = f32[128,8,512]{0,2,1:T(8,128)} fusion(f32[512,128,8]{1,0,2:T(8,128)S(1)} %fusion.21, bf16[128,8,512]{0,2,1:T(8,128)(2,1)S(1)} %copy.86, f32[128,8]{0,1:T(8,128)S(1)} %copy-done.14, pred[128,512]{0,1:T(8,128)(4,1)S(1)} %copy-done.12, bf16[512,576]{1,0:T(8,128)(2,1)S(1)} %bitcast.106), kind=kOutput, calls=%fused_computation.13 | convolution fusion | flops 539492352 | bytes 5836800 | tf_op jit(solution)/shard_map/thc,kc->thk/dot_general | solution.py:27
  54.9 3.6 %all-to-all-done.1 = bf16[8,4,16,576]{3,2,1,0:T(8,128)(2,1)S(1)} async-done(((bf16[8,4,16,576]{3,2,1,0:T(8,128)(2,1)}), bf16[8,4,16,576]{3,2,1,0:T(8,128)(2,1)S(1)}, u32[]{:S(2)}, u32[]{:S(2)}) %all-to-all-start.1) | async-done | bytes 589856 | tf_op jit(solution)/shard_map/all_to_all | solution.py:82
  66.6 5.1 %all-to-all-start.3 = ((f32[4,8,16,576]{3,2,0,1:T(8,128)}), f32[4,8,16,576]{3,2,0,1:T(8,128)}, u32[]{:S(2)}, u32[]{:S(2)}) async-start(f32[4,8,16,576]{3,2,0,1:T(8,128)} %copy.98), calls=%async_computation.3 | async-start | bytes 2621440 | tf_op jit(solution)/shard_map/all_to_all | solution.py:70
  71.7 2.6 %fusion.4 = bf16[128,8,512]{0,2,1:T(8,128)(2,1)S(1)} fusion(f32[128,8,512]{0,2,1:T(8,128)} %fusion.8, bf16[128,8,512]{0,2,1:T(8,128)(2,1)S(1)} %copy.88, f32[128,8]{0,1:T(8,128)S(1)} %copy.106, bf16[512,576]{1,0:T(8,128)(2,1)} %bitcast.107), kind=kOutput, calls=%fused_computation.7 | convolution fusion | flops 538443776 | bytes 4722688 | tf_op jit(solution)/shard_map/thc,kc->thk/dot_general | solution.py:33
  77.8 2.7 %copy.90 = f32[512,576]{1,0:T(8,128)} copy(f32[512,576]{0,1:T(8,128)} %pad_maximum_fusion) | data formatting | bytes 2359296 | tf_op jit(solution)/shard_map/concatenate | solution.py:45
  80.6 2.6 %copy.91 = f32[4,8,16,576]{3,2,0,1:T(8,128)} copy(f32[4,8,16,576]{3,2,1,0:T(8,128)} %bitcast.111) | data formatting | bytes 2359296 | tf_op jit(solution)/shard_map/reshape | solution.py:69
  83.2 6.3 %all-to-all-done.3 = f32[4,8,16,576]{3,2,0,1:T(8,128)} async-done(((f32[4,8,16,576]{3,2,0,1:T(8,128)}), f32[4,8,16,576]{3,2,0,1:T(8,128)}, u32[]{:S(2)}, u32[]{:S(2)}) %all-to-all-start.3) | async-done | bytes 1179680 | tf_op jit(solution)/shard_map/all_to_all | solution.py:70
  89.4 4.2 %all-to-all-start.2 = ((f32[4,8,16,576]{3,2,0,1:T(8,128)}), f32[4,8,16,576]{3,2,0,1:T(8,128)}, u32[]{:S(2)}, u32[]{:S(2)}) async-start(f32[4,8,16,576]{3,2,0,1:T(8,128)} %copy.91), calls=%async_computation.2 | async-start | bytes 2621440 | tf_op jit(solution)/shard_map/all_to_all | solution.py:70
  93.7 2.1 %fusion.19 = f32[128,8,512]{2,0,1:T(8,128)} fusion(bf16[128,8,512]{0,2,1:T(8,128)(2,1)S(1)} %fusion.4, bf16[512,576]{1,0:T(8,128)(2,1)S(1)} %bitcast.108), kind=kOutput, calls=%fused_computation.36 | convolution fusion | flops 536870912 | bytes 3670016 | tf_op jit(solution)/shard_map/thk,kc->thc/dot_general | solution.py:37
  95.8 2.1 %reduce_sum.19 = f32[4,16,576]{2,1,0:T(8,128)} reduce(f32[4,8,16,576]{3,2,0,1:T(8,128)} %all-to-all-done.3, f32[]{:T(128)} %constant.29.clone.1), dimensions={1}, to_apply=%region_1.2 | reduce | flops 258048 | bytes 1327108 | tf_op jit(solution)/shard_map/reduce_sum | solution.py:70
  97.8 1.9 %collective-permute-start.3 = (f32[4,16,576]{2,1,0:T(8,128)}, f32[4,16,576]{2,1,0:T(8,128)}, u32[]{:S(2)}, u32[]{:S(2)}) collective-permute-start(f32[4,16,576]{2,1,0:T(8,128)} %reduce_sum.19), channel_id=1, source_target_pairs={{32,0},{40,8},{48,16},{56,24},{64,32},{72,40},{80,48},{88,56},{96,... | collective-permute-start | bytes 442376 | tf_op jit(solution)/shard_map/ppermute | solution.py:14
  100.1 4.5 %all-to-all-done.2 = f32[4,8,16,576]{3,2,0,1:T(8,128)} async-done(((f32[4,8,16,576]{3,2,0,1:T(8,128)}), f32[4,8,16,576]{3,2,0,1:T(8,128)}, u32[]{:S(2)}, u32[]{:S(2)}) %all-to-all-start.2) | async-done | bytes 1179680 | tf_op jit(solution)/shard_map/all_to_all | solution.py:70
  104.5 2.1 %reduce_sum.18 = f32[4,16,576]{2,1,0:T(8,128)} reduce(f32[4,8,16,576]{3,2,0,1:T(8,128)} %all-to-all-done.2, f32[]{:T(128)} %constant.29.clone.1), dimensions={1}, to_apply=%region_0.1 | reduce | flops 258048 | bytes 1327108 | tf_op jit(solution)/shard_map/reduce_sum | solution.py:70
  107.6 1.9 %collective-permute-start.4 = (f32[2,16,576]{2,1,0:T(8,128)S(1)}, f32[2,16,576]{2,1,0:T(8,128)S(1)}, u32[]{:S(2)}, u32[]{:S(2)}) collective-permute-start(f32[2,16,576]{2,1,0:T(8,128)S(1)} %slice.47), channel_id=1, source_target_pairs={{16,0},{24,8},{32,16},{40,24},{48,32},{56,40},{64,48},{72,56},{80,... | collective-permute-start | bytes 221192 | tf_op jit(solution)/shard_map/ppermute | solution.py:14
  109.6 2.8 %multiply_convert_fusion = bf16[128,8,512]{2,0,1:T(8,128)(2,1)} fusion(f32[128,8,512]{2,0,1:T(8,128)S(1)} %copy-done.2, bf16[128,8,512]{0,2,1:T(8,128)(2,1)S(1)} %fusion, bf16[512,576]{1,0:T(8,128)(2,1)} %bitcast.103), kind=kOutput, calls=%fused_computation.14 | convolution fusion | flops 538443776 | bytes 4718592 | tf_op jit(solution)/shard_map/thk,kc->thc/dot_general | solution.py:37
  114.0 1.9 %collective-permute-start.5 = (f32[1,16,576]{2,1,0:T(8,128)S(1)}, f32[1,16,576]{2,1,0:T(8,128)S(1)}, u32[]{:S(2)}, u32[]{:S(2)}) collective-permute-start(f32[1,16,576]{2,1,0:T(8,128)S(1)} %slice.49), channel_id=1, source_target_pairs={{8,0},{16,8},{24,16},{32,24},{40,32},{48,40},{56,48},{64,56},{72,6... | collective-permute-start | bytes 110600 | tf_op jit(solution)/shard_map/ppermute | solution.py:14
  (75 shorter events, 29.2 us)
Async XLA Ops:
  0.6 31.4 %copy-start.13 = (s32[128]{0:T(128)S(1)}, s32[128]{0:T(128)}, u32[]{:S(2)}) copy-start(s32[128]{0:T(128)} %param.15) | copy-start | bytes 1540
  0.6 34.3 %copy-start.7 = (bf16[128,8,512]{2,1,0:T(8,128)(2,1)S(1)}, bf16[128,8,512]{2,1,0:T(8,128)(2,1)}, u32[]{:S(2)}) copy-start(bf16[128,8,512]{2,1,0:T(8,128)(2,1)} %param.11) | copy-start | bytes 3145732
  0.7 34.3 %copy-start.9 = (bf16[128,8,512]{2,1,0:T(8,128)(2,1)S(1)}, bf16[128,8,512]{2,1,0:T(8,128)(2,1)}, u32[]{:S(2)}) copy-start(bf16[128,8,512]{2,1,0:T(8,128)(2,1)} %param.10) | copy-start | bytes 3145732
  2.4 13.1 %collective-permute-start = (bf16[1,16,576]{2,1,0:T(8,128)(2,1)S(1)}, bf16[1,16,576]{2,1,0:T(8,128)(2,1)S(1)}, u32[]{:S(2)}, u32[]{:S(2)}) collective-permute-start(bf16[1,16,576]{2,1,0:T(8,128)(2,1)S(1)} %fusion.26), channel_id=1, source_target_pairs={{0,8},{8,16},{16,24},{24,32},{32,40},{40,48},{48,56},{56,64},{64,7... | collective-permute-start | bytes 55304 | tf_op jit(solution)/shard_map/ppermute | solution.py:14
  15.5 9.6 %collective-permute-start.1 = (bf16[2,16,576]{2,1,0:T(8,128)(2,1)S(1)}, bf16[2,16,576]{2,1,0:T(8,128)(2,1)S(1)}, u32[]{:S(2)}, u32[]{:S(2)}) collective-permute-start(bf16[2,16,576]{2,1,0:T(8,128)(2,1)S(1)} %pad_maximum_fusion.3), channel_id=1, source_target_pairs={{0,16},{8,24},{16,32},{24,40},{32,48},{40,56},{48,64},{56,72},{64,... | collective-permute-start | bytes 110600 | tf_op jit(solution)/shard_map/ppermute | solution.py:14
  26.1 17.9 %all-to-all-start = ((bf16[8,4,16,576]{3,2,1,0:T(8,128)(2,1)}), bf16[8,4,16,576]{3,2,1,0:T(8,128)(2,1)}, u32[]{:S(2)}, u32[]{:S(2)}) async-start(bf16[8,4,16,576]{3,2,1,0:T(8,128)(2,1)} %broadcast_in_dim.57), calls=%async_computation | async-start | bytes 1310720 | tf_op jit(solution)/shard_map/all_to_all | solution.py:82
  32.9 3.4 %copy-start.10 = (bf16[128,512]{1,0:T(8,128)(2,1)S(1)}, bf16[128,512]{1,0:T(8,128)(2,1)}, u32[]{:S(2)}) copy-start(bf16[128,512]{1,0:T(8,128)(2,1)} %param.9) | copy-start | bytes 393220
  32.9 11.1 %collective-permute-start.2 = (bf16[4,16,576]{2,1,0:T(8,128)(2,1)S(1)}, bf16[4,16,576]{2,1,0:T(8,128)(2,1)S(1)}, u32[]{:S(2)}, u32[]{:S(2)}) collective-permute-start(bf16[4,16,576]{2,1,0:T(8,128)(2,1)S(1)} %pad_maximum_fusion.2), channel_id=1, source_target_pairs={{0,32},{8,40},{16,48},{24,56},{32,64},{40,72},{48,80},{56,88},{64,... | collective-permute-start | bytes 221192 | tf_op jit(solution)/shard_map/ppermute | solution.py:14
  38.4 23.5 %copy-start = (bf16[128,8,512]{0,2,1:T(8,128)(2,1)}, bf16[128,8,512]{0,2,1:T(8,128)(2,1)S(1)}, u32[]{:S(2)}) copy-start(bf16[128,8,512]{0,2,1:T(8,128)(2,1)S(1)} %copy.86) | copy-start | bytes 3145732
  44.9 13.6 %all-to-all-start.1 = ((bf16[8,4,16,576]{3,2,1,0:T(8,128)(2,1)}), bf16[8,4,16,576]{3,2,1,0:T(8,128)(2,1)S(1)}, u32[]{:S(2)}, u32[]{:S(2)}) async-start(bf16[8,4,16,576]{3,2,1,0:T(8,128)(2,1)} %broadcast_in_dim.60), calls=%async_computation.1 | async-start | bytes 1310720 | tf_op jit(solution)/shard_map/all_to_all | solution.py:82
  50.6 2.0 %copy-start.12 = (pred[128,512]{0,1:T(8,128)(4,1)S(1)}, pred[128,512]{0,1:T(8,128)(4,1)}, u32[]{:S(2)}) copy-start(pred[128,512]{0,1:T(8,128)(4,1)} %get-tuple-element.17) | copy-start | bytes 196612
  50.6 2.0 %copy-start.14 = (f32[128,8]{0,1:T(8,128)S(1)}, f32[128,8]{0,1:T(8,128)}, u32[]{:S(2)}) copy-start(f32[128,8]{0,1:T(8,128)} %param.12) | copy-start | bytes 12292
  54.9 4.1 %copy-start.11 = (pred[128,512]{0,1:T(8,128)(4,1)S(1)}, pred[128,512]{0,1:T(8,128)(4,1)}, u32[]{:S(2)}) copy-start(pred[128,512]{0,1:T(8,128)(4,1)} %get-tuple-element.16) | copy-start | bytes 196612
  58.6 2.1 %copy-start.4 = (bf16[4,8,16,576]{3,2,1,0:T(8,128)(2,1)}, bf16[4,8,16,576]{3,2,1,0:T(8,128)(2,1)S(1)}, u32[]{:S(2)}) copy-start(bf16[4,8,16,576]{3,2,1,0:T(8,128)(2,1)S(1)} %copy.76) | copy-start | bytes 1769476
  66.6 22.8 %all-to-all-start.3 = ((f32[4,8,16,576]{3,2,0,1:T(8,128)}), f32[4,8,16,576]{3,2,0,1:T(8,128)}, u32[]{:S(2)}, u32[]{:S(2)}) async-start(f32[4,8,16,576]{3,2,0,1:T(8,128)} %copy.98), calls=%async_computation.3 | async-start | bytes 2621440 | tf_op jit(solution)/shard_map/all_to_all | solution.py:70
  71.7 3.1 %copy-start.3 = (f32[128,8,512]{0,2,1:T(8,128)S(1)}, f32[128,8,512]{0,2,1:T(8,128)}, u32[]{:S(2)}) copy-start(f32[128,8,512]{0,2,1:T(8,128)} %fusion.8) | copy-start | bytes 6291460
  74.8 1.2 %copy-start.1 = (bf16[128,8,512]{0,2,1:T(8,128)(2,1)S(1)}, bf16[128,8,512]{0,2,1:T(8,128)(2,1)}, u32[]{:S(2)}) copy-start(bf16[128,8,512]{0,2,1:T(8,128)(2,1)} %copy-done) | copy-start | bytes 3145732
  80.6 13.1 %copy-start.6 = (bf16[4,8,16,576]{3,2,1,0:T(8,128)(2,1)S(1)}, bf16[4,8,16,576]{3,2,1,0:T(8,128)(2,1)}, u32[]{:S(2)}) copy-start(bf16[4,8,16,576]{3,2,1,0:T(8,128)(2,1)} %copy-done.5) | copy-start | bytes 1769476
  89.4 15.1 %all-to-all-start.2 = ((f32[4,8,16,576]{3,2,0,1:T(8,128)}), f32[4,8,16,576]{3,2,0,1:T(8,128)}, u32[]{:S(2)}, u32[]{:S(2)}) async-start(f32[4,8,16,576]{3,2,0,1:T(8,128)} %copy.91), calls=%async_computation.2 | async-start | bytes 2621440 | tf_op jit(solution)/shard_map/all_to_all | solution.py:70
  97.8 8.8 %collective-permute-start.3 = (f32[4,16,576]{2,1,0:T(8,128)}, f32[4,16,576]{2,1,0:T(8,128)}, u32[]{:S(2)}, u32[]{:S(2)}) collective-permute-start(f32[4,16,576]{2,1,0:T(8,128)} %reduce_sum.19), channel_id=1, source_target_pairs={{32,0},{40,8},{48,16},{56,24},{64,32},{72,40},{80,48},{88,56},{96,... | collective-permute-start | bytes 442376 | tf_op jit(solution)/shard_map/ppermute | solution.py:14
  100.1 9.5 %copy-start.2 = (f32[128,8,512]{2,0,1:T(8,128)S(1)}, f32[128,8,512]{2,0,1:T(8,128)}, u32[]{:S(2)}) copy-start(f32[128,8,512]{2,0,1:T(8,128)} %fusion.19) | copy-start | bytes 6291460
  107.6 6.3 %collective-permute-start.4 = (f32[2,16,576]{2,1,0:T(8,128)S(1)}, f32[2,16,576]{2,1,0:T(8,128)S(1)}, u32[]{:S(2)}, u32[]{:S(2)}) collective-permute-start(f32[2,16,576]{2,1,0:T(8,128)S(1)} %slice.47), channel_id=1, source_target_pairs={{16,0},{24,8},{32,16},{40,24},{48,32},{56,40},{64,48},{72,56},{80,... | collective-permute-start | bytes 221192 | tf_op jit(solution)/shard_map/ppermute | solution.py:14
  112.3 5.6 %copy-start.8 = (bf16[128,8,512]{2,0,1:T(8,128)(2,1)S(1)}, bf16[128,8,512]{2,0,1:T(8,128)(2,1)}, u32[]{:S(2)}) copy-start(bf16[128,8,512]{2,0,1:T(8,128)(2,1)} %multiply_convert_fusion) | copy-start | bytes 3145732
  114.0 5.5 %collective-permute-start.5 = (f32[1,16,576]{2,1,0:T(8,128)S(1)}, f32[1,16,576]{2,1,0:T(8,128)S(1)}, u32[]{:S(2)}, u32[]{:S(2)}) collective-permute-start(f32[1,16,576]{2,1,0:T(8,128)S(1)} %slice.49), channel_id=1, source_target_pairs={{8,0},{16,8},{24,16},{32,24},{40,32},{48,40},{56,48},{64,56},{72,6... | collective-permute-start | bytes 110600 | tf_op jit(solution)/shard_map/ppermute | solution.py:14
  (1 other events, 0.8 us)

commit v4 on v3

--- a/solution.py
+++ b/solution.py
@@ -67,7 +67,9 @@
 
     def group_sum(part):
         part = part.reshape(-1, groups, block, lat_width + rope_width)
-        return lax.all_to_all(part, "head", 1, 1, tiled=True).sum(axis=1)
+        part = part.astype(jnp.bfloat16)
+        got = lax.all_to_all(part, "head", 1, 1, tiled=True)
+        return got.astype(jnp.float32).sum(axis=1)
 
     keys = jnp.concatenate([latent, key_rope], axis=1)
     rows = lax.dynamic_slice_in_dim(keys, lax.axis_index("head") * block, block, axis=0)[None]

time: 122 us -> 113 us (0.926)
  waiting for transfers between devices: 40.4 us -> 36.4 us
  other arithmetic: 9.37 us -> 6.95 us
  matrix products: 17.6 us -> 16.3 us
  local copies, waits for them, and re-layouts: 19.8 us -> 18.5 us
    all_to_all x2, waiting for transfers between devices: 10.7 us -> 4.03 us  [group_sum(): got = lax.all_to_all(part, 'head', 1, 1, tiled=True)]
    reshape x2 -> x0, local copies, waits for them, and re-layouts: 3.78 us -> none  [group_sum(): part = part.reshape(-1, groups, block, lat_width + rope_width)]
    ppermute x6, waiting for transfers between devices: 26 us -> 29.4 us  [shifted(): return lax.ppermute(x, axis, pairs)]
    convert_element_type x0 -> x2, local copies, waits for them, and re-layouts: none -> 2.91 us  [group_sum(): part = part.astype(jnp.bfloat16)]
    concatenate x2, local copies, waits for them, and re-layouts: 4.41 us -> 2.5 us  [window_terms(): return (grad_qlat, grad_qrot, jnp.concatenate([grad_lat, grad_rot], axis=1))]
    dot_general x2, matrix products: 3.33 us -> 1.45 us  [window_terms(): jnp.einsum('thc,kc->thk', grad_out, lat_all, preferred_element_type=jnp.f...]
    unnamed x36, local copies, waits for them, and re-layouts: 7.27 us -> 9.04 us
    dot_general x2, matrix products: 1.48 us -> 3.02 us  [window_terms(): jnp.einsum('thk,thc->kc', grad_b, q_latent, preferred_element_type=jnp.fl...]
  transfers between devices with their start and end apart: 10 -> 10, of which waited for: 7 -> 8; matrix products, arithmetic and copies ran while one was open for 27% -> 25% of each run, Pallas kernels for 0% -> 0%
where the time goes in v4:
time: 113 us; the launch traced here: 111 us
  waiting for transfers between devices  36.4 us (32%)
  starting transfers between devices  31.9 us (28%)
  local copies, waits for them, and re-layouts  18.5 us (16%)
  matrix products  16.3 us (14%)
  other arithmetic  6.95 us (6%)
    ppermute x6, waiting for transfers between devices, shifted(): return lax.ppermute(x, axis, pairs)  29.4 us
    ppermute x6, starting transfers between devices, shifted(): return lax.ppermute(x, axis, pairs)  11.8 us
    all_to_all x2, starting transfers between devices, assemble(): got = lax.all_to_all(spread, 'head', 0, 0, tiled=True)  11.6 us
    unnamed x36, local copies, waits for them, and re-layouts  9.04 us
    all_to_all x2, starting transfers between devices, group_sum(): got = lax.all_to_all(part, 'head', 1, 1, tiled=True)  8.49 us
    dot_general x2, matrix products, window_terms(): jnp.einsum('thk,kc->thc', grad_b, lat_all, preferred_element_type=jnp.flo...  4.4 us
    all_to_all x2, waiting for transfers between devices, group_sum(): got = lax.all_to_all(part, 'head', 1, 1, tiled=True)  4.03 us
    reduce_sum x2, other arithmetic, group_sum(): return got.astype(jnp.float32).sum(axis=1)  3.13 us
  transfers between devices with their start and end apart: 10, of which 8 were waited for; matrix products, arithmetic and copies ran while one was open for 25% of the time, Pallas kernels for 0%

profile of v4, /device:TPU:6, one launch (start us, length us, event | category | flops | bytes accessed | tf_op | source)
XLA Modules:
  0.0 111.1 jit_solution(12813400044123747417)
XLA Ops:
  2.4 1.9 %collective-permute-start = (bf16[1,16,576]{2,1,0:T(8,128)(2,1)S(1)}, bf16[1,16,576]{2,1,0:T(8,128)(2,1)S(1)}, u32[]{:S(2)}, u32[]{:S(2)}) collective-permute-start(bf16[1,16,576]{2,1,0:T(8,128)(2,1)S(1)} %fusion.30), channel_id=1, source_target_pairs={{0,8},{8,16},{16,24},{24,32},{32,40},{40,48},{48,56},{56,64},{64,7... | collective-permute-start | bytes 55304 | tf_op jit(solution)/shard_map/ppermute | solution.py:14
  4.3 11.2 %collective-permute-done = bf16[1,16,576]{2,1,0:T(8,128)(2,1)S(1)} collective-permute-done((bf16[1,16,576]{2,1,0:T(8,128)(2,1)S(1)}, bf16[1,16,576]{2,1,0:T(8,128)(2,1)S(1)}, u32[]{:S(2)}, u32[]{:S(2)}) %collective-permute-start) | collective-permute-done | bytes 18464 | tf_op jit(solution)/shard_map/ppermute | solution.py:14
  15.5 1.9 %collective-permute-start.1 = (bf16[2,16,576]{2,1,0:T(8,128)(2,1)S(1)}, bf16[2,16,576]{2,1,0:T(8,128)(2,1)S(1)}, u32[]{:S(2)}, u32[]{:S(2)}) collective-permute-start(bf16[2,16,576]{2,1,0:T(8,128)(2,1)S(1)} %pad_maximum_fusion.3), channel_id=1, source_target_pairs={{0,16},{8,24},{16,32},{24,40},{32,48},{40,56},{48,64},{56,72},{64,... | collective-permute-start | bytes 110600 | tf_op jit(solution)/shard_map/ppermute | solution.py:14
  17.5 7.7 %collective-permute-done.1 = bf16[2,16,576]{2,1,0:T(8,128)(2,1)S(1)} collective-permute-done((bf16[2,16,576]{2,1,0:T(8,128)(2,1)S(1)}, bf16[2,16,576]{2,1,0:T(8,128)(2,1)S(1)}, u32[]{:S(2)}, u32[]{:S(2)}) %collective-permute-start.1) | collective-permute-done | bytes 36896 | tf_op jit(solution)/shard_map/ppermute | solution.py:14
  26.1 5.9 %all-to-all-start = ((bf16[8,4,16,576]{3,2,1,0:T(8,128)(2,1)}), bf16[8,4,16,576]{3,2,1,0:T(8,128)(2,1)S(1)}, u32[]{:S(2)}, u32[]{:S(2)}) async-start(bf16[8,4,16,576]{3,2,1,0:T(8,128)(2,1)} %broadcast_in_dim.57), calls=%async_computation | async-start | bytes 1310720 | tf_op jit(solution)/shard_map/all_to_all | solution.py:84
  32.9 2.0 %collective-permute-start.2 = (bf16[4,16,576]{2,1,0:T(8,128)(2,1)S(1)}, bf16[4,16,576]{2,1,0:T(8,128)(2,1)}, u32[]{:S(2)}, u32[]{:S(2)}) collective-permute-start(bf16[4,16,576]{2,1,0:T(8,128)(2,1)S(1)} %pad_maximum_fusion.2), channel_id=1, source_target_pairs={{0,32},{8,40},{16,48},{24,56},{32,64},{40,72},{48,80},{56,88},{64,... | collective-permute-start | bytes 221192 | tf_op jit(solution)/shard_map/ppermute | solution.py:14
  36.4 2.7 %copy.86 = bf16[128,8,512]{0,2,1:T(8,128)(2,1)} copy(bf16[128,8,512]{2,1,0:T(8,128)(2,1)} %param.8) | data formatting | bytes 2097152 | tf_op args[0]
  39.1 4.9 %collective-permute-done.2 = bf16[4,16,576]{2,1,0:T(8,128)(2,1)} collective-permute-done((bf16[4,16,576]{2,1,0:T(8,128)(2,1)S(1)}, bf16[4,16,576]{2,1,0:T(8,128)(2,1)}, u32[]{:S(2)}, u32[]{:S(2)}) %collective-permute-start.2) | collective-permute-done | bytes 73760 | tf_op jit(solution)/shard_map/ppermute | solution.py:14
  45.9 5.7 %all-to-all-start.1 = ((bf16[8,4,16,576]{3,2,1,0:T(8,128)(2,1)}), bf16[8,4,16,576]{3,2,1,0:T(8,128)(2,1)S(1)}, u32[]{:S(2)}, u32[]{:S(2)}) async-start(bf16[8,4,16,576]{3,2,1,0:T(8,128)(2,1)} %broadcast_in_dim.60), calls=%async_computation.1 | async-start | bytes 1310720 | tf_op jit(solution)/shard_map/all_to_all | solution.py:84
  56.5 3.0 %all-to-all-done.1 = bf16[8,4,16,576]{3,2,1,0:T(8,128)(2,1)S(1)} async-done(((bf16[8,4,16,576]{3,2,1,0:T(8,128)(2,1)}), bf16[8,4,16,576]{3,2,1,0:T(8,128)(2,1)S(1)}, u32[]{:S(2)}, u32[]{:S(2)}) %all-to-all-start.1) | async-done | bytes 589856 | tf_op jit(solution)/shard_map/all_to_all | solution.py:84
  65.8 4.3 %all-to-all-start.3 = ((bf16[4,8,16,576]{3,2,0,1:T(8,128)(2,1)}), bf16[4,8,16,576]{3,2,0,1:T(8,128)(2,1)S(1)}, u32[]{:S(2)}, u32[]{:S(2)}) async-start(bf16[4,8,16,576]{3,2,0,1:T(8,128)(2,1)} %copy.98), calls=%async_computation.3 | async-start | bytes 1310720 | tf_op jit(solution)/shard_map/all_to_all | solution.py:71
  70.6 2.3 %fusion.13 = bf16[512,512]{0,1:T(8,128)(2,1)S(1)} fusion(f32[512,512]{0,1:T(8,128)} %convolution_bitcast_fusion.2, bf16[128,8,512]{0,2,1:T(8,128)(2,1)S(1)} %fusion.4, bf16[128,8,512]{0,2,1:T(8,128)(2,1)} %copy.86), kind=kOutput, calls=%fused_computation.25 | convolution fusion | flops 537657344 | bytes 3670016 | tf_op jit(solution)/shard_map/thk,thc->kc/dot_general | solution.py:39
  73.8 2.2 %copy.90 = bf16[512,576]{1,0:T(8,128)(2,1)} copy(bf16[512,576]{0,1:T(8,128)(2,1)} %pad_maximum_fusion) | data formatting | bytes 1179648 | tf_op jit(solution)/shard_map/concatenate | solution.py:45
  76.0 2.0 %copy.91 = bf16[4,8,16,576]{3,2,0,1:T(8,128)(2,1)} copy(bf16[4,8,16,576]{3,2,1,0:T(8,128)(2,1)} %bitcast.125) | data formatting | bytes 1179648 | tf_op jit(solution)/shard_map/convert_element_type | solution.py:70
  78.0 3.3 %all-to-all-done.3 = bf16[4,8,16,576]{3,2,0,1:T(8,128)(2,1)S(1)} async-done(((bf16[4,8,16,576]{3,2,0,1:T(8,128)(2,1)}), bf16[4,8,16,576]{3,2,0,1:T(8,128)(2,1)S(1)}, u32[]{:S(2)}, u32[]{:S(2)}) %all-to-all-start.3) | async-done | bytes 589856 | tf_op jit(solution)/shard_map/all_to_all | solution.py:71
  81.3 4.2 %all-to-all-start.2 = ((bf16[4,8,16,576]{3,2,0,1:T(8,128)(2,1)}), bf16[4,8,16,576]{3,2,0,1:T(8,128)(2,1)}, u32[]{:S(2)}, u32[]{:S(2)}) async-start(bf16[4,8,16,576]{3,2,0,1:T(8,128)(2,1)} %copy.91), calls=%async_computation.2 | async-start | bytes 1310720 | tf_op jit(solution)/shard_map/all_to_all | solution.py:71
  85.4 2.1 %fusion.23 = f32[128,8,512]{2,0,1:T(8,128)} fusion(bf16[128,8,512]{0,2,1:T(8,128)(2,1)S(1)} %fusion.4, bf16[512,576]{1,0:T(8,128)(2,1)S(1)} %bitcast.116), kind=kOutput, calls=%fused_computation.42 | convolution fusion | flops 536870912 | bytes 3670016 | tf_op jit(solution)/shard_map/thk,kc->thc/dot_general | solution.py:37
  87.5 1.9 %convert_reduce_fusion = f32[4,16,576]{2,1,0:T(8,128)} fusion(bf16[4,8,16,576]{3,2,0,1:T(8,128)(2,1)} %copy-done.5), kind=kLoop, calls=%fused_computation.23 | loop fusion | flops 552960 | bytes 737280 | tf_op jit(solution)/shard_map/reduce_sum | solution.py:72
  89.4 1.9 %collective-permute-start.3 = (f32[4,16,576]{2,1,0:T(8,128)}, f32[4,16,576]{2,1,0:T(8,128)}, u32[]{:S(2)}, u32[]{:S(2)}) collective-permute-start(f32[4,16,576]{2,1,0:T(8,128)} %convert_reduce_fusion), channel_id=1, source_target_pairs={{32,0},{40,8},{48,16},{56,24},{64,32},{72,40},{80,48},{88,56},{96,... | collective-permute-start | bytes 442376 | tf_op jit(solution)/shard_map/ppermute | solution.py:14
  94.3 3.5 %collective-permute-done.3 = f32[4,16,576]{2,1,0:T(8,128)} collective-permute-done((f32[4,16,576]{2,1,0:T(8,128)}, f32[4,16,576]{2,1,0:T(8,128)}, u32[]{:S(2)}, u32[]{:S(2)}) %collective-permute-start.3) | collective-permute-done | bytes 147488 | tf_op jit(solution)/shard_map/ppermute | solution.py:14
  98.8 2.1 %collective-permute-start.4 = (f32[2,16,576]{2,1,0:T(8,128)S(1)}, f32[2,16,576]{2,1,0:T(8,128)S(1)}, u32[]{:S(2)}, u32[]{:S(2)}) collective-permute-start(f32[2,16,576]{2,1,0:T(8,128)S(1)} %slice.47), channel_id=1, source_target_pairs={{16,0},{24,8},{32,16},{40,24},{48,32},{56,40},{64,48},{72,56},{80,... | collective-permute-start | bytes 221192 | tf_op jit(solution)/shard_map/ppermute | solution.py:14
  100.9 2.3 %multiply_convert_fusion = bf16[128,8,512]{2,0,1:T(8,128)(2,1)S(1)} fusion(f32[128,8,512]{2,0,1:T(8,128)} %fusion.23, bf16[128,8,512]{0,2,1:T(8,128)(2,1)S(1)} %fusion, bf16[512,576]{1,0:T(8,128)(2,1)S(1)} %bitcast.111), kind=kOutput, calls=%fused_computation.14 | convolution fusion | flops 538443776 | bytes 4718592 | tf_op jit(solution)/shard_map/thk,kc->thc/dot_general | solution.py:37
  103.2 2.1 %collective-permute-done.4 = f32[2,16,576]{2,1,0:T(8,128)S(1)} collective-permute-done((f32[2,16,576]{2,1,0:T(8,128)S(1)}, f32[2,16,576]{2,1,0:T(8,128)S(1)}, u32[]{:S(2)}, u32[]{:S(2)}) %collective-permute-start.4) | collective-permute-done | bytes 73760 | tf_op jit(solution)/shard_map/ppermute | solution.py:14
  105.3 1.9 %collective-permute-start.5 = (f32[1,16,576]{2,1,0:T(8,128)S(1)}, f32[1,16,576]{2,1,0:T(8,128)S(1)}, u32[]{:S(2)}, u32[]{:S(2)}) collective-permute-start(f32[1,16,576]{2,1,0:T(8,128)S(1)} %slice.49), channel_id=1, source_target_pairs={{8,0},{16,8},{24,16},{32,24},{40,32},{48,40},{56,48},{64,56},{72,6... | collective-permute-start | bytes 110600 | tf_op jit(solution)/shard_map/ppermute | solution.py:14
  (75 shorter events, 27.1 us)
Async XLA Ops:
  0.6 31.4 %copy-start.13 = (s32[128]{0:T(128)S(1)}, s32[128]{0:T(128)}, u32[]{:S(2)}) copy-start(s32[128]{0:T(128)} %param.15) | copy-start | bytes 1540
  0.6 34.3 %copy-start.4 = (bf16[128,8,512]{2,1,0:T(8,128)(2,1)S(1)}, bf16[128,8,512]{2,1,0:T(8,128)(2,1)}, u32[]{:S(2)}) copy-start(bf16[128,8,512]{2,1,0:T(8,128)(2,1)} %param.11) | copy-start | bytes 3145732
  0.7 34.3 %copy-start.6 = (bf16[128,8,512]{2,1,0:T(8,128)(2,1)S(1)}, bf16[128,8,512]{2,1,0:T(8,128)(2,1)}, u32[]{:S(2)}) copy-start(bf16[128,8,512]{2,1,0:T(8,128)(2,1)} %param.10) | copy-start | bytes 3145732
  2.4 13.1 %collective-permute-start = (bf16[1,16,576]{2,1,0:T(8,128)(2,1)S(1)}, bf16[1,16,576]{2,1,0:T(8,128)(2,1)S(1)}, u32[]{:S(2)}, u32[]{:S(2)}) collective-permute-start(bf16[1,16,576]{2,1,0:T(8,128)(2,1)S(1)} %fusion.30), channel_id=1, source_target_pairs={{0,8},{8,16},{16,24},{24,32},{32,40},{40,48},{48,56},{56,64},{64,7... | collective-permute-start | bytes 55304 | tf_op jit(solution)/shard_map/ppermute | solution.py:14
  15.5 9.6 %collective-permute-start.1 = (bf16[2,16,576]{2,1,0:T(8,128)(2,1)S(1)}, bf16[2,16,576]{2,1,0:T(8,128)(2,1)S(1)}, u32[]{:S(2)}, u32[]{:S(2)}) collective-permute-start(bf16[2,16,576]{2,1,0:T(8,128)(2,1)S(1)} %pad_maximum_fusion.3), channel_id=1, source_target_pairs={{0,16},{8,24},{16,32},{24,40},{32,48},{40,56},{48,64},{56,72},{64,... | collective-permute-start | bytes 110600 | tf_op jit(solution)/shard_map/ppermute | solution.py:14
  26.1 18.0 %all-to-all-start = ((bf16[8,4,16,576]{3,2,1,0:T(8,128)(2,1)}), bf16[8,4,16,576]{3,2,1,0:T(8,128)(2,1)S(1)}, u32[]{:S(2)}, u32[]{:S(2)}) async-start(bf16[8,4,16,576]{3,2,1,0:T(8,128)(2,1)} %broadcast_in_dim.57), calls=%async_computation | async-start | bytes 1310720 | tf_op jit(solution)/shard_map/all_to_all | solution.py:84
  32.9 3.4 %copy-start.10 = (bf16[128,512]{1,0:T(8,128)(2,1)S(1)}, bf16[128,512]{1,0:T(8,128)(2,1)}, u32[]{:S(2)}) copy-start(bf16[128,512]{1,0:T(8,128)(2,1)} %param.9) | copy-start | bytes 393220
  32.9 11.2 %collective-permute-start.2 = (bf16[4,16,576]{2,1,0:T(8,128)(2,1)S(1)}, bf16[4,16,576]{2,1,0:T(8,128)(2,1)}, u32[]{:S(2)}, u32[]{:S(2)}) collective-permute-start(bf16[4,16,576]{2,1,0:T(8,128)(2,1)S(1)} %pad_maximum_fusion.2), channel_id=1, source_target_pairs={{0,32},{8,40},{16,48},{24,56},{32,64},{40,72},{48,80},{56,88},{64,... | collective-permute-start | bytes 221192 | tf_op jit(solution)/shard_map/ppermute | solution.py:14
  45.9 13.6 %all-to-all-start.1 = ((bf16[8,4,16,576]{3,2,1,0:T(8,128)(2,1)}), bf16[8,4,16,576]{3,2,1,0:T(8,128)(2,1)S(1)}, u32[]{:S(2)}, u32[]{:S(2)}) async-start(bf16[8,4,16,576]{3,2,1,0:T(8,128)(2,1)} %broadcast_in_dim.60), calls=%async_computation.1 | async-start | bytes 1310720 | tf_op jit(solution)/shard_map/all_to_all | solution.py:84
  51.6 1.5 %copy-start.12 = (pred[128,512]{0,1:T(8,128)(4,1)S(1)}, pred[128,512]{0,1:T(8,128)(4,1)}, u32[]{:S(2)}) copy-start(pred[128,512]{0,1:T(8,128)(4,1)} %get-tuple-element.17) | copy-start | bytes 196612
  51.6 1.5 %copy-start.14 = (f32[128,8]{0,1:T(8,128)S(1)}, f32[128,8]{0,1:T(8,128)}, u32[]{:S(2)}) copy-start(f32[128,8]{0,1:T(8,128)} %param.12) | copy-start | bytes 12292
  51.6 4.1 %copy-start.2 = (bf16[4,8,16,576]{3,2,1,0:T(8,128)(2,1)}, bf16[4,8,16,576]{3,2,1,0:T(8,128)(2,1)S(1)}, u32[]{:S(2)}) copy-start(bf16[4,8,16,576]{3,2,1,0:T(8,128)(2,1)S(1)} %copy.70) | copy-start | bytes 1769476
  56.5 3.5 %copy-start.11 = (pred[128,512]{0,1:T(8,128)(4,1)S(1)}, pred[128,512]{0,1:T(8,128)(4,1)}, u32[]{:S(2)}) copy-start(pred[128,512]{0,1:T(8,128)(4,1)} %get-tuple-element.16) | copy-start | bytes 196612
  59.5 1.5 %copy-start.8 = (bf16[128,8,512]{0,2,1:T(8,128)(2,1)S(1)}, bf16[128,8,512]{0,2,1:T(8,128)(2,1)}, u32[]{:S(2)}) copy-start(bf16[128,8,512]{0,2,1:T(8,128)(2,1)} %copy.86) | copy-start | bytes 3145732
  59.6 2.3 %copy-start = (bf16[4,8,16,576]{3,2,1,0:T(8,128)(2,1)}, bf16[4,8,16,576]{3,2,1,0:T(8,128)(2,1)S(1)}, u32[]{:S(2)}) copy-start(bf16[4,8,16,576]{3,2,1,0:T(8,128)(2,1)S(1)} %copy.76) | copy-start | bytes 1769476
  65.8 15.4 %all-to-all-start.3 = ((bf16[4,8,16,576]{3,2,0,1:T(8,128)(2,1)}), bf16[4,8,16,576]{3,2,0,1:T(8,128)(2,1)S(1)}, u32[]{:S(2)}, u32[]{:S(2)}) async-start(bf16[4,8,16,576]{3,2,0,1:T(8,128)(2,1)} %copy.98), calls=%async_computation.3 | async-start | bytes 1310720 | tf_op jit(solution)/shard_map/all_to_all | solution.py:71
  73.8 11.7 %copy-start.3 = (bf16[4,8,16,576]{3,2,1,0:T(8,128)(2,1)S(1)}, bf16[4,8,16,576]{3,2,1,0:T(8,128)(2,1)}, u32[]{:S(2)}) copy-start(bf16[4,8,16,576]{3,2,1,0:T(8,128)(2,1)} %copy-done.2) | copy-start | bytes 1769476
  81.3 4.2 %copy-start.5 = (bf16[4,8,16,576]{3,2,0,1:T(8,128)(2,1)}, bf16[4,8,16,576]{3,2,0,1:T(8,128)(2,1)S(1)}, u32[]{:S(2)}) copy-start(bf16[4,8,16,576]{3,2,0,1:T(8,128)(2,1)S(1)} %all-to-all-done.3) | copy-start | bytes 1769476
  81.3 11.9 %all-to-all-start.2 = ((bf16[4,8,16,576]{3,2,0,1:T(8,128)(2,1)}), bf16[4,8,16,576]{3,2,0,1:T(8,128)(2,1)}, u32[]{:S(2)}, u32[]{:S(2)}) async-start(bf16[4,8,16,576]{3,2,0,1:T(8,128)(2,1)} %copy.91), calls=%async_computation.2 | async-start | bytes 1310720 | tf_op jit(solution)/shard_map/all_to_all | solution.py:71
  87.5 13.4 %copy-start.1 = (bf16[4,8,16,576]{3,2,1,0:T(8,128)(2,1)S(1)}, bf16[4,8,16,576]{3,2,1,0:T(8,128)(2,1)}, u32[]{:S(2)}) copy-start(bf16[4,8,16,576]{3,2,1,0:T(8,128)(2,1)} %copy-done) | copy-start | bytes 1769476
  89.4 8.4 %collective-permute-start.3 = (f32[4,16,576]{2,1,0:T(8,128)}, f32[4,16,576]{2,1,0:T(8,128)}, u32[]{:S(2)}, u32[]{:S(2)}) collective-permute-start(f32[4,16,576]{2,1,0:T(8,128)} %convert_reduce_fusion), channel_id=1, source_target_pairs={{32,0},{40,8},{48,16},{56,24},{64,32},{72,40},{80,48},{88,56},{96,... | collective-permute-start | bytes 442376 | tf_op jit(solution)/shard_map/ppermute | solution.py:14
  98.8 8.4 %copy-start.9 = (f32[128,8,64]{0,2,1:T(8,128)S(1)}, f32[128,8,64]{0,2,1:T(8,128)}, u32[]{:S(2)}) copy-start(f32[128,8,64]{0,2,1:T(8,128)} %fusion.24) | copy-start | bytes 786436
  98.8 6.5 %collective-permute-start.4 = (f32[2,16,576]{2,1,0:T(8,128)S(1)}, f32[2,16,576]{2,1,0:T(8,128)S(1)}, u32[]{:S(2)}, u32[]{:S(2)}) collective-permute-start(f32[2,16,576]{2,1,0:T(8,128)S(1)} %slice.47), channel_id=1, source_target_pairs={{16,0},{24,8},{32,16},{40,24},{48,32},{56,40},{64,48},{72,56},{80,... | collective-permute-start | bytes 221192 | tf_op jit(solution)/shard_map/ppermute | solution.py:14
  105.3 4.6 %collective-permute-start.5 = (f32[1,16,576]{2,1,0:T(8,128)S(1)}, f32[1,16,576]{2,1,0:T(8,128)S(1)}, u32[]{:S(2)}, u32[]{:S(2)}) collective-permute-start(f32[1,16,576]{2,1,0:T(8,128)S(1)} %slice.49), channel_id=1, source_target_pairs={{8,0},{16,8},{24,16},{32,24},{40,32},{48,40},{56,48},{64,56},{72,6... | collective-permute-start | bytes 110600 | tf_op jit(solution)/shard_map/ppermute | solution.py:14
  (1 other events, 1.5 us)

commit v5 on v4

--- a/solution.py
+++ b/solution.py
@@ -14,12 +14,12 @@
     return lax.ppermute(x, axis, pairs)
 
 
-def window_terms(q_latent, q_rot, grad_out, row_delta, log_total, doc_start, query_pos, keys, key_first):
+def window_terms(q_latent, q_rot, grad_out, row_delta, log_total, doc_start, query_pos, keys, key_first, key_order):
     lat_width = q_latent.shape[2]
     softmax_scale = (NOPE + ROPE) ** (-0.5)
     lat_all = keys[:, :lat_width]
     rot_all = keys[:, lat_width:]
-    key_pos = key_first + jnp.arange(keys.shape[0], dtype=jnp.int32)
+    key_pos = key_first + key_order
     visible = (
         (key_pos[None, :] >= doc_start[:, None]) & (key_pos[None, :] <= query_pos[:, None])
     )[:, None, :]
@@ -58,18 +58,24 @@
     own_tile = lax.axis_index("ctx")
     query_pos = own_tile * tok_rows + jnp.arange(tok_rows, dtype=jnp.int32)
 
+    key_order = (
+        jnp.arange(groups, dtype=jnp.int32)[:, None, None] * block
+        + jnp.arange(half_span, dtype=jnp.int32)[None, :, None] * tok_rows
+        + jnp.arange(block, dtype=jnp.int32)[None, None, :]
+    ).reshape(-1)
+
     def terms(keys, first_tile):
         flat = keys.reshape(-1, lat_width + rope_width)
         return window_terms(
             q_latent, q_rot, grad_out, row_delta, log_total, doc_start, query_pos,
-            flat, first_tile * tok_rows,
+            flat, first_tile * tok_rows, key_order,
         )
 
     def group_sum(part):
-        part = part.reshape(-1, groups, block, lat_width + rope_width)
+        part = part.reshape(groups, half_span, block, lat_width + rope_width)
         part = part.astype(jnp.bfloat16)
-        got = lax.all_to_all(part, "head", 1, 1, tiled=True)
-        return got.astype(jnp.float32).sum(axis=1)
+        got = lax.all_to_all(part, "head", 0, 0, tiled=True)
+        return got.astype(jnp.float32).sum(axis=0)
 
     keys = jnp.concatenate([latent, key_rope], axis=1)
     rows = lax.dynamic_slice_in_dim(keys, lax.axis_index("head") * block, block, axis=0)[None]
@@ -81,8 +87,7 @@
 
     def assemble(part):
         spread = jnp.broadcast_to(part[None], (groups,) + part.shape)
-        got = lax.all_to_all(spread, "head", 0, 0, tiled=True)
-        return got.transpose(1, 0, 2, 3)
+        return lax.all_to_all(spread, "head", 0, 0, tiled=True)
 
     near = assemble(rows)
     far = assemble(far_rows)

time: 113 us -> 114 us (level)
  starting transfers between devices: 31.9 us -> 35.5 us
  waiting for transfers between devices: 36.4 us -> 33.7 us
  matrix products: 16.3 us -> 18.6 us
  local copies, waits for them, and re-layouts: 18.5 us -> 16.6 us
    ppermute x6, waiting for transfers between devices: 29.4 us -> 25.5 us  [shifted(): return lax.ppermute(x, axis, pairs)]
    ppermute x6, starting transfers between devices: 11.8 us -> 15 us  [shifted(): return lax.ppermute(x, axis, pairs)]
    convert_element_type x2 -> x0, local copies, waits for them, and re-layouts: 2.91 us -> none  [group_sum(): part = part.astype(jnp.bfloat16)]
    dot_general x2, matrix products: 1.88 us -> 3.13 us  [window_terms(): jnp.einsum('thc,kc->thk', q_latent, lat_all, preferred_element_type=jnp.f...]
  transfers between devices with their start and end apart: 10 -> 10, of which waited for: 8 -> 7; matrix products, arithmetic and copies ran while one was open for 25% -> 25% of each run, Pallas kernels for 0% -> 0%
where the time goes in v5:
time: 114 us; the launch traced here: 112 us
  starting transfers between devices  35.5 us (31%)
  waiting for transfers between devices  33.7 us (30%)
  matrix products  18.6 us (16%)
  local copies, waits for them, and re-layouts  16.6 us (15%)
  other arithmetic  7.11 us (6%)
    ppermute x6, waiting for transfers between devices, shifted(): return lax.ppermute(x, axis, pairs)  25.5 us
    ppermute x6, starting transfers between devices, shifted(): return lax.ppermute(x, axis, pairs)  15 us
    all_to_all x2, starting transfers between devices, assemble(): return lax.all_to_all(spread, 'head', 0, 0, tiled=True)  11.6 us
    unnamed x36, local copies, waits for them, and re-layouts  9.12 us
    all_to_all x2, starting transfers between devices, group_sum(): got = lax.all_to_all(part, 'head', 0, 0, tiled=True)  8.78 us
    all_to_all x2, waiting for transfers between devices, group_sum(): got = lax.all_to_all(part, 'head', 0, 0, tiled=True)  5.34 us
    dot_general x2, matrix products, window_terms(): jnp.einsum('thk,kc->thc', grad_b, lat_all, preferred_element_type=jnp.flo...  4.39 us
    concatenate x2, local copies, waits for them, and re-layouts, window_terms(): return (grad_qlat, grad_qrot, jnp.concatenate([grad_lat, grad_rot], axis=1))  3.23 us
  transfers between devices with their start and end apart: 10, of which 7 were waited for; matrix products, arithmetic and copies ran while one was open for 25% of the time, Pallas kernels for 0%

profile of v5, /device:TPU:6, one launch (start us, length us, event | category | flops | bytes accessed | tf_op | source)
XLA Modules:
  0.0 112.4 jit_solution(2706087818843356459)
XLA Ops:
  2.4 1.9 %collective-permute-start = (bf16[1,16,576]{2,1,0:T(8,128)(2,1)S(1)}, bf16[1,16,576]{2,1,0:T(8,128)(2,1)S(1)}, u32[]{:S(2)}, u32[]{:S(2)}) collective-permute-start(bf16[1,16,576]{2,1,0:T(8,128)(2,1)S(1)} %fusion.30), channel_id=1, source_target_pairs={{0,8},{8,16},{16,24},{24,32},{32,40},{40,48},{48,56},{56,64},{64,7... | collective-permute-start | bytes 55304 | tf_op jit(solution)/shard_map/ppermute | solution.py:14
  4.4 11.1 %collective-permute-done = bf16[1,16,576]{2,1,0:T(8,128)(2,1)S(1)} collective-permute-done((bf16[1,16,576]{2,1,0:T(8,128)(2,1)S(1)}, bf16[1,16,576]{2,1,0:T(8,128)(2,1)S(1)}, u32[]{:S(2)}, u32[]{:S(2)}) %collective-permute-start) | collective-permute-done | bytes 18464 | tf_op jit(solution)/shard_map/ppermute | solution.py:14
  15.5 1.9 %collective-permute-start.1 = (bf16[2,16,576]{2,1,0:T(8,128)(2,1)S(1)}, bf16[2,16,576]{2,1,0:T(8,128)(2,1)S(1)}, u32[]{:S(2)}, u32[]{:S(2)}) collective-permute-start(bf16[2,16,576]{2,1,0:T(8,128)(2,1)S(1)} %pad_maximum_fusion.3), channel_id=1, source_target_pairs={{0,16},{8,24},{16,32},{24,40},{32,48},{40,56},{48,64},{56,72},{64,... | collective-permute-start | bytes 110600 | tf_op jit(solution)/shard_map/ppermute | solution.py:14
  17.7 7.4 %collective-permute-done.1 = bf16[2,16,576]{2,1,0:T(8,128)(2,1)S(1)} collective-permute-done((bf16[2,16,576]{2,1,0:T(8,128)(2,1)S(1)}, bf16[2,16,576]{2,1,0:T(8,128)(2,1)S(1)}, u32[]{:S(2)}, u32[]{:S(2)}) %collective-permute-start.1) | collective-permute-done | bytes 36896 | tf_op jit(solution)/shard_map/ppermute | solution.py:14
  26.1 5.9 %all-to-all-start = ((bf16[8,4,16,576]{3,2,1,0:T(8,128)(2,1)}), bf16[8,4,16,576]{3,2,1,0:T(8,128)(2,1)S(1)}, u32[]{:S(2)}, u32[]{:S(2)}) async-start(bf16[8,4,16,576]{3,2,1,0:T(8,128)(2,1)} %broadcast_in_dim.60), calls=%async_computation | async-start | bytes 1310720 | tf_op jit(solution)/shard_map/all_to_all | solution.py:90
  32.9 2.0 %collective-permute-start.2 = (bf16[4,16,576]{2,1,0:T(8,128)(2,1)S(1)}, bf16[4,16,576]{2,1,0:T(8,128)(2,1)}, u32[]{:S(2)}, u32[]{:S(2)}) collective-permute-start(bf16[4,16,576]{2,1,0:T(8,128)(2,1)S(1)} %pad_maximum_fusion.2), channel_id=1, source_target_pairs={{0,32},{8,40},{16,48},{24,56},{32,64},{40,72},{48,80},{56,88},{64,... | collective-permute-start | bytes 221192 | tf_op jit(solution)/shard_map/ppermute | solution.py:14
  35.3 1.9 %copy.58 = bf16[128,8,512]{0,2,1:T(8,128)(2,1)S(1)} copy(bf16[128,8,512]{2,1,0:T(8,128)(2,1)} %param.11) | data formatting | bytes 2097152 | tf_op args[3]
  37.4 2.7 %copy.56 = bf16[128,8,512]{0,2,1:T(8,128)(2,1)} copy(bf16[128,8,512]{2,1,0:T(8,128)(2,1)} %param.8) | data formatting | bytes 2097152 | tf_op args[0]
  40.1 4.0 %collective-permute-done.2 = bf16[4,16,576]{2,1,0:T(8,128)(2,1)} collective-permute-done((bf16[4,16,576]{2,1,0:T(8,128)(2,1)S(1)}, bf16[4,16,576]{2,1,0:T(8,128)(2,1)}, u32[]{:S(2)}, u32[]{:S(2)}) %collective-permute-start.2) | collective-permute-done | bytes 73760 | tf_op jit(solution)/shard_map/ppermute | solution.py:14
  44.1 1.9 %broadcast_in_dim.63 = bf16[8,4,16,576]{3,2,1,0:T(8,128)(2,1)} broadcast(bf16[4,16,576]{2,1,0:T(8,128)(2,1)} %collective-permute-done.2), dimensions={1,2,3} | broadcast | bytes 663552 | tf_op jit(solution)/shard_map/broadcast_in_dim | solution.py:89
  45.9 5.7 %all-to-all-start.1 = ((bf16[8,4,16,576]{3,2,1,0:T(8,128)(2,1)}), bf16[8,4,16,576]{3,2,1,0:T(8,128)(2,1)S(1)}, u32[]{:S(2)}, u32[]{:S(2)}) async-start(bf16[8,4,16,576]{3,2,1,0:T(8,128)(2,1)} %broadcast_in_dim.63), calls=%async_computation.1 | async-start | bytes 1310720 | tf_op jit(solution)/shard_map/all_to_all | solution.py:90
  52.1 2.2 %fusion.8 = f32[128,8,512]{0,2,1:T(8,128)S(1)} fusion(f32[512,128,8]{1,0,2:T(8,128)S(1)} %fusion.25, bf16[128,8,512]{0,2,1:T(8,128)(2,1)} %copy.56, f32[128,8]{0,1:T(8,128)S(1)} %copy-done.14, pred[128,512]{0,1:T(8,128)(4,1)S(1)} %copy-done.12, bf16[512,576]{1,0:T(8,128)(2,1)S(1)} %bitcast.112), kind=kOutput, calls=%fused_computation.13 | convolution fusion | flops 539492352 | bytes 5836800 | tf_op jit(solution)/shard_map/thc,kc->thk/dot_general | solution.py:27
  56.8 2.8 %all-to-all-done.1 = bf16[8,4,16,576]{3,2,1,0:T(8,128)(2,1)S(1)} async-done(((bf16[8,4,16,576]{3,2,1,0:T(8,128)(2,1)}), bf16[8,4,16,576]{3,2,1,0:T(8,128)(2,1)S(1)}, u32[]{:S(2)}, u32[]{:S(2)}) %all-to-all-start.1) | async-done | bytes 589856 | tf_op jit(solution)/shard_map/all_to_all | solution.py:90
  66.9 4.3 %all-to-all-start.3 = ((bf16[8,4,16,576]{3,2,1,0:T(8,128)(2,1)}), bf16[8,4,16,576]{3,2,1,0:T(8,128)(2,1)S(1)}, u32[]{:S(2)}, u32[]{:S(2)}) async-start(bf16[8,4,16,576]{3,2,1,0:T(8,128)(2,1)} %bitcast.22), calls=%async_computation.3 | async-start | bytes 1310720 | tf_op jit(solution)/shard_map/all_to_all | solution.py:77
  71.6 2.3 %fusion.13 = bf16[512,512]{0,1:T(8,128)(2,1)S(1)} fusion(f32[512,512]{0,1:T(8,128)} %convolution_bitcast_fusion.2, bf16[128,8,512]{0,2,1:T(8,128)(2,1)S(1)} %fusion.4, bf16[128,8,512]{0,2,1:T(8,128)(2,1)} %copy.56), kind=kOutput, calls=%fused_computation.25 | convolution fusion | flops 537657344 | bytes 3670016 | tf_op jit(solution)/shard_map/thk,thc->kc/dot_general | solution.py:39
  74.8 2.1 %copy.60 = bf16[512,576]{1,0:T(8,128)(2,1)} copy(bf16[512,576]{0,1:T(8,128)(2,1)} %pad_maximum_fusion) | data formatting | bytes 1179648 | tf_op jit(solution)/shard_map/concatenate | solution.py:45
  76.9 5.3 %all-to-all-done.3 = bf16[8,4,16,576]{3,2,1,0:T(8,128)(2,1)S(1)} async-done(((bf16[8,4,16,576]{3,2,1,0:T(8,128)(2,1)}), bf16[8,4,16,576]{3,2,1,0:T(8,128)(2,1)S(1)}, u32[]{:S(2)}, u32[]{:S(2)}) %all-to-all-start.3) | async-done | bytes 589856 | tf_op jit(solution)/shard_map/all_to_all | solution.py:77
  82.3 4.4 %all-to-all-start.2 = ((bf16[8,4,16,576]{3,2,1,0:T(8,128)(2,1)}), bf16[8,4,16,576]{3,2,1,0:T(8,128)(2,1)}, u32[]{:S(2)}, u32[]{:S(2)}) async-start(bf16[8,4,16,576]{3,2,1,0:T(8,128)(2,1)} %bitcast.120), calls=%async_computation.2 | async-start | bytes 1310720 | tf_op jit(solution)/shard_map/all_to_all | solution.py:77
  86.7 2.1 %fusion.23 = f32[128,8,512]{2,0,1:T(8,128)} fusion(bf16[128,8,512]{0,2,1:T(8,128)(2,1)S(1)} %fusion.4, bf16[512,576]{1,0:T(8,128)(2,1)S(1)} %bitcast.114), kind=kOutput, calls=%fused_computation.42 | convolution fusion | flops 536870912 | bytes 3670016 | tf_op jit(solution)/shard_map/thk,kc->thc/dot_general | solution.py:37
  88.8 1.9 %convert_reduce_fusion = f32[4,16,576]{2,1,0:T(8,128)} fusion(bf16[8,4,16,576]{3,2,1,0:T(8,128)(2,1)} %copy-done.6), kind=kLoop, calls=%fused_computation.23 | loop fusion | flops 552960 | bytes 737280 | tf_op jit(solution)/shard_map/reduce_sum | solution.py:78
  90.7 4.3 %collective-permute-start.3 = (f32[4,16,576]{2,1,0:T(8,128)}, f32[4,16,576]{2,1,0:T(8,128)}, u32[]{:S(2)}, u32[]{:S(2)}) collective-permute-start(f32[4,16,576]{2,1,0:T(8,128)} %convert_reduce_fusion), channel_id=1, source_target_pairs={{32,0},{40,8},{48,16},{56,24},{64,32},{72,40},{80,48},{88,56},{96,... | collective-permute-start | bytes 442376 | tf_op jit(solution)/shard_map/ppermute | solution.py:14
  100.1 2.9 %collective-permute-start.4 = (f32[2,16,576]{2,1,0:T(8,128)S(1)}, f32[2,16,576]{2,1,0:T(8,128)S(1)}, u32[]{:S(2)}, u32[]{:S(2)}) collective-permute-start(f32[2,16,576]{2,1,0:T(8,128)S(1)} %slice.47), channel_id=1, source_target_pairs={{16,0},{24,8},{32,16},{40,24},{48,32},{56,40},{64,48},{72,56},{80,... | collective-permute-start | bytes 221192 | tf_op jit(solution)/shard_map/ppermute | solution.py:14
  103.0 2.3 %multiply_convert_fusion = bf16[128,8,512]{2,0,1:T(8,128)(2,1)S(1)} fusion(f32[128,8,512]{2,0,1:T(8,128)} %fusion.23, bf16[128,8,512]{0,2,1:T(8,128)(2,1)S(1)} %fusion, bf16[512,576]{1,0:T(8,128)(2,1)S(1)} %bitcast.109), kind=kOutput, calls=%fused_computation.14 | convolution fusion | flops 538443776 | bytes 4718592 | tf_op jit(solution)/shard_map/thk,kc->thc/dot_general | solution.py:37
  106.6 1.9 %collective-permute-start.5 = (f32[1,16,576]{2,1,0:T(8,128)S(1)}, f32[1,16,576]{2,1,0:T(8,128)S(1)}, u32[]{:S(2)}, u32[]{:S(2)}) collective-permute-start(f32[1,16,576]{2,1,0:T(8,128)S(1)} %slice.49), channel_id=1, source_target_pairs={{8,0},{16,8},{24,16},{32,24},{40,32},{48,40},{56,48},{64,56},{72,6... | collective-permute-start | bytes 110600 | tf_op jit(solution)/shard_map/ppermute | solution.py:14
  (76 shorter events, 25.9 us)
Async XLA Ops:
  0.6 31.4 %copy-start.13 = (s32[128]{0:T(128)S(1)}, s32[128]{0:T(128)}, u32[]{:S(2)}) copy-start(s32[128]{0:T(128)} %param.15) | copy-start | bytes 1540
  0.6 34.3 %copy-start.5 = (bf16[128,8,512]{2,1,0:T(8,128)(2,1)S(1)}, bf16[128,8,512]{2,1,0:T(8,128)(2,1)}, u32[]{:S(2)}) copy-start(bf16[128,8,512]{2,1,0:T(8,128)(2,1)} %param.11) | copy-start | bytes 3145732
  0.7 34.3 %copy-start.7 = (bf16[128,8,512]{2,1,0:T(8,128)(2,1)S(1)}, bf16[128,8,512]{2,1,0:T(8,128)(2,1)}, u32[]{:S(2)}) copy-start(bf16[128,8,512]{2,1,0:T(8,128)(2,1)} %param.10) | copy-start | bytes 3145732
  2.4 13.1 %collective-permute-start = (bf16[1,16,576]{2,1,0:T(8,128)(2,1)S(1)}, bf16[1,16,576]{2,1,0:T(8,128)(2,1)S(1)}, u32[]{:S(2)}, u32[]{:S(2)}) collective-permute-start(bf16[1,16,576]{2,1,0:T(8,128)(2,1)S(1)} %fusion.30), channel_id=1, source_target_pairs={{0,8},{8,16},{16,24},{24,32},{32,40},{40,48},{48,56},{56,64},{64,7... | collective-permute-start | bytes 55304 | tf_op jit(solution)/shard_map/ppermute | solution.py:14
  15.5 9.6 %collective-permute-start.1 = (bf16[2,16,576]{2,1,0:T(8,128)(2,1)S(1)}, bf16[2,16,576]{2,1,0:T(8,128)(2,1)S(1)}, u32[]{:S(2)}, u32[]{:S(2)}) collective-permute-start(bf16[2,16,576]{2,1,0:T(8,128)(2,1)S(1)} %pad_maximum_fusion.3), channel_id=1, source_target_pairs={{0,16},{8,24},{16,32},{24,40},{32,48},{40,56},{48,64},{56,72},{64,... | collective-permute-start | bytes 110600 | tf_op jit(solution)/shard_map/ppermute | solution.py:14
  26.1 18.0 %all-to-all-start = ((bf16[8,4,16,576]{3,2,1,0:T(8,128)(2,1)}), bf16[8,4,16,576]{3,2,1,0:T(8,128)(2,1)S(1)}, u32[]{:S(2)}, u32[]{:S(2)}) async-start(bf16[8,4,16,576]{3,2,1,0:T(8,128)(2,1)} %broadcast_in_dim.60), calls=%async_computation | async-start | bytes 1310720 | tf_op jit(solution)/shard_map/all_to_all | solution.py:90
  32.9 4.4 %copy-start.10 = (bf16[128,512]{1,0:T(8,128)(2,1)S(1)}, bf16[128,512]{1,0:T(8,128)(2,1)}, u32[]{:S(2)}) copy-start(bf16[128,512]{1,0:T(8,128)(2,1)} %param.9) | copy-start | bytes 393220
  32.9 11.2 %collective-permute-start.2 = (bf16[4,16,576]{2,1,0:T(8,128)(2,1)S(1)}, bf16[4,16,576]{2,1,0:T(8,128)(2,1)}, u32[]{:S(2)}, u32[]{:S(2)}) collective-permute-start(bf16[4,16,576]{2,1,0:T(8,128)(2,1)S(1)} %pad_maximum_fusion.2), channel_id=1, source_target_pairs={{0,32},{8,40},{16,48},{24,56},{32,64},{40,72},{48,80},{56,88},{64,... | collective-permute-start | bytes 221192 | tf_op jit(solution)/shard_map/ppermute | solution.py:14
  40.1 12.0 %copy-start.12 = (pred[128,512]{0,1:T(8,128)(4,1)S(1)}, pred[128,512]{0,1:T(8,128)(4,1)}, u32[]{:S(2)}) copy-start(pred[128,512]{0,1:T(8,128)(4,1)} %get-tuple-element.15) | copy-start | bytes 196612
  40.1 12.0 %copy-start.14 = (f32[128,8]{0,1:T(8,128)S(1)}, f32[128,8]{0,1:T(8,128)}, u32[]{:S(2)}) copy-start(f32[128,8]{0,1:T(8,128)} %param.12) | copy-start | bytes 12292
  44.1 8.0 %copy-start.2 = (bf16[8,4,16,576]{3,2,1,0:T(8,128)(2,1)}, bf16[8,4,16,576]{3,2,1,0:T(8,128)(2,1)S(1)}, u32[]{:S(2)}) copy-start(bf16[8,4,16,576]{3,2,1,0:T(8,128)(2,1)S(1)} %all-to-all-done) | copy-start | bytes 1769476
  45.9 13.6 %all-to-all-start.1 = ((bf16[8,4,16,576]{3,2,1,0:T(8,128)(2,1)}), bf16[8,4,16,576]{3,2,1,0:T(8,128)(2,1)S(1)}, u32[]{:S(2)}, u32[]{:S(2)}) async-start(bf16[8,4,16,576]{3,2,1,0:T(8,128)(2,1)} %broadcast_in_dim.63), calls=%async_computation.1 | async-start | bytes 1310720 | tf_op jit(solution)/shard_map/all_to_all | solution.py:90
  54.3 1.8 %copy-start.3 = (bf16[8,4,16,576]{3,2,1,0:T(8,128)(2,1)S(1)}, bf16[8,4,16,576]{3,2,1,0:T(8,128)(2,1)}, u32[]{:S(2)}) copy-start(bf16[8,4,16,576]{3,2,1,0:T(8,128)(2,1)} %copy-done.2) | copy-start | bytes 1769476
  56.8 3.7 %copy-start.11 = (pred[128,512]{0,1:T(8,128)(4,1)S(1)}, pred[128,512]{0,1:T(8,128)(4,1)}, u32[]{:S(2)}) copy-start(pred[128,512]{0,1:T(8,128)(4,1)} %get-tuple-element.14) | copy-start | bytes 196612
  59.6 1.5 %copy-start.8 = (bf16[128,8,512]{0,2,1:T(8,128)(2,1)S(1)}, bf16[128,8,512]{0,2,1:T(8,128)(2,1)}, u32[]{:S(2)}) copy-start(bf16[128,8,512]{0,2,1:T(8,128)(2,1)} %copy.56) | copy-start | bytes 3145732
  66.9 15.4 %all-to-all-start.3 = ((bf16[8,4,16,576]{3,2,1,0:T(8,128)(2,1)}), bf16[8,4,16,576]{3,2,1,0:T(8,128)(2,1)S(1)}, u32[]{:S(2)}, u32[]{:S(2)}) async-start(bf16[8,4,16,576]{3,2,1,0:T(8,128)(2,1)} %bitcast.22), calls=%async_computation.3 | async-start | bytes 1310720 | tf_op jit(solution)/shard_map/all_to_all | solution.py:77
  73.9 12.8 %copy-start.4 = (bf16[8,4,16,576]{3,2,1,0:T(8,128)(2,1)S(1)}, bf16[8,4,16,576]{3,2,1,0:T(8,128)(2,1)}, u32[]{:S(2)}) copy-start(bf16[8,4,16,576]{3,2,1,0:T(8,128)(2,1)} %copy-done.2) | copy-start | bytes 1769476
  82.3 4.5 %copy-start.6 = (bf16[8,4,16,576]{3,2,1,0:T(8,128)(2,1)}, bf16[8,4,16,576]{3,2,1,0:T(8,128)(2,1)S(1)}, u32[]{:S(2)}) copy-start(bf16[8,4,16,576]{3,2,1,0:T(8,128)(2,1)S(1)} %all-to-all-done.3) | copy-start | bytes 1769476
  82.3 13.8 %all-to-all-start.2 = ((bf16[8,4,16,576]{3,2,1,0:T(8,128)(2,1)}), bf16[8,4,16,576]{3,2,1,0:T(8,128)(2,1)}, u32[]{:S(2)}, u32[]{:S(2)}) async-start(bf16[8,4,16,576]{3,2,1,0:T(8,128)(2,1)} %bitcast.120), calls=%async_computation.2 | async-start | bytes 1310720 | tf_op jit(solution)/shard_map/all_to_all | solution.py:77
  88.8 14.2 %copy-start.1 = (bf16[8,4,16,576]{3,2,1,0:T(8,128)(2,1)S(1)}, bf16[8,4,16,576]{3,2,1,0:T(8,128)(2,1)}, u32[]{:S(2)}) copy-start(bf16[8,4,16,576]{3,2,1,0:T(8,128)(2,1)} %copy-done) | copy-start | bytes 1769476
  90.7 8.4 %collective-permute-start.3 = (f32[4,16,576]{2,1,0:T(8,128)}, f32[4,16,576]{2,1,0:T(8,128)}, u32[]{:S(2)}, u32[]{:S(2)}) collective-permute-start(f32[4,16,576]{2,1,0:T(8,128)} %convert_reduce_fusion), channel_id=1, source_target_pairs={{32,0},{40,8},{48,16},{56,24},{64,32},{72,40},{80,48},{88,56},{96,... | collective-permute-start | bytes 442376 | tf_op jit(solution)/shard_map/ppermute | solution.py:14
  100.1 8.4 %copy-start.9 = (f32[128,8,64]{0,2,1:T(8,128)S(1)}, f32[128,8,64]{0,2,1:T(8,128)}, u32[]{:S(2)}) copy-start(f32[128,8,64]{0,2,1:T(8,128)} %fusion.24) | copy-start | bytes 786436
  100.1 6.5 %collective-permute-start.4 = (f32[2,16,576]{2,1,0:T(8,128)S(1)}, f32[2,16,576]{2,1,0:T(8,128)S(1)}, u32[]{:S(2)}, u32[]{:S(2)}) collective-permute-start(f32[2,16,576]{2,1,0:T(8,128)S(1)} %slice.47), channel_id=1, source_target_pairs={{16,0},{24,8},{32,16},{40,24},{48,32},{56,40},{64,48},{72,56},{80,... | collective-permute-start | bytes 221192 | tf_op jit(solution)/shard_map/ppermute | solution.py:14
  106.6 4.6 %collective-permute-start.5 = (f32[1,16,576]{2,1,0:T(8,128)S(1)}, f32[1,16,576]{2,1,0:T(8,128)S(1)}, u32[]{:S(2)}, u32[]{:S(2)}) collective-permute-start(f32[1,16,576]{2,1,0:T(8,128)S(1)} %slice.49), channel_id=1, source_target_pairs={{8,0},{16,8},{24,16},{32,24},{40,32},{48,40},{56,48},{64,56},{72,6... | collective-permute-start | bytes 110600 | tf_op jit(solution)/shard_map/ppermute | solution.py:14
  (1 other events, 0.9 us)

commit v6 on v5

--- a/solution.py
+++ b/solution.py
@@ -77,19 +77,19 @@
         got = lax.all_to_all(part, "head", 0, 0, tiled=True)
         return got.astype(jnp.float32).sum(axis=0)
 
-    keys = jnp.concatenate([latent, key_rope], axis=1)
-    rows = lax.dynamic_slice_in_dim(keys, lax.axis_index("head") * block, block, axis=0)[None]
+    near_full = jnp.concatenate([latent, key_rope], axis=1)[None]
     width = 1
     while width < half_span:
-        rows = jnp.concatenate([shifted(rows, "ctx", width), rows], axis=0)
+        near_full = jnp.concatenate([shifted(near_full, "ctx", width), near_full], axis=0)
         width *= 2
+    rows = lax.dynamic_slice_in_dim(near_full, lax.axis_index("head") * block, block, axis=1)
     far_rows = shifted(rows, "ctx", half_span)
 
     def assemble(part):
         spread = jnp.broadcast_to(part[None], (groups,) + part.shape)
         return lax.all_to_all(spread, "head", 0, 0, tiled=True)
 
-    near = assemble(rows)
+    near = near_full.reshape(half_span, groups, block, -1).transpose(1, 0, 2, 3)
     far = assemble(far_rows)
 
     near_qlat, near_qrot, near_part = terms(near, own_tile - half_span + 1)

time: 114 us -> 112 us (0.982)
  starting transfers between devices: 35.5 us -> 30.7 us
  waiting for transfers between devices: 33.7 us -> 37.5 us
  local copies, waits for them, and re-layouts: 16.6 us -> 13.6 us
  matrix products: 18.6 us -> 21 us
    all_to_all x2 -> x1, starting transfers between devices: 11.6 us -> 5.93 us  [assemble(): return lax.all_to_all(spread, 'head', 0, 0, tiled=True)]
    ppermute x6, waiting for transfers between devices: 25.5 us -> 29 us  [shifted(): return lax.ppermute(x, axis, pairs)]
    broadcast_in_dim x2 -> x1, local copies, waits for them, and re-layouts: 2.79 us -> 0.9 us  [assemble(): spread = jnp.broadcast_to(part[None], (groups,) + part.shape)]
    dot_general x2, matrix products: 2.5 us -> 4.11 us  [window_terms(): jnp.einsum('thc,kc->thk', grad_out, lat_all, preferred_element_type=jnp.f...]
    all_to_all x2, starting transfers between devices: 8.78 us -> 10.1 us  [group_sum(): got = lax.all_to_all(part, 'head', 0, 0, tiled=True)]
    unnamed x1, other arithmetic: 0.34 us -> 1.57 us
    all_to_all x2 -> x1, waiting for transfers between devices: 2.8 us -> 3.97 us  [assemble(): return lax.all_to_all(spread, 'head', 0, 0, tiled=True)]
    unnamed x36 -> x30, local copies, waits for them, and re-layouts: 9.12 us -> 8.09 us
  transfers between devices with their start and end apart: 10 -> 9, of which waited for: 7 -> 7; matrix products, arithmetic and copies ran while one was open for 25% -> 26% of each run, Pallas kernels for 0% -> 0%
where the time goes in v6:
time: 112 us; the launch traced here: 110 us
  waiting for transfers between devices  37.5 us (33%)
  starting transfers between devices  30.7 us (27%)
  matrix products  21 us (19%)
  local copies, waits for them, and re-layouts  13.6 us (12%)
  other arithmetic  6.36 us (6%)
    ppermute x6, waiting for transfers between devices, shifted(): return lax.ppermute(x, axis, pairs)  29 us
    ppermute x6, starting transfers between devices, shifted(): return lax.ppermute(x, axis, pairs)  14.7 us
    all_to_all x2, starting transfers between devices, group_sum(): got = lax.all_to_all(part, 'head', 0, 0, tiled=True)  10.1 us
    unnamed x30, local copies, waits for them, and re-layouts  8.09 us
    all_to_all x1, starting transfers between devices, assemble(): return lax.all_to_all(spread, 'head', 0, 0, tiled=True)  5.93 us
    dot_general x2, matrix products, window_terms(): jnp.einsum('thk,kc->thc', grad_b, lat_all, preferred_element_type=jnp.flo...  4.58 us
    all_to_all x2, waiting for transfers between devices, group_sum(): got = lax.all_to_all(part, 'head', 0, 0, tiled=True)  4.51 us
    dot_general x2, matrix products, window_terms(): jnp.einsum('thc,kc->thk', grad_out, lat_all, preferred_element_type=jnp.f...  4.11 us
  transfers between devices with their start and end apart: 9, of which 7 were waited for; matrix products, arithmetic and copies ran while one was open for 26% of the time, Pallas kernels for 0%

profile of v6, /device:TPU:6, one launch (start us, length us, event | category | flops | bytes accessed | tf_op | source)
XLA Modules:
  0.0 110.2 jit_solution(2658747525148511787)
XLA Ops:
  2.5 1.9 %collective-permute-start = (bf16[1,128,576]{2,1,0:T(8,128)(2,1)S(1)}, bf16[1,128,576]{2,1,0:T(8,128)(2,1)S(1)}, u32[]{:S(2)}, u32[]{:S(2)}) collective-permute-start(bf16[1,128,576]{2,1,0:T(8,128)(2,1)S(1)} %get-tuple-element.12), channel_id=1, source_target_pairs={{0,8},{8,16},{16,24},{24,32},{32,40},{40,48},{48,56},{56,64},{64,7... | collective-permute-start | bytes 442376 | tf_op jit(solution)/shard_map/ppermute | solution.py:14
  4.8 2.0 %copy.64 = bf16[128,8,512]{0,2,1:T(8,128)(2,1)S(1)} copy(bf16[128,8,512]{2,1,0:T(8,128)(2,1)} %param.11) | data formatting | bytes 2097152 | tf_op args[3]
  8.6 2.7 %copy.62 = bf16[128,8,512]{0,2,1:T(8,128)(2,1)} copy(bf16[128,8,512]{2,1,0:T(8,128)(2,1)} %param.8) | data formatting | bytes 2097152 | tf_op args[0]
  11.2 5.9 %collective-permute-done = bf16[1,128,576]{2,1,0:T(8,128)(2,1)S(1)} collective-permute-done((bf16[1,128,576]{2,1,0:T(8,128)(2,1)S(1)}, bf16[1,128,576]{2,1,0:T(8,128)(2,1)S(1)}, u32[]{:S(2)}, u32[]{:S(2)}) %collective-permute-start) | collective-permute-done | bytes 147488 | tf_op jit(solution)/shard_map/ppermute | solution.py:14
  17.2 1.9 %collective-permute-start.1 = (bf16[2,128,576]{2,1,0:T(8,128)(2,1)S(1)}, bf16[2,128,576]{2,1,0:T(8,128)(2,1)S(1)}, u32[]{:S(2)}, u32[]{:S(2)}) collective-permute-start(bf16[2,128,576]{2,1,0:T(8,128)(2,1)S(1)} %pad_maximum_fusion.3), channel_id=1, source_target_pairs={{0,16},{8,24},{16,32},{24,40},{32,48},{40,56},{48,64},{56,72},{64,... | collective-permute-start | bytes 884744 | tf_op jit(solution)/shard_map/ppermute | solution.py:14
  19.4 11.8 %collective-permute-done.1 = bf16[2,128,576]{2,1,0:T(8,128)(2,1)S(1)} collective-permute-done((bf16[2,128,576]{2,1,0:T(8,128)(2,1)S(1)}, bf16[2,128,576]{2,1,0:T(8,128)(2,1)S(1)}, u32[]{:S(2)}, u32[]{:S(2)}) %collective-permute-start.1) | collective-permute-done | bytes 294944 | tf_op jit(solution)/shard_map/ppermute | solution.py:14
  31.3 1.9 %collective-permute-start.2 = (bf16[4,16,576]{2,1,0:T(8,128)(2,1)S(1)}, bf16[4,16,576]{2,1,0:T(8,128)(2,1)S(1)}, u32[]{:S(2)}, u32[]{:S(2)}) collective-permute-start(bf16[4,16,576]{2,1,0:T(8,128)(2,1)S(1)} %fusion.28), channel_id=1, source_target_pairs={{0,32},{8,40},{16,48},{24,56},{32,64},{40,72},{48,80},{56,88},{64,... | collective-permute-start | bytes 221192 | tf_op jit(solution)/shard_map/ppermute | solution.py:14
  34.7 8.2 %collective-permute-done.2 = bf16[4,16,576]{2,1,0:T(8,128)(2,1)S(1)} collective-permute-done((bf16[4,16,576]{2,1,0:T(8,128)(2,1)S(1)}, bf16[4,16,576]{2,1,0:T(8,128)(2,1)S(1)}, u32[]{:S(2)}, u32[]{:S(2)}) %collective-permute-start.2) | collective-permute-done | bytes 73760 | tf_op jit(solution)/shard_map/ppermute | solution.py:14
  43.8 5.9 %all-to-all-start = ((bf16[8,4,16,576]{3,2,1,0:T(8,128)(2,1)}), bf16[8,4,16,576]{3,2,1,0:T(8,128)(2,1)}, u32[]{:S(2)}, u32[]{:S(2)}) async-start(bf16[8,4,16,576]{3,2,1,0:T(8,128)(2,1)} %broadcast_in_dim.56), calls=%async_computation | async-start | bytes 1310720 | tf_op jit(solution)/shard_map/all_to_all | solution.py:90
  51.4 2.3 %fusion.4 = bf16[128,8,512]{0,2,1:T(8,128)(2,1)S(1)} fusion(f32[128,8,512]{0,2,1:T(8,128)} %copy-done, bf16[128,8,512]{0,2,1:T(8,128)(2,1)S(1)} %copy.64, f32[128,8]{0,1:T(8,128)S(1)} %copy.80, bf16[512,576]{1,0:T(8,128)(2,1)S(1)} %bitcast.117), kind=kOutput, calls=%fused_computation.7 | convolution fusion | flops 538443776 | bytes 4722688 | tf_op jit(solution)/shard_map/thc,kc->thk/dot_general | solution.py:33
  53.8 4.0 %all-to-all-done = bf16[8,4,16,576]{3,2,1,0:T(8,128)(2,1)} async-done(((bf16[8,4,16,576]{3,2,1,0:T(8,128)(2,1)}), bf16[8,4,16,576]{3,2,1,0:T(8,128)(2,1)}, u32[]{:S(2)}, u32[]{:S(2)}) %all-to-all-start) | async-done | bytes 589856 | tf_op jit(solution)/shard_map/all_to_all | solution.py:90
  59.1 2.0 %fusion.3 = f32[128,8,512]{0,2,1:T(8,128)S(1)} fusion(f32[512,128,8]{1,0,2:T(8,128)S(1)} %fusion.26, bf16[128,8,512]{0,2,1:T(8,128)(2,1)S(1)} %copy-done.6, f32[128,8]{0,1:T(8,128)S(1)} %copy-done.11, pred[128,512]{0,1:T(8,128)(4,1)S(1)} %get-tuple-element.16, bf16[512,576]{1,0:T(8,128)(2,1)} %bitcast.14), kind=kOutput, calls=%fused_computation.5 | convolution fusion | flops 539492352 | bytes 5836800 | tf_op jit(solution)/shard_map/thc,kc->thk/dot_general | solution.py:27
  66.0 5.1 %all-to-all-start.2 = ((bf16[8,4,16,576]{3,2,1,0:T(8,128)(2,1)}), bf16[8,4,16,576]{3,2,1,0:T(8,128)(2,1)}, u32[]{:S(2)}, u32[]{:S(2)}) async-start(bf16[8,4,16,576]{3,2,1,0:T(8,128)(2,1)} %bitcast.29), calls=%async_computation.2 | async-start | bytes 1310720 | tf_op jit(solution)/shard_map/all_to_all | solution.py:77
  71.5 2.0 %fusion.13 = bf16[512,512]{0,1:T(8,128)(2,1)S(1)} fusion(f32[512,512]{0,1:T(8,128)} %convolution_bitcast_fusion.2, bf16[128,8,512]{0,2,1:T(8,128)(2,1)S(1)} %fusion.4, bf16[128,8,512]{0,2,1:T(8,128)(2,1)S(1)} %copy-done.8), kind=kOutput, calls=%fused_computation.25 | convolution fusion | flops 537657344 | bytes 3670016 | tf_op jit(solution)/shard_map/thk,thc->kc/dot_general | solution.py:39
  74.4 2.1 %copy.66 = bf16[512,576]{1,0:T(8,128)(2,1)} copy(bf16[512,576]{0,1:T(8,128)(2,1)} %pad_maximum_fusion.1) | data formatting | bytes 1179648 | tf_op jit(solution)/shard_map/concatenate | solution.py:45
  76.5 2.6 %all-to-all-done.2 = bf16[8,4,16,576]{3,2,1,0:T(8,128)(2,1)} async-done(((bf16[8,4,16,576]{3,2,1,0:T(8,128)(2,1)}), bf16[8,4,16,576]{3,2,1,0:T(8,128)(2,1)}, u32[]{:S(2)}, u32[]{:S(2)}) %all-to-all-start.2) | async-done | bytes 589856 | tf_op jit(solution)/shard_map/all_to_all | solution.py:77
  79.1 5.0 %all-to-all-start.1 = ((bf16[8,4,16,576]{3,2,1,0:T(8,128)(2,1)}), bf16[8,4,16,576]{3,2,1,0:T(8,128)(2,1)}, u32[]{:S(2)}, u32[]{:S(2)}) async-start(bf16[8,4,16,576]{3,2,1,0:T(8,128)(2,1)} %bitcast.124), calls=%async_computation.1 | async-start | bytes 1310720 | tf_op jit(solution)/shard_map/all_to_all | solution.py:77
  84.1 2.1 %fusion.23 = f32[128,8,512]{2,0,1:T(8,128)} fusion(bf16[128,8,512]{0,2,1:T(8,128)(2,1)S(1)} %fusion.4, bf16[512,576]{1,0:T(8,128)(2,1)S(1)} %bitcast.118), kind=kOutput, calls=%fused_computation.47 | convolution fusion | flops 536870912 | bytes 3670016 | tf_op jit(solution)/shard_map/thk,kc->thc/dot_general | solution.py:37
  87.4 2.5 %collective-permute-start.3 = (f32[4,16,576]{2,1,0:T(8,128)S(1)}, f32[4,16,576]{2,1,0:T(8,128)S(1)}, u32[]{:S(2)}, u32[]{:S(2)}) collective-permute-start(f32[4,16,576]{2,1,0:T(8,128)S(1)} %convert_reduce_fusion), channel_id=1, source_target_pairs={{32,0},{40,8},{48,16},{56,24},{64,32},{72,40},{80,48},{88,56},{96,... | collective-permute-start | bytes 442376 | tf_op jit(solution)/shard_map/ppermute | solution.py:14
  90.2 1.9 %all-to-all-done.1 = bf16[8,4,16,576]{3,2,1,0:T(8,128)(2,1)} async-done(((bf16[8,4,16,576]{3,2,1,0:T(8,128)(2,1)}), bf16[8,4,16,576]{3,2,1,0:T(8,128)(2,1)}, u32[]{:S(2)}, u32[]{:S(2)}) %all-to-all-start.1) | async-done | bytes 589856 | tf_op jit(solution)/shard_map/all_to_all | solution.py:77
  93.3 3.0 %collective-permute-done.3 = f32[4,16,576]{2,1,0:T(8,128)S(1)} collective-permute-done((f32[4,16,576]{2,1,0:T(8,128)S(1)}, f32[4,16,576]{2,1,0:T(8,128)S(1)}, u32[]{:S(2)}, u32[]{:S(2)}) %collective-permute-start.3) | collective-permute-done | bytes 147488 | tf_op jit(solution)/shard_map/ppermute | solution.py:14
  96.4 4.4 %collective-permute-start.4 = (f32[2,16,576]{2,1,0:T(8,128)S(1)}, f32[2,16,576]{2,1,0:T(8,128)S(1)}, u32[]{:S(2)}, u32[]{:S(2)}) collective-permute-start(f32[2,16,576]{2,1,0:T(8,128)S(1)} %slice.47), channel_id=1, source_target_pairs={{16,0},{24,8},{32,16},{40,24},{48,32},{56,40},{64,48},{72,56},{80,... | collective-permute-start | bytes 221192 | tf_op jit(solution)/shard_map/ppermute | solution.py:14
  100.8 2.5 %multiply_convert_fusion = bf16[128,8,512]{2,0,1:T(8,128)(2,1)S(1)} fusion(f32[128,8,512]{2,0,1:T(8,128)} %fusion.23, bf16[128,8,512]{0,2,1:T(8,128)(2,1)S(1)} %fusion, bf16[512,576]{1,0:T(8,128)(2,1)} %bitcast.14), kind=kOutput, calls=%fused_computation.14 | convolution fusion | flops 538443776 | bytes 4718592 | tf_op jit(solution)/shard_map/thk,kc->thc/dot_general | solution.py:37
  103.3 2.1 %collective-permute-start.5 = (f32[1,16,576]{2,1,0:T(8,128)S(1)}, f32[1,16,576]{2,1,0:T(8,128)S(1)}, u32[]{:S(2)}, u32[]{:S(2)}) collective-permute-start(f32[1,16,576]{2,1,0:T(8,128)S(1)} %slice.49), channel_id=1, source_target_pairs={{8,0},{16,8},{24,16},{32,24},{40,32},{48,40},{56,48},{64,56},{72,6... | collective-permute-start | bytes 110600 | tf_op jit(solution)/shard_map/ppermute | solution.py:14
  (68 shorter events, 23.3 us)
Async XLA Ops:
  0.6 6.2 %copy-start.4 = (bf16[128,8,512]{2,1,0:T(8,128)(2,1)S(1)}, bf16[128,8,512]{2,1,0:T(8,128)(2,1)}, u32[]{:S(2)}) copy-start(bf16[128,8,512]{2,1,0:T(8,128)(2,1)} %param.11) | copy-start | bytes 3145732
  2.5 14.7 %collective-permute-start = (bf16[1,128,576]{2,1,0:T(8,128)(2,1)S(1)}, bf16[1,128,576]{2,1,0:T(8,128)(2,1)S(1)}, u32[]{:S(2)}, u32[]{:S(2)}) collective-permute-start(bf16[1,128,576]{2,1,0:T(8,128)(2,1)S(1)} %get-tuple-element.12), channel_id=1, source_target_pairs={{0,8},{8,16},{16,24},{24,32},{32,40},{40,48},{48,56},{56,64},{64,7... | collective-permute-start | bytes 442376 | tf_op jit(solution)/shard_map/ppermute | solution.py:14
  4.8 3.6 %copy-start.9 = (bf16[128,512]{1,0:T(8,128)(2,1)S(1)}, bf16[128,512]{1,0:T(8,128)(2,1)}, u32[]{:S(2)}) copy-start(bf16[128,512]{1,0:T(8,128)(2,1)} %param.9) | copy-start | bytes 393220
  6.8 12.4 %copy-start.10 = (s32[128]{0:T(128)S(1)}, s32[128]{0:T(128)}, u32[]{:S(2)}) copy-start(s32[128]{0:T(128)} %param.15) | copy-start | bytes 1540
  17.2 14.0 %collective-permute-start.1 = (bf16[2,128,576]{2,1,0:T(8,128)(2,1)S(1)}, bf16[2,128,576]{2,1,0:T(8,128)(2,1)S(1)}, u32[]{:S(2)}, u32[]{:S(2)}) collective-permute-start(bf16[2,128,576]{2,1,0:T(8,128)(2,1)S(1)} %pad_maximum_fusion.3), channel_id=1, source_target_pairs={{0,16},{8,24},{16,32},{24,40},{32,48},{40,56},{48,64},{56,72},{64,... | collective-permute-start | bytes 884744 | tf_op jit(solution)/shard_map/ppermute | solution.py:14
  19.4 14.3 %copy-start.5 = (bf16[128,8,512]{0,2,1:T(8,128)(2,1)S(1)}, bf16[128,8,512]{0,2,1:T(8,128)(2,1)}, u32[]{:S(2)}) copy-start(bf16[128,8,512]{0,2,1:T(8,128)(2,1)} %copy.62) | copy-start | bytes 3145732
  19.4 14.3 %copy-start.11 = (f32[128,8]{0,1:T(8,128)S(1)}, f32[128,8]{0,1:T(8,128)}, u32[]{:S(2)}) copy-start(f32[128,8]{0,1:T(8,128)} %param.12) | copy-start | bytes 12292
  31.3 11.6 %collective-permute-start.2 = (bf16[4,16,576]{2,1,0:T(8,128)(2,1)S(1)}, bf16[4,16,576]{2,1,0:T(8,128)(2,1)S(1)}, u32[]{:S(2)}, u32[]{:S(2)}) collective-permute-start(bf16[4,16,576]{2,1,0:T(8,128)(2,1)S(1)} %fusion.28), channel_id=1, source_target_pairs={{0,32},{8,40},{16,48},{24,56},{32,64},{40,72},{48,80},{56,88},{64,... | collective-permute-start | bytes 221192 | tf_op jit(solution)/shard_map/ppermute | solution.py:14
  33.3 1.4 %copy-start.1 = (bf16[4,8,16,576]{3,2,0,1:T(8,128)(2,1)}, bf16[4,8,16,576]{3,2,0,1:T(8,128)(2,1)S(1)}, u32[]{:S(2)}) copy-start(bf16[4,8,16,576]{3,2,0,1:T(8,128)(2,1)S(1)} %pad_maximum_fusion) | copy-start | bytes 1769476
  34.7 15.0 %copy-start = (f32[128,8,512]{0,2,1:T(8,128)}, f32[128,8,512]{0,2,1:T(8,128)S(1)}, u32[]{:S(2)}) copy-start(f32[128,8,512]{0,2,1:T(8,128)S(1)} %fusion.8) | copy-start | bytes 6291460
  43.8 14.0 %all-to-all-start = ((bf16[8,4,16,576]{3,2,1,0:T(8,128)(2,1)}), bf16[8,4,16,576]{3,2,1,0:T(8,128)(2,1)}, u32[]{:S(2)}, u32[]{:S(2)}) async-start(bf16[8,4,16,576]{3,2,1,0:T(8,128)(2,1)} %broadcast_in_dim.56), calls=%async_computation | async-start | bytes 1310720 | tf_op jit(solution)/shard_map/all_to_all | solution.py:90
  49.7 1.7 %copy-start.2 = (bf16[4,8,16,576]{3,2,0,1:T(8,128)(2,1)S(1)}, bf16[4,8,16,576]{3,2,0,1:T(8,128)(2,1)}, u32[]{:S(2)}) copy-start(bf16[4,8,16,576]{3,2,0,1:T(8,128)(2,1)} %copy-done.1) | copy-start | bytes 1769476
  53.8 5.3 %copy-start.6 = (bf16[128,8,512]{0,2,1:T(8,128)(2,1)S(1)}, bf16[128,8,512]{0,2,1:T(8,128)(2,1)}, u32[]{:S(2)}) copy-start(bf16[128,8,512]{0,2,1:T(8,128)(2,1)} %copy.62) | copy-start | bytes 3145732
  62.9 1.2 %copy-start.7 = (bf16[128,8,512]{0,2,1:T(8,128)(2,1)S(1)}, bf16[128,8,512]{0,2,1:T(8,128)(2,1)}, u32[]{:S(2)}) copy-start(bf16[128,8,512]{0,2,1:T(8,128)(2,1)} %copy.62) | copy-start | bytes 3145732
  66.0 5.5 %copy-start.8 = (bf16[128,8,512]{0,2,1:T(8,128)(2,1)S(1)}, bf16[128,8,512]{0,2,1:T(8,128)(2,1)}, u32[]{:S(2)}) copy-start(bf16[128,8,512]{0,2,1:T(8,128)(2,1)} %copy.62) | copy-start | bytes 3145732
  66.0 13.2 %all-to-all-start.2 = ((bf16[8,4,16,576]{3,2,1,0:T(8,128)(2,1)}), bf16[8,4,16,576]{3,2,1,0:T(8,128)(2,1)}, u32[]{:S(2)}, u32[]{:S(2)}) async-start(bf16[8,4,16,576]{3,2,1,0:T(8,128)(2,1)} %bitcast.29), calls=%async_computation.2 | async-start | bytes 1310720 | tf_op jit(solution)/shard_map/all_to_all | solution.py:77
  73.5 10.6 %copy-start.3 = (bf16[4,8,16,576]{3,2,0,1:T(8,128)(2,1)S(1)}, bf16[4,8,16,576]{3,2,0,1:T(8,128)(2,1)}, u32[]{:S(2)}) copy-start(bf16[4,8,16,576]{3,2,0,1:T(8,128)(2,1)} %copy-done.1) | copy-start | bytes 1769476
  79.1 13.0 %all-to-all-start.1 = ((bf16[8,4,16,576]{3,2,1,0:T(8,128)(2,1)}), bf16[8,4,16,576]{3,2,1,0:T(8,128)(2,1)}, u32[]{:S(2)}, u32[]{:S(2)}) async-start(bf16[8,4,16,576]{3,2,1,0:T(8,128)(2,1)} %bitcast.124), calls=%async_computation.1 | async-start | bytes 1310720 | tf_op jit(solution)/shard_map/all_to_all | solution.py:77
  87.4 9.0 %collective-permute-start.3 = (f32[4,16,576]{2,1,0:T(8,128)S(1)}, f32[4,16,576]{2,1,0:T(8,128)S(1)}, u32[]{:S(2)}, u32[]{:S(2)}) collective-permute-start(f32[4,16,576]{2,1,0:T(8,128)S(1)} %convert_reduce_fusion), channel_id=1, source_target_pairs={{32,0},{40,8},{48,16},{56,24},{64,32},{72,40},{80,48},{88,56},{96,... | collective-permute-start | bytes 442376 | tf_op jit(solution)/shard_map/ppermute | solution.py:14
  96.4 6.9 %collective-permute-start.4 = (f32[2,16,576]{2,1,0:T(8,128)S(1)}, f32[2,16,576]{2,1,0:T(8,128)S(1)}, u32[]{:S(2)}, u32[]{:S(2)}) collective-permute-start(f32[2,16,576]{2,1,0:T(8,128)S(1)} %slice.47), channel_id=1, source_target_pairs={{16,0},{24,8},{32,16},{40,24},{48,32},{56,40},{64,48},{72,56},{80,... | collective-permute-start | bytes 221192 | tf_op jit(solution)/shard_map/ppermute | solution.py:14
  103.3 5.7 %collective-permute-start.5 = (f32[1,16,576]{2,1,0:T(8,128)S(1)}, f32[1,16,576]{2,1,0:T(8,128)S(1)}, u32[]{:S(2)}, u32[]{:S(2)}) collective-permute-start(f32[1,16,576]{2,1,0:T(8,128)S(1)} %slice.49), channel_id=1, source_target_pairs={{8,0},{16,8},{24,16},{32,24},{40,32},{48,40},{56,48},{64,56},{72,6... | collective-permute-start | bytes 110600 | tf_op jit(solution)/shard_map/ppermute | solution.py:14

commit v7 on v6

--- a/solution.py
+++ b/solution.py
@@ -90,9 +90,11 @@
         return lax.all_to_all(spread, "head", 0, 0, tiled=True)
 
     near = near_full.reshape(half_span, groups, block, -1).transpose(1, 0, 2, 3)
+    near_terms = terms(near, own_tile - half_span + 1)
+    far_rows, near_terms = lax.optimization_barrier((far_rows, near_terms))
+    near_qlat, near_qrot, near_part = near_terms
     far = assemble(far_rows)
 
-    near_qlat, near_qrot, near_part = terms(near, own_tile - half_span + 1)
     far_qlat, far_qrot, far_part = terms(far, own_tile - span + 1)
     grad_qlat = softmax_scale * (near_qlat + far_qlat)
     grad_qrot = softmax_scale * (near_qrot + far_qrot)

time: 112 us -> 112 us (level)
  blocking collectives: 0 us -> 13.8 us
  matrix products: 21 us -> 13.7 us
  starting transfers between devices: 30.7 us -> 24.3 us
  waiting for transfers between devices: 37.5 us -> 40.2 us
  other arithmetic: 6.36 us -> 4.94 us
    all_to_all x0 -> x1, blocking collectives: none -> 13.8 us  [assemble(): return lax.all_to_all(spread, 'head', 0, 0, tiled=True)]
    all_to_all x1 -> x0, starting transfers between devices: 5.93 us -> none  [assemble(): return lax.all_to_all(spread, 'head', 0, 0, tiled=True)]
    all_to_all x2, waiting for transfers between devices: 4.51 us -> 10.2 us  [group_sum(): got = lax.all_to_all(part, 'head', 0, 0, tiled=True)]
    all_to_all x1 -> x0, waiting for transfers between devices: 3.97 us -> none  [assemble(): return lax.all_to_all(spread, 'head', 0, 0, tiled=True)]
    concatenate x2 -> x1, local copies, waits for them, and re-layouts: 3.22 us -> 1.08 us  [window_terms(): return (grad_qlat, grad_qrot, jnp.concatenate([grad_lat, grad_rot], axis=1))]
    dot_general x2, matrix products: 4.11 us -> 2.11 us  [window_terms(): jnp.einsum('thc,kc->thk', grad_out, lat_all, preferred_element_type=jnp.f...]
    dot_general x2, matrix products: 4.58 us -> 2.8 us  [window_terms(): jnp.einsum('thk,kc->thc', grad_b, lat_all, preferred_element_type=jnp.flo...]
    concatenate x0 -> x1, other arithmetic: none -> 1.61 us  [local(): near_full = jnp.concatenate([latent, key_rope], axis=1)[None]]
  transfers between devices with their start and end apart: 9 -> 8, of which waited for: 7 -> 7; matrix products, arithmetic and copies ran while one was open for 26% -> 13% of each run, Pallas kernels for 0% -> 0%
where the time goes in v7:
time: 112 us; the launch traced here: 111 us
  waiting for transfers between devices  40.2 us (36%)
  starting transfers between devices  24.3 us (22%)
  blocking collectives  13.8 us (12%)
  matrix products  13.7 us (12%)
  local copies, waits for them, and re-layouts  12.6 us (11%)
  other arithmetic  4.94 us (4%)
    ppermute x6, waiting for transfers between devices, shifted(): return lax.ppermute(x, axis, pairs)  30 us
    ppermute x6, starting transfers between devices, shifted(): return lax.ppermute(x, axis, pairs)  15.2 us
    all_to_all x1, blocking collectives, assemble(): return lax.all_to_all(spread, 'head', 0, 0, tiled=True)  13.8 us
    all_to_all x2, waiting for transfers between devices, group_sum(): got = lax.all_to_all(part, 'head', 0, 0, tiled=True)  10.2 us
    all_to_all x2, starting transfers between devices, group_sum(): got = lax.all_to_all(part, 'head', 0, 0, tiled=True)  9.14 us
    unnamed x24, local copies, waits for them, and re-layouts  8.98 us
    dot_general x2, matrix products, window_terms(): jnp.einsum('thk,kc->thc', grad_b, lat_all, preferred_element_type=jnp.flo...  2.8 us
    dot_general x2, matrix products, window_terms(): jnp.einsum('thc,kc->thk', q_latent, lat_all, preferred_element_type=jnp.f...  2.67 us
  transfers between devices with their start and end apart: 8, of which 7 were waited for; matrix products, arithmetic and copies ran while one was open for 13% of the time, Pallas kernels for 0%

profile of v7, /device:TPU:6, one launch (start us, length us, event | category | flops | bytes accessed | tf_op | source)
XLA Modules:
  0.0 110.6 jit_solution(18259775026465921554)
XLA Ops:
  1.6 1.6 %pad_maximum_fusion.4 = (bf16[128,576]{1,0:T(8,128)(2,1)}, bf16[1,128,576]{2,1,0:T(8,128)(2,1)S(1)}) fusion(bf16[128,64]{1,0:T(8,128)(2,1)S(1)} %copy.44, bf16[128,512]{1,0:T(8,128)(2,1)} %param.13), kind=kLoop, calls=%fused_computation.51 | loop fusion | flops 294912 | bytes 442368 | tf_op jit(solution)/shard_map/concatenate | solution.py:80
  3.2 1.9 %collective-permute-start = (bf16[1,128,576]{2,1,0:T(8,128)(2,1)S(1)}, bf16[1,128,576]{2,1,0:T(8,128)(2,1)S(1)}, u32[]{:S(2)}, u32[]{:S(2)}) collective-permute-start(bf16[1,128,576]{2,1,0:T(8,128)(2,1)S(1)} %get-tuple-element.21), channel_id=1, source_target_pairs={{0,8},{8,16},{16,24},{24,32},{32,40},{40,48},{48,56},{56,64},{64,7... | collective-permute-start | bytes 442376 | tf_op jit(solution)/shard_map/ppermute | solution.py:14
  5.5 1.9 %copy.58 = bf16[128,8,512]{0,2,1:T(8,128)(2,1)S(1)} copy(bf16[128,8,512]{2,1,0:T(8,128)(2,1)} %param.11) | data formatting | bytes 2097152 | tf_op args[3]
  8.9 2.7 %copy.56 = bf16[128,8,512]{0,2,1:T(8,128)(2,1)} copy(bf16[128,8,512]{2,1,0:T(8,128)(2,1)} %param.8) | data formatting | bytes 2097152 | tf_op args[0]
  11.6 6.3 %collective-permute-done = bf16[1,128,576]{2,1,0:T(8,128)(2,1)S(1)} collective-permute-done((bf16[1,128,576]{2,1,0:T(8,128)(2,1)S(1)}, bf16[1,128,576]{2,1,0:T(8,128)(2,1)S(1)}, u32[]{:S(2)}, u32[]{:S(2)}) %collective-permute-start) | collective-permute-done | bytes 147488 | tf_op jit(solution)/shard_map/ppermute | solution.py:14
  18.0 1.9 %collective-permute-start.1 = (bf16[2,128,576]{2,1,0:T(8,128)(2,1)S(1)}, bf16[2,128,576]{2,1,0:T(8,128)(2,1)S(1)}, u32[]{:S(2)}, u32[]{:S(2)}) collective-permute-start(bf16[2,128,576]{2,1,0:T(8,128)(2,1)S(1)} %pad_maximum_fusion.3), channel_id=1, source_target_pairs={{0,16},{8,24},{16,32},{24,40},{32,48},{40,56},{48,64},{56,72},{64,... | collective-permute-start | bytes 884744 | tf_op jit(solution)/shard_map/ppermute | solution.py:14
  20.1 11.6 %collective-permute-done.1 = bf16[2,128,576]{2,1,0:T(8,128)(2,1)S(1)} collective-permute-done((bf16[2,128,576]{2,1,0:T(8,128)(2,1)S(1)}, bf16[2,128,576]{2,1,0:T(8,128)(2,1)S(1)}, u32[]{:S(2)}, u32[]{:S(2)}) %collective-permute-start.1) | collective-permute-done | bytes 294944 | tf_op jit(solution)/shard_map/ppermute | solution.py:14
  32.3 1.3 %fusion.8 = f32[128,8,512]{0,2,1:T(8,128)S(1)} fusion(f32[512,128,8]{1,0,2:T(8,128)S(1)} %fusion.26, f32[128,8]{0,1:T(8,128)S(1)} %copy-done.8, pred[128,512]{0,1:T(8,128)(4,1)S(1)} %get-tuple-element.25, bf16[128,8,512]{2,1,0:T(8,128)(2,1)S(1)} %copy-done.3, bf16[512,576]{1,0:T(8,128)(2,1)S(1)} %bitcast.113), kind=kOutput, calls=%fused_computation.13 | convolution fusion | flops 539492352 | bytes 5836800 | tf_op jit(solution)/shard_map/thc,kc->thk/dot_general | solution.py:27
  36.2 2.1 %fusion.23 = f32[128,8,512]{2,0,1:T(8,128)} fusion(bf16[128,8,512]{0,2,1:T(8,128)(2,1)S(1)} %fusion.4, bf16[512,576]{1,0:T(8,128)(2,1)S(1)} %bitcast.116), kind=kOutput, calls=%fused_computation.46 | convolution fusion | flops 536870912 | bytes 3670016 | tf_op jit(solution)/shard_map/thk,kc->thc/dot_general | solution.py:37
  38.3 2.1 %collective-permute-start.2 = (bf16[4,16,576]{2,1,0:T(8,128)(2,1)S(1)}, bf16[4,16,576]{2,1,0:T(8,128)(2,1)S(1)}, u32[]{:S(2)}, u32[]{:S(2)}) collective-permute-start(bf16[4,16,576]{2,1,0:T(8,128)(2,1)S(1)} %fusion.30), channel_id=1, source_target_pairs={{0,32},{8,40},{16,48},{24,56},{32,64},{40,72},{48,80},{56,88},{64,... | collective-permute-start | bytes 221192 | tf_op jit(solution)/shard_map/ppermute | solution.py:14
  41.9 8.1 %collective-permute-done.2 = bf16[4,16,576]{2,1,0:T(8,128)(2,1)S(1)} collective-permute-done((bf16[4,16,576]{2,1,0:T(8,128)(2,1)S(1)}, bf16[4,16,576]{2,1,0:T(8,128)(2,1)S(1)}, u32[]{:S(2)}, u32[]{:S(2)}) %collective-permute-start.2) | collective-permute-done | bytes 73760 | tf_op jit(solution)/shard_map/ppermute | solution.py:14
  50.1 13.8 %all_to_all.15 = bf16[8,4,16,576]{3,2,1,0:T(8,128)(2,1)S(1)} all-to-all(bf16[8,4,16,576]{3,2,1,0:T(8,128)(2,1)S(1)} %broadcast_in_dim.56), channel_id=1, replica_groups=mesh['ctx'=64,'head'=8] {'head'}, dimensions={0} | all-to-all | bytes 1179648 | tf_op jit(solution)/shard_map/all_to_all | solution.py:90
  64.3 1.4 %fusion.3 = f32[128,8,512]{0,2,1:T(8,128)S(1)} fusion(f32[512,128,8]{1,0,2:T(8,128)S(1)} %fusion.28, f32[128,8]{0,1:T(8,128)S(1)} %copy-done.8, pred[128,512]{0,1:T(8,128)(4,1)S(1)} %get-tuple-element.24, bf16[128,8,512]{2,1,0:T(8,128)(2,1)S(1)} %copy-done.3, bf16[512,576]{1,0:T(8,128)(2,1)S(1)} %bitcast.108), kind=kOutput, calls=%fused_computation.5 | convolution fusion | flops 539492352 | bytes 5836800 | tf_op jit(solution)/shard_map/thc,kc->thk/dot_general | solution.py:27
  68.7 1.1 copy.72
  69.7 4.8 %all-to-all-start.2 = ((bf16[8,4,16,576]{3,2,1,0:T(8,128)(2,1)}), bf16[8,4,16,576]{3,2,1,0:T(8,128)(2,1)S(1)}, u32[]{:S(2)}, u32[]{:S(2)}) async-start(bf16[8,4,16,576]{3,2,1,0:T(8,128)(2,1)} %bitcast.29), calls=%async_computation.2 | async-start | bytes 1310720 | tf_op jit(solution)/shard_map/all_to_all | solution.py:77
  75.6 6.9 %all-to-all-done.2 = bf16[8,4,16,576]{3,2,1,0:T(8,128)(2,1)S(1)} async-done(((bf16[8,4,16,576]{3,2,1,0:T(8,128)(2,1)}), bf16[8,4,16,576]{3,2,1,0:T(8,128)(2,1)S(1)}, u32[]{:S(2)}, u32[]{:S(2)}) %all-to-all-start.2) | async-done | bytes 589856 | tf_op jit(solution)/shard_map/all_to_all | solution.py:77
  82.5 4.3 %all-to-all-start.1 = ((bf16[8,4,16,576]{3,2,1,0:T(8,128)(2,1)}), bf16[8,4,16,576]{3,2,1,0:T(8,128)(2,1)S(1)}, u32[]{:S(2)}, u32[]{:S(2)}) async-start(bf16[8,4,16,576]{3,2,1,0:T(8,128)(2,1)} %bitcast.25), calls=%async_computation.1 | async-start | bytes 1310720 | tf_op jit(solution)/shard_map/all_to_all | solution.py:77
  88.3 2.5 %collective-permute-start.3 = (f32[4,16,576]{2,1,0:T(8,128)}, f32[4,16,576]{2,1,0:T(8,128)}, u32[]{:S(2)}, u32[]{:S(2)}) collective-permute-start(f32[4,16,576]{2,1,0:T(8,128)} %convert_reduce_fusion), channel_id=1, source_target_pairs={{32,0},{40,8},{48,16},{56,24},{64,32},{72,40},{80,48},{88,56},{96,... | collective-permute-start | bytes 442376 | tf_op jit(solution)/shard_map/ppermute | solution.py:14
  91.4 3.3 %all-to-all-done.1 = bf16[8,4,16,576]{3,2,1,0:T(8,128)(2,1)S(1)} async-done(((bf16[8,4,16,576]{3,2,1,0:T(8,128)(2,1)}), bf16[8,4,16,576]{3,2,1,0:T(8,128)(2,1)S(1)}, u32[]{:S(2)}, u32[]{:S(2)}) %all-to-all-start.1) | async-done | bytes 589856 | tf_op jit(solution)/shard_map/all_to_all | solution.py:77
  94.9 2.3 %collective-permute-done.3 = f32[4,16,576]{2,1,0:T(8,128)} collective-permute-done((f32[4,16,576]{2,1,0:T(8,128)}, f32[4,16,576]{2,1,0:T(8,128)}, u32[]{:S(2)}, u32[]{:S(2)}) %collective-permute-start.3) | collective-permute-done | bytes 147488 | tf_op jit(solution)/shard_map/ppermute | solution.py:14
  98.1 4.9 %collective-permute-start.4 = (f32[2,16,576]{2,1,0:T(8,128)S(1)}, f32[2,16,576]{2,1,0:T(8,128)S(1)}, u32[]{:S(2)}, u32[]{:S(2)}) collective-permute-start(f32[2,16,576]{2,1,0:T(8,128)S(1)} %slice.47), channel_id=1, source_target_pairs={{16,0},{24,8},{32,16},{40,24},{48,32},{56,40},{64,48},{72,56},{80,... | collective-permute-start | bytes 221192 | tf_op jit(solution)/shard_map/ppermute | solution.py:14
  103.3 1.7 %collective-permute-done.4 = f32[2,16,576]{2,1,0:T(8,128)S(1)} collective-permute-done((f32[2,16,576]{2,1,0:T(8,128)S(1)}, f32[2,16,576]{2,1,0:T(8,128)S(1)}, u32[]{:S(2)}, u32[]{:S(2)}) %collective-permute-start.4) | collective-permute-done | bytes 73760 | tf_op jit(solution)/shard_map/ppermute | solution.py:14
  105.0 1.9 %collective-permute-start.5 = (f32[1,16,576]{2,1,0:T(8,128)S(1)}, f32[1,16,576]{2,1,0:T(8,128)S(1)}, u32[]{:S(2)}, u32[]{:S(2)}) collective-permute-start(f32[1,16,576]{2,1,0:T(8,128)S(1)} %slice.49), channel_id=1, source_target_pairs={{8,0},{16,8},{24,16},{32,24},{40,32},{48,40},{56,48},{64,56},{72,6... | collective-permute-start | bytes 110600 | tf_op jit(solution)/shard_map/ppermute | solution.py:14
  107.8 1.5 %copy.73 = bf16[128,8,512]{2,1,0:T(8,128)(2,1)} copy(bf16[128,8,512]{2,0,1:T(8,128)(2,1)S(1)} %multiply_convert_fusion) | data formatting | bytes 2097152
  (63 shorter events, 17.6 us)
Async XLA Ops:
  0.6 6.8 %copy-start = (bf16[128,8,512]{2,1,0:T(8,128)(2,1)S(1)}, bf16[128,8,512]{2,1,0:T(8,128)(2,1)}, u32[]{:S(2)}) copy-start(bf16[128,8,512]{2,1,0:T(8,128)(2,1)} %param.11) | copy-start | bytes 3145732
  0.6 6.8 %copy-start.2 = (bf16[128,8,512]{2,1,0:T(8,128)(2,1)S(1)}, bf16[128,8,512]{2,1,0:T(8,128)(2,1)}, u32[]{:S(2)}) copy-start(bf16[128,8,512]{2,1,0:T(8,128)(2,1)} %param.10) | copy-start | bytes 3145732
  3.2 14.7 %collective-permute-start = (bf16[1,128,576]{2,1,0:T(8,128)(2,1)S(1)}, bf16[1,128,576]{2,1,0:T(8,128)(2,1)S(1)}, u32[]{:S(2)}, u32[]{:S(2)}) collective-permute-start(bf16[1,128,576]{2,1,0:T(8,128)(2,1)S(1)} %get-tuple-element.21), channel_id=1, source_target_pairs={{0,8},{8,16},{16,24},{24,32},{32,40},{40,48},{48,56},{56,64},{64,7... | collective-permute-start | bytes 442376 | tf_op jit(solution)/shard_map/ppermute | solution.py:14
  7.5 12.4 %copy-start.7 = (s32[128]{0:T(128)S(1)}, s32[128]{0:T(128)}, u32[]{:S(2)}) copy-start(s32[128]{0:T(128)} %param.15) | copy-start | bytes 1540
  7.8 23.9 %copy-start.6 = (bf16[128,576]{1,0:T(8,128)(2,1)S(1)}, bf16[128,576]{1,0:T(8,128)(2,1)}, u32[]{:S(2)}) copy-start(bf16[128,576]{1,0:T(8,128)(2,1)} %get-tuple-element.20) | copy-start | bytes 442372
  11.6 20.6 %copy-start.3 = (bf16[128,8,512]{2,1,0:T(8,128)(2,1)S(1)}, bf16[128,8,512]{2,1,0:T(8,128)(2,1)}, u32[]{:S(2)}) copy-start(bf16[128,8,512]{2,1,0:T(8,128)(2,1)} %param.8) | copy-start | bytes 3145732
  11.6 20.6 %copy-start.8 = (f32[128,8]{0,1:T(8,128)S(1)}, f32[128,8]{0,1:T(8,128)}, u32[]{:S(2)}) copy-start(f32[128,8]{0,1:T(8,128)} %param.12) | copy-start | bytes 12292
  18.0 13.8 %collective-permute-start.1 = (bf16[2,128,576]{2,1,0:T(8,128)(2,1)S(1)}, bf16[2,128,576]{2,1,0:T(8,128)(2,1)S(1)}, u32[]{:S(2)}, u32[]{:S(2)}) collective-permute-start(bf16[2,128,576]{2,1,0:T(8,128)(2,1)S(1)} %pad_maximum_fusion.3), channel_id=1, source_target_pairs={{0,16},{8,24},{16,32},{24,40},{32,48},{40,56},{48,64},{56,72},{64,... | collective-permute-start | bytes 884744 | tf_op jit(solution)/shard_map/ppermute | solution.py:14
  38.2 2.8 %copy-start.4 = (bf16[128,8,512]{0,2,1:T(8,128)(2,1)S(1)}, bf16[128,8,512]{0,2,1:T(8,128)(2,1)}, u32[]{:S(2)}) copy-start(bf16[128,8,512]{0,2,1:T(8,128)(2,1)} %copy.56) | copy-start | bytes 3145732
  38.3 11.8 %collective-permute-start.2 = (bf16[4,16,576]{2,1,0:T(8,128)(2,1)S(1)}, bf16[4,16,576]{2,1,0:T(8,128)(2,1)S(1)}, u32[]{:S(2)}, u32[]{:S(2)}) collective-permute-start(bf16[4,16,576]{2,1,0:T(8,128)(2,1)S(1)} %fusion.30), channel_id=1, source_target_pairs={{0,32},{8,40},{16,48},{24,56},{32,64},{40,72},{48,80},{56,88},{64,... | collective-permute-start | bytes 221192 | tf_op jit(solution)/shard_map/ppermute | solution.py:14
  69.7 12.8 %all-to-all-start.2 = ((bf16[8,4,16,576]{3,2,1,0:T(8,128)(2,1)}), bf16[8,4,16,576]{3,2,1,0:T(8,128)(2,1)S(1)}, u32[]{:S(2)}, u32[]{:S(2)}) async-start(bf16[8,4,16,576]{3,2,1,0:T(8,128)(2,1)} %bitcast.29), calls=%async_computation.2 | async-start | bytes 1310720 | tf_op jit(solution)/shard_map/all_to_all | solution.py:77
  82.5 12.3 %all-to-all-start.1 = ((bf16[8,4,16,576]{3,2,1,0:T(8,128)(2,1)}), bf16[8,4,16,576]{3,2,1,0:T(8,128)(2,1)S(1)}, u32[]{:S(2)}, u32[]{:S(2)}) async-start(bf16[8,4,16,576]{3,2,1,0:T(8,128)(2,1)} %bitcast.25), calls=%async_computation.1 | async-start | bytes 1310720 | tf_op jit(solution)/shard_map/all_to_all | solution.py:77
  86.8 4.0 %copy-start.1 = (f32[128,8,512]{2,0,1:T(8,128)S(1)}, f32[128,8,512]{2,0,1:T(8,128)}, u32[]{:S(2)}) copy-start(f32[128,8,512]{2,0,1:T(8,128)} %fusion.23) | copy-start | bytes 6291460
  88.3 8.8 %collective-permute-start.3 = (f32[4,16,576]{2,1,0:T(8,128)}, f32[4,16,576]{2,1,0:T(8,128)}, u32[]{:S(2)}, u32[]{:S(2)}) collective-permute-start(f32[4,16,576]{2,1,0:T(8,128)} %convert_reduce_fusion), channel_id=1, source_target_pairs={{32,0},{40,8},{48,16},{56,24},{64,32},{72,40},{80,48},{88,56},{96,... | collective-permute-start | bytes 442376 | tf_op jit(solution)/shard_map/ppermute | solution.py:14
  94.8 12.2 %copy-start.5 = (f32[128,8,64]{0,2,1:T(8,128)S(1)}, f32[128,8,64]{0,2,1:T(8,128)}, u32[]{:S(2)}) copy-start(f32[128,8,64]{0,2,1:T(8,128)} %fusion.25) | copy-start | bytes 786436
  98.1 6.9 %collective-permute-start.4 = (f32[2,16,576]{2,1,0:T(8,128)S(1)}, f32[2,16,576]{2,1,0:T(8,128)S(1)}, u32[]{:S(2)}, u32[]{:S(2)}) collective-permute-start(f32[2,16,576]{2,1,0:T(8,128)S(1)} %slice.47), channel_id=1, source_target_pairs={{16,0},{24,8},{32,16},{40,24},{48,32},{56,40},{64,48},{72,56},{80,... | collective-permute-start | bytes 221192 | tf_op jit(solution)/shard_map/ppermute | solution.py:14
  105.0 4.3 %collective-permute-start.5 = (f32[1,16,576]{2,1,0:T(8,128)S(1)}, f32[1,16,576]{2,1,0:T(8,128)S(1)}, u32[]{:S(2)}, u32[]{:S(2)}) collective-permute-start(f32[1,16,576]{2,1,0:T(8,128)S(1)} %slice.49), channel_id=1, source_target_pairs={{8,0},{16,8},{24,16},{32,24},{40,32},{48,40},{56,48},{64,56},{72,6... | collective-permute-start | bytes 110600 | tf_op jit(solution)/shard_map/ppermute | solution.py:14

commit v8 on v6

--- a/solution.py
+++ b/solution.py
@@ -77,13 +77,13 @@
         got = lax.all_to_all(part, "head", 0, 0, tiled=True)
         return got.astype(jnp.float32).sum(axis=0)
 
-    near_full = jnp.concatenate([latent, key_rope], axis=1)[None]
-    width = 1
-    while width < half_span:
-        near_full = jnp.concatenate([shifted(near_full, "ctx", width), near_full], axis=0)
-        width *= 2
-    rows = lax.dynamic_slice_in_dim(near_full, lax.axis_index("head") * block, block, axis=1)
-    far_rows = shifted(rows, "ctx", half_span)
+    pair = jnp.concatenate([latent, key_rope], axis=1)[None]
+    pair = jnp.concatenate([shifted(pair, "ctx", 1), pair], axis=0)
+    near_full = jnp.concatenate([shifted(pair, "ctx", 2), pair], axis=0)
+    rows = lax.dynamic_slice_in_dim(pair, lax.axis_index("head") * block, block, axis=1)
+    far_rows = jnp.concatenate(
+        [shifted(rows, "ctx", half_span + 2), shifted(rows, "ctx", half_span)], axis=0
+    )
 
     def assemble(part):
         spread = jnp.broadcast_to(part[None], (groups,) + part.shape)

time: 112 us -> 109 us (0.973)
  waiting for transfers between devices: 37.5 us -> 23.8 us
  starting transfers between devices: 30.7 us -> 40.5 us
  other arithmetic: 6.36 us -> 11.5 us
  matrix products: 21 us -> 17.3 us
    ppermute x6 -> x7, waiting for transfers between devices: 29 us -> 16.5 us  [shifted(): return lax.ppermute(x, axis, pairs)]
    ppermute x6 -> x7, starting transfers between devices: 14.7 us -> 24.4 us  [shifted(): return lax.ppermute(x, axis, pairs)]
    concatenate x3 -> x4, other arithmetic: 0.13 us -> 3.32 us  [the longest x2 1.39 us: local(): pair = jnp.concatenate([shifted(pair, 'ctx', 1), pair], axis=0)]
    dot_general x2, matrix products: 4.11 us -> 2.51 us  [window_terms(): jnp.einsum('thc,kc->thk', grad_out, lat_all, preferred_element_type=jnp.f...]
    and x1, other arithmetic: 0.2 us -> 1.48 us  [window_terms(): (key_pos[None, :] >= doc_start[:, None]) & (key_pos[None, :] <= query_pos...]
  transfers between devices with their start and end apart: 9 -> 10, of which waited for: 7 -> 4; matrix products, arithmetic and copies ran while one was open for 26% -> 29% of each run, Pallas kernels for 0% -> 0%
where the time goes in v8:
time: 109 us; the launch traced here: 108 us
  starting transfers between devices  40.5 us (37%)
  waiting for transfers between devices  23.8 us (22%)
  matrix products  17.3 us (16%)
  local copies, waits for them, and re-layouts  13.7 us (13%)
  other arithmetic  11.5 us (11%)
    ppermute x7, starting transfers between devices, shifted(): return lax.ppermute(x, axis, pairs)  24.4 us
    ppermute x7, waiting for transfers between devices, shifted(): return lax.ppermute(x, axis, pairs)  16.5 us
    all_to_all x2, starting transfers between devices, group_sum(): got = lax.all_to_all(part, 'head', 0, 0, tiled=True)  10.1 us
    unnamed x30, local copies, waits for them, and re-layouts  8.06 us
    all_to_all x1, starting transfers between devices, assemble(): return lax.all_to_all(spread, 'head', 0, 0, tiled=True)  5.93 us
    dot_general x2, matrix products, window_terms(): jnp.einsum('thk,kc->thc', grad_b, lat_all, preferred_element_type=jnp.flo...  4.41 us
    all_to_all x1, waiting for transfers between devices, assemble(): return lax.all_to_all(spread, 'head', 0, 0, tiled=True)  3.87 us
    all_to_all x2, waiting for transfers between devices, group_sum(): got = lax.all_to_all(part, 'head', 0, 0, tiled=True)  3.43 us
  transfers between devices with their start and end apart: 10, of which 4 were waited for; matrix products, arithmetic and copies ran while one was open for 29% of the time, Pallas kernels for 0%

profile of v8, /device:TPU:6, one launch (start us, length us, event | category | flops | bytes accessed | tf_op | source)
XLA Modules:
  0.0 107.7 jit_solution(5649434927374862)
XLA Ops:
  1.6 1.6 %fusion.32 = (bf16[1,128,576]{2,1,0:T(8,128)(2,1)S(1)}, bf16[128,576]{1,0:T(8,128)(2,1)}) fusion(bf16[128,64]{1,0:T(8,128)(2,1)S(1)} %copy.44, bf16[128,512]{1,0:T(8,128)(2,1)} %param.13), kind=kLoop, calls=%fused_computation.68 | loop fusion | flops 294912 | bytes 442368 | tf_op jit(solution)/shard_map/broadcast_in_dim | solution.py:80
  3.2 1.9 %collective-permute-start = (bf16[1,128,576]{2,1,0:T(8,128)(2,1)S(1)}, bf16[1,128,576]{2,1,0:T(8,128)(2,1)S(1)}, u32[]{:S(2)}, u32[]{:S(2)}) collective-permute-start(bf16[1,128,576]{2,1,0:T(8,128)(2,1)S(1)} %get-tuple-element.12), channel_id=1, source_target_pairs={{0,8},{8,16},{16,24},{24,32},{32,40},{40,48},{48,56},{56,64},{64,7... | collective-permute-start | bytes 442376 | tf_op jit(solution)/shard_map/ppermute | solution.py:14
  6.9 10.9 %collective-permute-done = bf16[1,128,576]{2,1,0:T(8,128)(2,1)S(1)} collective-permute-done((bf16[1,128,576]{2,1,0:T(8,128)(2,1)S(1)}, bf16[1,128,576]{2,1,0:T(8,128)(2,1)S(1)}, u32[]{:S(2)}, u32[]{:S(2)}) %collective-permute-start) | collective-permute-done | bytes 147488 | tf_op jit(solution)/shard_map/ppermute | solution.py:14
  18.5 1.9 %collective-permute-start.3 = (bf16[2,16,576]{2,1,0:T(8,128)(2,1)}, bf16[2,16,576]{2,1,0:T(8,128)(2,1)S(1)}, u32[]{:S(2)}, u32[]{:S(2)}) collective-permute-start(bf16[2,16,576]{2,1,0:T(8,128)(2,1)} %fusion.27), channel_id=1, source_target_pairs={{0,32},{8,40},{16,48},{24,56},{32,64},{40,72},{48,80},{56,88},{64,... | collective-permute-start | bytes 110600 | tf_op jit(solution)/shard_map/ppermute | solution.py:14
  20.4 3.0 %collective-permute-start.2 = (bf16[2,16,576]{2,1,0:T(8,128)(2,1)}, bf16[2,16,576]{2,1,0:T(8,128)(2,1)}, u32[]{:S(2)}, u32[]{:S(2)}) collective-permute-start(bf16[2,16,576]{2,1,0:T(8,128)(2,1)} %fusion.27), channel_id=1, source_target_pairs={{0,48},{8,56},{16,64},{24,72},{32,80},{40,88},{48,96},{56,104},{64... | collective-permute-start | bytes 110600 | tf_op jit(solution)/shard_map/ppermute | solution.py:14
  24.1 3.9 %collective-permute-start.1 = (bf16[2,128,576]{2,1,0:T(8,128)(2,1)}, bf16[2,128,576]{2,1,0:T(8,128)(2,1)}, u32[]{:S(2)}, u32[]{:S(2)}) collective-permute-start(bf16[2,128,576]{2,1,0:T(8,128)(2,1)} %pad_maximum_fusion.3), channel_id=1, source_target_pairs={{0,16},{8,24},{16,32},{24,40},{32,48},{40,56},{48,64},{56,72},{64,... | collective-permute-start | bytes 884744 | tf_op jit(solution)/shard_map/ppermute | solution.py:14
  28.1 1.6 %fusion.5 = f32[128,8]{1,0:T(8,128)S(1)} fusion(bf16[128,8,512]{2,1,0:T(8,128)(2,1)S(1)} %copy-done.4, bf16[128,8,512]{2,1,0:T(8,128)(2,1)} %param.10), kind=kLoop, calls=%fused_computation.9 | loop fusion | flops 2096128 | bytes 2101248
  31.8 1.7 %copy.62 = bf16[128,8,512]{0,2,1:T(8,128)(2,1)} copy(bf16[128,8,512]{2,1,0:T(8,128)(2,1)S(1)} %copy-done.5) | data formatting | bytes 2097152 | tf_op args[0]
  35.2 5.9 %all-to-all-start = ((bf16[8,4,16,576]{3,2,1,0:T(8,128)(2,1)}), bf16[8,4,16,576]{3,2,1,0:T(8,128)(2,1)S(1)}, u32[]{:S(2)}, u32[]{:S(2)}) async-start(bf16[8,4,16,576]{3,2,1,0:T(8,128)(2,1)} %broadcast_in_dim.56), calls=%async_computation | async-start | bytes 1310720 | tf_op jit(solution)/shard_map/all_to_all | solution.py:90
  43.7 1.7 %convolution_bitcast_fusion.2 = f32[512,512]{0,1:T(8,128)} fusion(bf16[128,8,512]{0,2,1:T(8,128)(2,1)S(1)} %copy.64, f32[128,8,512]{0,2,1:T(8,128)S(1)} %fusion.8), kind=kOutput, calls=%fused_computation.19 | convolution fusion | flops 537395200 | bytes 4194304 | tf_op jit(solution)/shard_map/thk,thc->kc/dot_general | solution.py:41
  46.2 3.9 %all-to-all-done = bf16[8,4,16,576]{3,2,1,0:T(8,128)(2,1)S(1)} async-done(((bf16[8,4,16,576]{3,2,1,0:T(8,128)(2,1)}), bf16[8,4,16,576]{3,2,1,0:T(8,128)(2,1)S(1)}, u32[]{:S(2)}, u32[]{:S(2)}) %all-to-all-start) | async-done | bytes 589856 | tf_op jit(solution)/shard_map/all_to_all | solution.py:90
  52.5 1.8 %fusion = bf16[128,8,512]{0,2,1:T(8,128)(2,1)S(1)} fusion(f32[128,8,512]{0,2,1:T(8,128)S(1)} %fusion.3, bf16[128,8,512]{0,2,1:T(8,128)(2,1)S(1)} %copy.64, f32[128,8]{0,1:T(8,128)S(1)} %copy.80, bf16[512,576]{1,0:T(8,128)(2,1)} %bitcast.117), kind=kOutput, calls=%fused_computation.1 | convolution fusion | flops 538443776 | bytes 4722688 | tf_op jit(solution)/shard_map/thc,kc->thk/dot_general | solution.py:33
  57.4 5.1 %all-to-all-start.2 = ((bf16[8,4,16,576]{3,2,1,0:T(8,128)(2,1)}), bf16[8,4,16,576]{3,2,1,0:T(8,128)(2,1)}, u32[]{:S(2)}, u32[]{:S(2)}) async-start(bf16[8,4,16,576]{3,2,1,0:T(8,128)(2,1)} %bitcast.29), calls=%async_computation.2 | async-start | bytes 1310720 | tf_op jit(solution)/shard_map/all_to_all | solution.py:77
  62.9 2.0 %fusion.13 = bf16[512,512]{0,1:T(8,128)(2,1)S(1)} fusion(f32[512,512]{0,1:T(8,128)} %convolution_bitcast_fusion.2, bf16[128,8,512]{0,2,1:T(8,128)(2,1)S(1)} %fusion.4, bf16[128,8,512]{0,2,1:T(8,128)(2,1)S(1)} %copy-done.8), kind=kOutput, calls=%fused_computation.25 | convolution fusion | flops 537657344 | bytes 3670016 | tf_op jit(solution)/shard_map/thk,thc->kc/dot_general | solution.py:39
  65.8 2.1 %copy.66 = bf16[512,576]{1,0:T(8,128)(2,1)} copy(bf16[512,576]{0,1:T(8,128)(2,1)} %pad_maximum_fusion.1) | data formatting | bytes 1179648 | tf_op jit(solution)/shard_map/concatenate | solution.py:45
  67.9 3.4 %all-to-all-done.2 = bf16[8,4,16,576]{3,2,1,0:T(8,128)(2,1)} async-done(((bf16[8,4,16,576]{3,2,1,0:T(8,128)(2,1)}), bf16[8,4,16,576]{3,2,1,0:T(8,128)(2,1)}, u32[]{:S(2)}, u32[]{:S(2)}) %all-to-all-start.2) | async-done | bytes 589856 | tf_op jit(solution)/shard_map/all_to_all | solution.py:77
  71.3 5.0 %all-to-all-start.1 = ((bf16[8,4,16,576]{3,2,1,0:T(8,128)(2,1)}), bf16[8,4,16,576]{3,2,1,0:T(8,128)(2,1)}, u32[]{:S(2)}, u32[]{:S(2)}) async-start(bf16[8,4,16,576]{3,2,1,0:T(8,128)(2,1)} %bitcast.129), calls=%async_computation.1 | async-start | bytes 1310720 | tf_op jit(solution)/shard_map/all_to_all | solution.py:77
  76.3 2.1 %fusion.23 = f32[128,8,512]{2,0,1:T(8,128)} fusion(bf16[128,8,512]{0,2,1:T(8,128)(2,1)S(1)} %fusion.4, bf16[512,576]{1,0:T(8,128)(2,1)S(1)} %bitcast.124), kind=kOutput, calls=%fused_computation.46 | convolution fusion | flops 536870912 | bytes 3670016 | tf_op jit(solution)/shard_map/thk,kc->thc/dot_general | solution.py:37
  79.7 4.6 %collective-permute-start.4 = (f32[4,16,576]{2,1,0:T(8,128)S(1)}, f32[4,16,576]{2,1,0:T(8,128)S(1)}, u32[]{:S(2)}, u32[]{:S(2)}) collective-permute-start(f32[4,16,576]{2,1,0:T(8,128)S(1)} %convert_reduce_fusion), channel_id=1, source_target_pairs={{32,0},{40,8},{48,16},{56,24},{64,32},{72,40},{80,48},{88,56},{96,... | collective-permute-start | bytes 442376 | tf_op jit(solution)/shard_map/ppermute | solution.py:14
  86.7 5.6 %collective-permute-done.4 = f32[4,16,576]{2,1,0:T(8,128)S(1)} collective-permute-done((f32[4,16,576]{2,1,0:T(8,128)S(1)}, f32[4,16,576]{2,1,0:T(8,128)S(1)}, u32[]{:S(2)}, u32[]{:S(2)}) %collective-permute-start.4) | collective-permute-done | bytes 147488 | tf_op jit(solution)/shard_map/ppermute | solution.py:14
  92.3 4.8 %collective-permute-start.5 = (f32[2,16,576]{2,1,0:T(8,128)S(1)}, f32[2,16,576]{2,1,0:T(8,128)S(1)}, u32[]{:S(2)}, u32[]{:S(2)}) collective-permute-start(f32[2,16,576]{2,1,0:T(8,128)S(1)} %slice.47), channel_id=1, source_target_pairs={{16,0},{24,8},{32,16},{40,24},{48,32},{56,40},{64,48},{72,56},{80,... | collective-permute-start | bytes 221192 | tf_op jit(solution)/shard_map/ppermute | solution.py:14
  97.1 2.3 %multiply_convert_fusion = bf16[128,8,512]{2,0,1:T(8,128)(2,1)S(1)} fusion(f32[128,8,512]{2,0,1:T(8,128)} %fusion.23, bf16[128,8,512]{0,2,1:T(8,128)(2,1)S(1)} %fusion, bf16[512,576]{1,0:T(8,128)(2,1)S(1)} %bitcast.118), kind=kOutput, calls=%fused_computation.14 | convolution fusion | flops 538443776 | bytes 4718592 | tf_op jit(solution)/shard_map/thk,kc->thc/dot_general | solution.py:37
  99.5 4.3 %collective-permute-start.6 = (f32[1,16,576]{2,1,0:T(8,128)S(1)}, f32[1,16,576]{2,1,0:T(8,128)S(1)}, u32[]{:S(2)}, u32[]{:S(2)}) collective-permute-start(f32[1,16,576]{2,1,0:T(8,128)S(1)} %slice.49), channel_id=1, source_target_pairs={{8,0},{16,8},{24,16},{32,24},{40,32},{48,40},{56,48},{64,56},{72,6... | collective-permute-start | bytes 110600 | tf_op jit(solution)/shard_map/ppermute | solution.py:14
  105.0 1.5 %copy.73 = bf16[128,8,512]{2,1,0:T(8,128)(2,1)} copy(bf16[128,8,512]{2,0,1:T(8,128)(2,1)S(1)} %multiply_convert_fusion) | data formatting | bytes 2097152
  (71 shorter events, 24.0 us)
Async XLA Ops:
  0.6 27.4 %copy-start.4 = (bf16[128,8,512]{2,1,0:T(8,128)(2,1)S(1)}, bf16[128,8,512]{2,1,0:T(8,128)(2,1)}, u32[]{:S(2)}) copy-start(bf16[128,8,512]{2,1,0:T(8,128)(2,1)} %param.11) | copy-start | bytes 3145732
  3.2 14.7 %collective-permute-start = (bf16[1,128,576]{2,1,0:T(8,128)(2,1)S(1)}, bf16[1,128,576]{2,1,0:T(8,128)(2,1)S(1)}, u32[]{:S(2)}, u32[]{:S(2)}) collective-permute-start(bf16[1,128,576]{2,1,0:T(8,128)(2,1)S(1)} %get-tuple-element.12), channel_id=1, source_target_pairs={{0,8},{8,16},{16,24},{24,32},{32,40},{40,48},{48,56},{56,64},{64,7... | collective-permute-start | bytes 442376 | tf_op jit(solution)/shard_map/ppermute | solution.py:14
  18.5 15.0 %collective-permute-start.3 = (bf16[2,16,576]{2,1,0:T(8,128)(2,1)}, bf16[2,16,576]{2,1,0:T(8,128)(2,1)S(1)}, u32[]{:S(2)}, u32[]{:S(2)}) collective-permute-start(bf16[2,16,576]{2,1,0:T(8,128)(2,1)} %fusion.27), channel_id=1, source_target_pairs={{0,32},{8,40},{16,48},{24,56},{32,64},{40,72},{48,80},{56,88},{64,... | collective-permute-start | bytes 110600 | tf_op jit(solution)/shard_map/ppermute | solution.py:14
  20.4 13.1 %collective-permute-start.2 = (bf16[2,16,576]{2,1,0:T(8,128)(2,1)}, bf16[2,16,576]{2,1,0:T(8,128)(2,1)}, u32[]{:S(2)}, u32[]{:S(2)}) collective-permute-start(bf16[2,16,576]{2,1,0:T(8,128)(2,1)} %fusion.27), channel_id=1, source_target_pairs={{0,48},{8,56},{16,64},{24,72},{32,80},{40,88},{48,96},{56,104},{64... | collective-permute-start | bytes 110600 | tf_op jit(solution)/shard_map/ppermute | solution.py:14
  24.1 7.6 %copy-start.5 = (bf16[128,8,512]{2,1,0:T(8,128)(2,1)S(1)}, bf16[128,8,512]{2,1,0:T(8,128)(2,1)}, u32[]{:S(2)}) copy-start(bf16[128,8,512]{2,1,0:T(8,128)(2,1)} %param.8) | copy-start | bytes 3145732
  24.1 17.0 %collective-permute-start.1 = (bf16[2,128,576]{2,1,0:T(8,128)(2,1)}, bf16[2,128,576]{2,1,0:T(8,128)(2,1)}, u32[]{:S(2)}, u32[]{:S(2)}) collective-permute-start(bf16[2,128,576]{2,1,0:T(8,128)(2,1)} %pad_maximum_fusion.3), channel_id=1, source_target_pairs={{0,16},{8,24},{16,32},{24,40},{32,48},{40,56},{48,64},{56,72},{64,... | collective-permute-start | bytes 884744 | tf_op jit(solution)/shard_map/ppermute | solution.py:14
  31.8 9.4 %copy-start.9 = (bf16[128,576]{1,0:T(8,128)(2,1)S(1)}, bf16[128,576]{1,0:T(8,128)(2,1)}, u32[]{:S(2)}) copy-start(bf16[128,576]{1,0:T(8,128)(2,1)} %get-tuple-element.13) | copy-start | bytes 442372
  35.2 14.8 %all-to-all-start = ((bf16[8,4,16,576]{3,2,1,0:T(8,128)(2,1)}), bf16[8,4,16,576]{3,2,1,0:T(8,128)(2,1)S(1)}, u32[]{:S(2)}, u32[]{:S(2)}) async-start(bf16[8,4,16,576]{3,2,1,0:T(8,128)(2,1)} %broadcast_in_dim.56), calls=%async_computation | async-start | bytes 1310720 | tf_op jit(solution)/shard_map/all_to_all | solution.py:90
  41.1 1.6 %copy-start.6 = (bf16[128,8,512]{0,2,1:T(8,128)(2,1)S(1)}, bf16[128,8,512]{0,2,1:T(8,128)(2,1)}, u32[]{:S(2)}) copy-start(bf16[128,8,512]{0,2,1:T(8,128)(2,1)} %copy.62) | copy-start | bytes 3145732
  41.1 1.6 %copy-start.10 = (pred[128,512]{0,1:T(8,128)(4,1)S(1)}, pred[128,512]{0,1:T(8,128)(4,1)}, u32[]{:S(2)}) copy-start(pred[128,512]{0,1:T(8,128)(4,1)} %get-tuple-element.17) | copy-start | bytes 196612
  41.2 1.6 %copy-start.11 = (f32[128,8]{0,1:T(8,128)S(1)}, f32[128,8]{0,1:T(8,128)}, u32[]{:S(2)}) copy-start(f32[128,8]{0,1:T(8,128)} %param.12) | copy-start | bytes 12292
  42.3 3.1 %copy-start.2 = (bf16[4,8,16,576]{3,2,0,1:T(8,128)(2,1)}, bf16[4,8,16,576]{3,2,0,1:T(8,128)(2,1)S(1)}, u32[]{:S(2)}) copy-start(bf16[4,8,16,576]{3,2,0,1:T(8,128)(2,1)S(1)} %pad_maximum_fusion) | copy-start | bytes 1769476
  50.1 0.8 copy-start
  50.1 1.5 %copy-start.7 = (bf16[128,8,512]{0,2,1:T(8,128)(2,1)S(1)}, bf16[128,8,512]{0,2,1:T(8,128)(2,1)}, u32[]{:S(2)}) copy-start(bf16[128,8,512]{0,2,1:T(8,128)(2,1)} %copy.62) | copy-start | bytes 3145732
  57.4 5.6 %copy-start.8 = (bf16[128,8,512]{0,2,1:T(8,128)(2,1)S(1)}, bf16[128,8,512]{0,2,1:T(8,128)(2,1)}, u32[]{:S(2)}) copy-start(bf16[128,8,512]{0,2,1:T(8,128)(2,1)} %copy.62) | copy-start | bytes 3145732
  57.4 14.0 %all-to-all-start.2 = ((bf16[8,4,16,576]{3,2,1,0:T(8,128)(2,1)}), bf16[8,4,16,576]{3,2,1,0:T(8,128)(2,1)}, u32[]{:S(2)}, u32[]{:S(2)}) async-start(bf16[8,4,16,576]{3,2,1,0:T(8,128)(2,1)} %bitcast.29), calls=%async_computation.2 | async-start | bytes 1310720 | tf_op jit(solution)/shard_map/all_to_all | solution.py:77
  64.9 11.4 %copy-start.3 = (bf16[4,8,16,576]{3,2,0,1:T(8,128)(2,1)S(1)}, bf16[4,8,16,576]{3,2,0,1:T(8,128)(2,1)}, u32[]{:S(2)}) copy-start(bf16[4,8,16,576]{3,2,0,1:T(8,128)(2,1)} %copy-done.2) | copy-start | bytes 1769476
  71.3 14.2 %all-to-all-start.1 = ((bf16[8,4,16,576]{3,2,1,0:T(8,128)(2,1)}), bf16[8,4,16,576]{3,2,1,0:T(8,128)(2,1)}, u32[]{:S(2)}, u32[]{:S(2)}) async-start(bf16[8,4,16,576]{3,2,1,0:T(8,128)(2,1)} %bitcast.129), calls=%async_computation.1 | async-start | bytes 1310720 | tf_op jit(solution)/shard_map/all_to_all | solution.py:77
  78.4 18.7 %copy-start.1 = (bf16[8,4,16,576]{3,2,1,0:T(8,128)(2,1)S(1)}, bf16[8,4,16,576]{3,2,1,0:T(8,128)(2,1)}, u32[]{:S(2)}) copy-start(bf16[8,4,16,576]{3,2,1,0:T(8,128)(2,1)} %copy-done) | copy-start | bytes 1769476
  79.7 12.6 %collective-permute-start.4 = (f32[4,16,576]{2,1,0:T(8,128)S(1)}, f32[4,16,576]{2,1,0:T(8,128)S(1)}, u32[]{:S(2)}, u32[]{:S(2)}) collective-permute-start(f32[4,16,576]{2,1,0:T(8,128)S(1)} %convert_reduce_fusion), channel_id=1, source_target_pairs={{32,0},{40,8},{48,16},{56,24},{64,32},{72,40},{80,48},{88,56},{96,... | collective-permute-start | bytes 442376 | tf_op jit(solution)/shard_map/ppermute | solution.py:14
  92.3 7.1 %collective-permute-start.5 = (f32[2,16,576]{2,1,0:T(8,128)S(1)}, f32[2,16,576]{2,1,0:T(8,128)S(1)}, u32[]{:S(2)}, u32[]{:S(2)}) collective-permute-start(f32[2,16,576]{2,1,0:T(8,128)S(1)} %slice.47), channel_id=1, source_target_pairs={{16,0},{24,8},{32,16},{40,24},{48,32},{56,40},{64,48},{72,56},{80,... | collective-permute-start | bytes 221192 | tf_op jit(solution)/shard_map/ppermute | solution.py:14
  99.5 7.0 %collective-permute-start.6 = (f32[1,16,576]{2,1,0:T(8,128)S(1)}, f32[1,16,576]{2,1,0:T(8,128)S(1)}, u32[]{:S(2)}, u32[]{:S(2)}) collective-permute-start(f32[1,16,576]{2,1,0:T(8,128)S(1)} %slice.49), channel_id=1, source_target_pairs={{8,0},{16,8},{24,16},{32,24},{40,32},{48,40},{56,48},{64,56},{72,6... | collective-permute-start | bytes 110600 | tf_op jit(solution)/shard_map/ppermute | solution.py:14

commit v9 on v8

--- a/solution.py
+++ b/solution.py
@@ -97,9 +97,15 @@
     grad_qlat = softmax_scale * (near_qlat + far_qlat)
     grad_qrot = softmax_scale * (near_qrot + far_qrot)
 
-    far_sum = shifted(group_sum(far_part), "ctx", -half_span)
-    part = group_sum(near_part) + far_sum
-    width = half_span
+    part = jnp.concatenate(
+        [
+            far_part.reshape(groups, half_span, block, lat_width + rope_width),
+            near_part.reshape(groups, half_span, block, lat_width + rope_width),
+        ],
+        axis=1,
+    ).astype(jnp.bfloat16)
+    part = lax.all_to_all(part, "head", 0, 0, tiled=True).astype(jnp.float32).sum(axis=0)
+    width = span
     while width > 1:
         half = width // 2
         part = part[half:] + shifted(part[:half], "ctx", -half)

time: 109 us -> 113 us (1.037)
  waiting for transfers between devices: 23.8 us -> 32.6 us
  matrix products: 17.3 us -> 13.5 us
    all_to_all x2 -> x1, waiting for transfers between devices: 3.43 us -> 13.7 us  [local(): lax.all_to_all(part, 'head', 0, 0, tiled=True).astype(jnp.float32)]
    ppermute x7, starting transfers between devices: 24.4 us -> 30 us  [shifted(): return lax.ppermute(x, axis, pairs)]
    all_to_all x2 -> x1, starting transfers between devices: 10.1 us -> 5.03 us  [local(): lax.all_to_all(part, 'head', 0, 0, tiled=True).astype(jnp.float32)]
    all_to_all x1, waiting for transfers between devices: 3.87 us -> 0.7 us  [assemble(): return lax.all_to_all(spread, 'head', 0, 0, tiled=True)]
    concatenate x0 -> x1, other arithmetic: none -> 2.61 us  [local(): jnp.concatenate([far_part.reshape(groups, half_span, block, lat_width + r...]
    ppermute x7, waiting for transfers between devices: 16.5 us -> 18.2 us  [shifted(): return lax.ppermute(x, axis, pairs)]
    dot_general x2, matrix products: 4.41 us -> 2.82 us  [window_terms(): jnp.einsum('thk,kc->thc', grad_b, lat_all, preferred_element_type=jnp.flo...]
    dot_general x2, matrix products: 2.71 us -> 1.49 us  [window_terms(): jnp.einsum('thk,thc->kc', grad_b, q_latent, preferred_element_type=jnp.fl...]
  transfers between devices with their start and end apart: 10 -> 9, of which waited for: 4 -> 5; matrix products, arithmetic and copies ran while one was open for 29% -> 20% of each run, Pallas kernels for 0% -> 0%
where the time goes in v9:
time: 113 us; the launch traced here: 112 us
  starting transfers between devices  41 us (36%)
  waiting for transfers between devices  32.6 us (29%)
  matrix products  13.5 us (12%)
  local copies, waits for them, and re-layouts  13.1 us (12%)
  other arithmetic  10.6 us (9%)
    ppermute x7, starting transfers between devices, shifted(): return lax.ppermute(x, axis, pairs)  30 us
    ppermute x7, waiting for transfers between devices, shifted(): return lax.ppermute(x, axis, pairs)  18.2 us
    all_to_all x1, waiting for transfers between devices, local(): lax.all_to_all(part, 'head', 0, 0, tiled=True).astype(jnp.float32)  13.7 us
    unnamed x28, local copies, waits for them, and re-layouts  7.44 us
    all_to_all x1, starting transfers between devices, assemble(): return lax.all_to_all(spread, 'head', 0, 0, tiled=True)  5.93 us
    all_to_all x1, starting transfers between devices, local(): lax.all_to_all(part, 'head', 0, 0, tiled=True).astype(jnp.float32)  5.03 us
    concatenate x2, local copies, waits for them, and re-layouts, window_terms(): return (grad_qlat, grad_qrot, jnp.concatenate([grad_lat, grad_rot], axis=1))  3.22 us
    dot_general x2, matrix products, window_terms(): jnp.einsum('thk,kc->thc', grad_b, lat_all, preferred_element_type=jnp.flo...  2.82 us
  transfers between devices with their start and end apart: 9, of which 5 were waited for; matrix products, arithmetic and copies ran while one was open for 20% of the time, Pallas kernels for 0%

profile of v9, /device:TPU:6, one launch (start us, length us, event | category | flops | bytes accessed | tf_op | source)
XLA Modules:
  0.0 111.9 jit_solution(38225411442452457)
XLA Ops:
  2.5 1.9 %collective-permute-start = (bf16[1,128,576]{2,1,0:T(8,128)(2,1)S(1)}, bf16[1,128,576]{2,1,0:T(8,128)(2,1)S(1)}, u32[]{:S(2)}, u32[]{:S(2)}) collective-permute-start(bf16[1,128,576]{2,1,0:T(8,128)(2,1)S(1)} %get-tuple-element.12), channel_id=1, source_target_pairs={{0,8},{8,16},{16,24},{24,32},{32,40},{40,48},{48,56},{56,64},{64,7... | collective-permute-start | bytes 442376 | tf_op jit(solution)/shard_map/ppermute | solution.py:14
  5.7 11.5 %collective-permute-done = bf16[1,128,576]{2,1,0:T(8,128)(2,1)S(1)} collective-permute-done((bf16[1,128,576]{2,1,0:T(8,128)(2,1)S(1)}, bf16[1,128,576]{2,1,0:T(8,128)(2,1)S(1)}, u32[]{:S(2)}, u32[]{:S(2)}) %collective-permute-start) | collective-permute-done | bytes 147488 | tf_op jit(solution)/shard_map/ppermute | solution.py:14
  17.2 1.9 %collective-permute-start.3 = (bf16[2,16,576]{2,1,0:T(8,128)(2,1)S(1)}, bf16[2,16,576]{2,1,0:T(8,128)(2,1)S(1)}, u32[]{:S(2)}, u32[]{:S(2)}) collective-permute-start(bf16[2,16,576]{2,1,0:T(8,128)(2,1)S(1)} %fusion.27), channel_id=1, source_target_pairs={{0,32},{8,40},{16,48},{24,56},{32,64},{40,72},{48,80},{56,88},{64,... | collective-permute-start | bytes 110600 | tf_op jit(solution)/shard_map/ppermute | solution.py:14
  19.1 3.0 %collective-permute-start.2 = (bf16[2,16,576]{2,1,0:T(8,128)(2,1)S(1)}, bf16[2,16,576]{2,1,0:T(8,128)(2,1)S(1)}, u32[]{:S(2)}, u32[]{:S(2)}) collective-permute-start(bf16[2,16,576]{2,1,0:T(8,128)(2,1)S(1)} %fusion.27), channel_id=1, source_target_pairs={{0,48},{8,56},{16,64},{24,72},{32,80},{40,88},{48,96},{56,104},{64... | collective-permute-start | bytes 110600 | tf_op jit(solution)/shard_map/ppermute | solution.py:14
  22.9 3.9 %collective-permute-start.1 = (bf16[2,128,576]{2,1,0:T(8,128)(2,1)}, bf16[2,128,576]{2,1,0:T(8,128)(2,1)}, u32[]{:S(2)}, u32[]{:S(2)}) collective-permute-start(bf16[2,128,576]{2,1,0:T(8,128)(2,1)} %pad_maximum_fusion.4), channel_id=1, source_target_pairs={{0,16},{8,24},{16,32},{24,40},{32,48},{40,56},{48,64},{56,72},{64,... | collective-permute-start | bytes 884744 | tf_op jit(solution)/shard_map/ppermute | solution.py:14
  26.8 1.6 %fusion.5 = f32[128,8]{1,0:T(8,128)S(1)} fusion(bf16[128,8,512]{2,1,0:T(8,128)(2,1)S(1)} %copy-done.5, bf16[128,8,512]{2,1,0:T(8,128)(2,1)} %param.10), kind=kLoop, calls=%fused_computation.10 | loop fusion | flops 2096128 | bytes 2101248
  29.6 1.9 %copy.62 = bf16[128,8,512]{0,2,1:T(8,128)(2,1)S(1)} copy(bf16[128,8,512]{2,1,0:T(8,128)(2,1)} %param.8) | data formatting | bytes 2097152 | tf_op args[0]
  32.6 5.9 %all-to-all-start = ((bf16[8,4,16,576]{3,2,1,0:T(8,128)(2,1)}), bf16[8,4,16,576]{3,2,1,0:T(8,128)(2,1)S(1)}, u32[]{:S(2)}, u32[]{:S(2)}) async-start(bf16[8,4,16,576]{3,2,1,0:T(8,128)(2,1)} %broadcast_in_dim.56), calls=%async_computation | async-start | bytes 1310720 | tf_op jit(solution)/shard_map/all_to_all | solution.py:90
  38.6 1.0 pad_maximum_fusion.1
  44.6 2.1 %copy.72 = bf16[512,576]{1,0:T(8,128)(2,1)} copy(bf16[512,576]{0,1:T(8,128)(2,1)} %pad_maximum_fusion.3) | data formatting | bytes 1179648 | tf_op jit(solution)/shard_map/concatenate | solution.py:45
  49.9 1.8 %fusion = bf16[128,8,512]{0,2,1:T(8,128)(2,1)S(1)} fusion(f32[128,8,512]{0,2,1:T(8,128)S(1)} %fusion.3, bf16[128,8,512]{0,2,1:T(8,128)(2,1)S(1)} %copy.64, f32[128,8]{0,1:T(8,128)S(1)} %copy.80, bf16[512,576]{1,0:T(8,128)(2,1)} %bitcast.117), kind=kOutput, calls=%fused_computation.2 | convolution fusion | flops 538443776 | bytes 4722688 | tf_op jit(solution)/shard_map/thc,kc->thk/dot_general | solution.py:33
  53.7 1.1 copy.66
  54.8 2.6 %pad_maximum_fusion = bf16[8,8,16,576]{3,2,1,0:T(8,128)(2,1)} fusion(bf16[8,4,16,576]{3,2,1,0:T(8,128)(2,1)} %bitcast.129, bf16[8,4,16,576]{3,2,1,0:T(8,128)(2,1)} %bitcast.130), kind=kLoop, calls=%fused_computation.24 | loop fusion | flops 589824 | bytes 2359296 | tf_op jit(solution)/shard_map/concatenate | solution.py:100
  57.4 5.0 %all-to-all-start.1 = ((bf16[8,8,16,576]{3,2,1,0:T(8,128)(2,1)}), bf16[8,8,16,576]{3,2,1,0:T(8,128)(2,1)}, u32[]{:S(2)}, u32[]{:S(2)}) async-start(bf16[8,8,16,576]{3,2,1,0:T(8,128)(2,1)} %pad_maximum_fusion), calls=%async_computation.1 | async-start | bytes 2621440 | tf_op jit(solution)/shard_map/all_to_all | solution.py:107
  62.4 2.1 %fusion.23 = f32[128,8,512]{2,0,1:T(8,128)} fusion(bf16[128,8,512]{0,2,1:T(8,128)(2,1)S(1)} %fusion.4, bf16[512,576]{1,0:T(8,128)(2,1)S(1)} %bitcast.124), kind=kOutput, calls=%fused_computation.46 | convolution fusion | flops 536870912 | bytes 3670016 | tf_op jit(solution)/shard_map/thk,kc->thc/dot_general | solution.py:37
  64.5 13.7 %all-to-all-done.1 = bf16[8,8,16,576]{3,2,1,0:T(8,128)(2,1)} async-done(((bf16[8,8,16,576]{3,2,1,0:T(8,128)(2,1)}), bf16[8,8,16,576]{3,2,1,0:T(8,128)(2,1)}, u32[]{:S(2)}, u32[]{:S(2)}) %all-to-all-start.1) | async-done | bytes 1179680 | tf_op jit(solution)/shard_map/all_to_all | solution.py:107
  78.2 1.7 %convert_reduce_fusion = f32[8,16,576]{2,1,0:T(8,128)S(1)} fusion(bf16[8,8,16,576]{3,2,1,0:T(8,128)(2,1)} %all-to-all-done.1), kind=kLoop, calls=%fused_computation | loop fusion | flops 1105920 | bytes 1474560 | tf_op jit(solution)/shard_map/reduce_sum | solution.py:107
  79.9 4.8 %collective-permute-start.4 = (f32[4,16,576]{2,1,0:T(8,128)S(1)}, f32[4,16,576]{2,1,0:T(8,128)S(1)}, u32[]{:S(2)}, u32[]{:S(2)}) collective-permute-start(f32[4,16,576]{2,1,0:T(8,128)S(1)} %slice.55), channel_id=1, source_target_pairs={{32,0},{40,8},{48,16},{56,24},{64,32},{72,40},{80,48},{88,56},{96,... | collective-permute-start | bytes 442376 | tf_op jit(solution)/shard_map/ppermute | solution.py:14
  84.7 1.2 %fusion.24 = f32[128,8,64]{0,2,1:T(8,128)S(1)} fusion(bf16[128,8,512]{0,2,1:T(8,128)(2,1)S(1)} %fusion.4, bf16[512,576]{1,0:T(8,128)(2,1)} %bitcast.123), kind=kOutput, calls=%fused_computation.53 | convolution fusion | flops 67108864 | bytes 1441792 | tf_op jit(solution)/shard_map/thk,kr->thr/dot_general | solution.py:38
  86.0 5.4 %collective-permute-done.4 = f32[4,16,576]{2,1,0:T(8,128)S(1)} collective-permute-done((f32[4,16,576]{2,1,0:T(8,128)S(1)}, f32[4,16,576]{2,1,0:T(8,128)S(1)}, u32[]{:S(2)}, u32[]{:S(2)}) %collective-permute-start.4) | collective-permute-done | bytes 147488 | tf_op jit(solution)/shard_map/ppermute | solution.py:14
  91.5 8.2 %collective-permute-start.5 = (f32[2,16,576]{2,1,0:T(8,128)S(1)}, f32[2,16,576]{2,1,0:T(8,128)S(1)}, u32[]{:S(2)}, u32[]{:S(2)}) collective-permute-start(f32[2,16,576]{2,1,0:T(8,128)S(1)} %slice.57), channel_id=1, source_target_pairs={{16,0},{24,8},{32,16},{40,24},{48,32},{56,40},{64,48},{72,56},{80,... | collective-permute-start | bytes 221192 | tf_op jit(solution)/shard_map/ppermute | solution.py:14
  100.4 1.3 %collective-permute-done.5 = f32[2,16,576]{2,1,0:T(8,128)S(1)} collective-permute-done((f32[2,16,576]{2,1,0:T(8,128)S(1)}, f32[2,16,576]{2,1,0:T(8,128)S(1)}, u32[]{:S(2)}, u32[]{:S(2)}) %collective-permute-start.5) | collective-permute-done | bytes 73760 | tf_op jit(solution)/shard_map/ppermute | solution.py:14
  101.7 6.3 %collective-permute-start.6 = (f32[1,16,576]{2,1,0:T(8,128)S(1)}, f32[1,16,576]{2,1,0:T(8,128)S(1)}, u32[]{:S(2)}, u32[]{:S(2)}) collective-permute-start(f32[1,16,576]{2,1,0:T(8,128)S(1)} %slice.59), channel_id=1, source_target_pairs={{8,0},{16,8},{24,16},{32,24},{40,32},{48,40},{56,48},{64,56},{72,6... | collective-permute-start | bytes 110600 | tf_op jit(solution)/shard_map/ppermute | solution.py:14
  109.1 1.5 %copy.73 = bf16[128,8,512]{2,1,0:T(8,128)(2,1)} copy(bf16[128,8,512]{2,0,1:T(8,128)(2,1)S(1)} %multiply_convert_fusion) | data formatting | bytes 2097152
  (68 shorter events, 19.2 us)
Async XLA Ops:
  0.6 26.2 %copy-start.5 = (bf16[128,8,512]{2,1,0:T(8,128)(2,1)S(1)}, bf16[128,8,512]{2,1,0:T(8,128)(2,1)}, u32[]{:S(2)}) copy-start(bf16[128,8,512]{2,1,0:T(8,128)(2,1)} %param.11) | copy-start | bytes 3145732
  2.5 14.7 %collective-permute-start = (bf16[1,128,576]{2,1,0:T(8,128)(2,1)S(1)}, bf16[1,128,576]{2,1,0:T(8,128)(2,1)S(1)}, u32[]{:S(2)}, u32[]{:S(2)}) collective-permute-start(bf16[1,128,576]{2,1,0:T(8,128)(2,1)S(1)} %get-tuple-element.12), channel_id=1, source_target_pairs={{0,8},{8,16},{16,24},{24,32},{32,40},{40,48},{48,56},{56,64},{64,7... | collective-permute-start | bytes 442376 | tf_op jit(solution)/shard_map/ppermute | solution.py:14
  17.2 14.4 %collective-permute-start.3 = (bf16[2,16,576]{2,1,0:T(8,128)(2,1)S(1)}, bf16[2,16,576]{2,1,0:T(8,128)(2,1)S(1)}, u32[]{:S(2)}, u32[]{:S(2)}) collective-permute-start(bf16[2,16,576]{2,1,0:T(8,128)(2,1)S(1)} %fusion.27), channel_id=1, source_target_pairs={{0,32},{8,40},{16,48},{24,56},{32,64},{40,72},{48,80},{56,88},{64,... | collective-permute-start | bytes 110600 | tf_op jit(solution)/shard_map/ppermute | solution.py:14
  19.1 12.5 %collective-permute-start.2 = (bf16[2,16,576]{2,1,0:T(8,128)(2,1)S(1)}, bf16[2,16,576]{2,1,0:T(8,128)(2,1)S(1)}, u32[]{:S(2)}, u32[]{:S(2)}) collective-permute-start(bf16[2,16,576]{2,1,0:T(8,128)(2,1)S(1)} %fusion.27), channel_id=1, source_target_pairs={{0,48},{8,56},{16,64},{24,72},{32,80},{40,88},{48,96},{56,104},{64... | collective-permute-start | bytes 110600 | tf_op jit(solution)/shard_map/ppermute | solution.py:14
  22.9 6.6 %copy-start.9 = (bf16[128,512]{1,0:T(8,128)(2,1)S(1)}, bf16[128,512]{1,0:T(8,128)(2,1)}, u32[]{:S(2)}) copy-start(bf16[128,512]{1,0:T(8,128)(2,1)} %param.9) | copy-start | bytes 393220
  22.9 15.7 %collective-permute-start.1 = (bf16[2,128,576]{2,1,0:T(8,128)(2,1)}, bf16[2,128,576]{2,1,0:T(8,128)(2,1)}, u32[]{:S(2)}, u32[]{:S(2)}) collective-permute-start(bf16[2,128,576]{2,1,0:T(8,128)(2,1)} %pad_maximum_fusion.4), channel_id=1, source_target_pairs={{0,16},{8,24},{16,32},{24,40},{32,48},{40,56},{48,64},{56,72},{64,... | collective-permute-start | bytes 884744 | tf_op jit(solution)/shard_map/ppermute | solution.py:14
  31.6 8.5 %copy-start.6 = (bf16[128,8,512]{0,2,1:T(8,128)(2,1)}, bf16[128,8,512]{0,2,1:T(8,128)(2,1)S(1)}, u32[]{:S(2)}) copy-start(bf16[128,8,512]{0,2,1:T(8,128)(2,1)S(1)} %copy.62) | copy-start | bytes 3145732
  32.6 14.8 %all-to-all-start = ((bf16[8,4,16,576]{3,2,1,0:T(8,128)(2,1)}), bf16[8,4,16,576]{3,2,1,0:T(8,128)(2,1)S(1)}, u32[]{:S(2)}, u32[]{:S(2)}) async-start(bf16[8,4,16,576]{3,2,1,0:T(8,128)(2,1)} %broadcast_in_dim.56), calls=%async_computation | async-start | bytes 1310720 | tf_op jit(solution)/shard_map/all_to_all | solution.py:90
  38.6 1.5 %copy-start.10 = (f32[128,8]{0,1:T(8,128)S(1)}, f32[128,8]{0,1:T(8,128)}, u32[]{:S(2)}) copy-start(f32[128,8]{0,1:T(8,128)} %param.12) | copy-start | bytes 12292
  39.6 2.2 %copy-start.3 = (bf16[4,8,16,576]{3,2,0,1:T(8,128)(2,1)}, bf16[4,8,16,576]{3,2,0,1:T(8,128)(2,1)S(1)}, u32[]{:S(2)}) copy-start(bf16[4,8,16,576]{3,2,0,1:T(8,128)(2,1)S(1)} %pad_maximum_fusion.1) | copy-start | bytes 1769476
  41.8 1.2 %copy-start.7 = (bf16[128,8,512]{0,2,1:T(8,128)(2,1)S(1)}, bf16[128,8,512]{0,2,1:T(8,128)(2,1)}, u32[]{:S(2)}) copy-start(bf16[128,8,512]{0,2,1:T(8,128)(2,1)} %copy-done.6) | copy-start | bytes 3145732
  47.5 0.8 copy-start.1
  47.5 1.5 %copy-start.8 = (bf16[128,8,512]{0,2,1:T(8,128)(2,1)S(1)}, bf16[128,8,512]{0,2,1:T(8,128)(2,1)}, u32[]{:S(2)}) copy-start(bf16[128,8,512]{0,2,1:T(8,128)(2,1)} %copy-done.6) | copy-start | bytes 3145732
  54.8 7.6 %copy-start.4 = (bf16[4,8,16,576]{3,2,0,1:T(8,128)(2,1)S(1)}, bf16[4,8,16,576]{3,2,0,1:T(8,128)(2,1)}, u32[]{:S(2)}) copy-start(bf16[4,8,16,576]{3,2,0,1:T(8,128)(2,1)} %copy-done.3) | copy-start | bytes 1769476
  57.4 20.8 %all-to-all-start.1 = ((bf16[8,8,16,576]{3,2,1,0:T(8,128)(2,1)}), bf16[8,8,16,576]{3,2,1,0:T(8,128)(2,1)}, u32[]{:S(2)}, u32[]{:S(2)}) async-start(bf16[8,8,16,576]{3,2,1,0:T(8,128)(2,1)} %pad_maximum_fusion), calls=%async_computation.1 | async-start | bytes 2621440 | tf_op jit(solution)/shard_map/all_to_all | solution.py:107
  64.5 35.2 %copy-start.2 = (bf16[8,4,16,576]{3,2,1,0:T(8,128)(2,1)S(1)}, bf16[8,4,16,576]{3,2,1,0:T(8,128)(2,1)}, u32[]{:S(2)}) copy-start(bf16[8,4,16,576]{3,2,1,0:T(8,128)(2,1)} %copy-done.1) | copy-start | bytes 1769476
  78.2 21.5 %copy-start = (f32[128,8,512]{2,0,1:T(8,128)S(1)}, f32[128,8,512]{2,0,1:T(8,128)}, u32[]{:S(2)}) copy-start(f32[128,8,512]{2,0,1:T(8,128)} %fusion.23) | copy-start | bytes 6291460
  79.9 11.5 %collective-permute-start.4 = (f32[4,16,576]{2,1,0:T(8,128)S(1)}, f32[4,16,576]{2,1,0:T(8,128)S(1)}, u32[]{:S(2)}, u32[]{:S(2)}) collective-permute-start(f32[4,16,576]{2,1,0:T(8,128)S(1)} %slice.55), channel_id=1, source_target_pairs={{32,0},{40,8},{48,16},{56,24},{64,32},{72,40},{80,48},{88,56},{96,... | collective-permute-start | bytes 442376 | tf_op jit(solution)/shard_map/ppermute | solution.py:14
  91.5 10.2 %collective-permute-start.5 = (f32[2,16,576]{2,1,0:T(8,128)S(1)}, f32[2,16,576]{2,1,0:T(8,128)S(1)}, u32[]{:S(2)}, u32[]{:S(2)}) collective-permute-start(f32[2,16,576]{2,1,0:T(8,128)S(1)} %slice.57), channel_id=1, source_target_pairs={{16,0},{24,8},{32,16},{40,24},{48,32},{56,40},{64,48},{72,56},{80,... | collective-permute-start | bytes 221192 | tf_op jit(solution)/shard_map/ppermute | solution.py:14
  101.7 9.0 %collective-permute-start.6 = (f32[1,16,576]{2,1,0:T(8,128)S(1)}, f32[1,16,576]{2,1,0:T(8,128)S(1)}, u32[]{:S(2)}, u32[]{:S(2)}) collective-permute-start(f32[1,16,576]{2,1,0:T(8,128)S(1)} %slice.59), channel_id=1, source_target_pairs={{8,0},{16,8},{24,16},{32,24},{40,32},{48,40},{56,48},{64,56},{72,6... | collective-permute-start | bytes 110600 | tf_op jit(solution)/shard_map/ppermute | solution.py:14

commit v10 on v8

--- a/solution.py
+++ b/solution.py
@@ -97,19 +97,21 @@
     grad_qlat = softmax_scale * (near_qlat + far_qlat)
     grad_qrot = softmax_scale * (near_qrot + far_qrot)
 
-    far_sum = shifted(group_sum(far_part), "ctx", -half_span)
+    far_sum = group_sum(far_part)
+    near_part, far_sum = lax.optimization_barrier((near_part, far_sum))
+    far_sum = shifted(far_sum, "ctx", -half_span)
     part = group_sum(near_part) + far_sum
     width = half_span
-    while width > 1:
+    while width > 2:
         half = width // 2
         part = part[half:] + shifted(part[:half], "ctx", -half)
         width = half
-    owned = part[0]
+    last = shifted(part[0], "ctx", -1)
     return (
         grad_qlat.astype(jnp.bfloat16),
         grad_qrot.reshape(tok_rows, head_count * rope_width).astype(jnp.bfloat16),
-        owned[:, :lat_width].astype(jnp.bfloat16),
-        owned[:, lat_width:].astype(jnp.bfloat16),
+        (part[1, :, :lat_width] + last[:, :lat_width]).astype(jnp.bfloat16),
+        (part[1, :, lat_width:] + last[:, lat_width:]).astype(jnp.bfloat16),
     )
 
 

time: 109 us -> 111 us (1.018)
  waiting for transfers between devices: 23.8 us -> 25.9 us
  other arithmetic: 11.5 us -> 12.7 us
  local copies, waits for them, and re-layouts: 13.7 us -> 12.5 us
    all_to_all x2, waiting for transfers between devices: 3.43 us -> 5.89 us  [group_sum(): got = lax.all_to_all(part, 'head', 0, 0, tiled=True)]
    concatenate x2 -> x1, local copies, waits for them, and re-layouts: 3.26 us -> 1.08 us  [window_terms(): return (grad_qlat, grad_qrot, jnp.concatenate([grad_lat, grad_rot], axis=1))]
    convert_element_type x0 -> x1, local copies, waits for them, and re-layouts: none -> 2.14 us  [group_sum(): part = part.astype(jnp.bfloat16)]
    convert_element_type x0 -> x2, other arithmetic: none -> 1.21 us  [the longest x1 0.61 us: local(): (part[1, :, :lat_width] + last[:, :lat_width]).astype(jnp.bfloat16)]
    slice x2 -> x0, local copies, waits for them, and re-layouts: 1.2 us -> none  [the longest x1 0.61 us: local(): owned[:, :lat_width].astype(jnp.bfloat16)]
  transfers between devices with their start and end apart: 10 -> 10, of which waited for: 4 -> 5; matrix products, arithmetic and copies ran while one was open for 29% -> 25% of each run, Pallas kernels for 0% -> 0%
where the time goes in v10:
time: 111 us; the launch traced here: 110 us
  starting transfers between devices  40.3 us (36%)
  waiting for transfers between devices  25.9 us (23%)
  matrix products  17.3 us (16%)
  other arithmetic  12.7 us (11%)
  local copies, waits for them, and re-layouts  12.5 us (11%)
    ppermute x7, starting transfers between devices, shifted(): return lax.ppermute(x, axis, pairs)  24.3 us
    ppermute x7, waiting for transfers between devices, shifted(): return lax.ppermute(x, axis, pairs)  16.1 us
    all_to_all x2, starting transfers between devices, group_sum(): got = lax.all_to_all(part, 'head', 0, 0, tiled=True)  10.1 us
    unnamed x30, local copies, waits for them, and re-layouts  8.06 us
    all_to_all x1, starting transfers between devices, assemble(): return lax.all_to_all(spread, 'head', 0, 0, tiled=True)  5.93 us
    all_to_all x2, waiting for transfers between devices, group_sum(): got = lax.all_to_all(part, 'head', 0, 0, tiled=True)  5.89 us
    dot_general x2, matrix products, window_terms(): jnp.einsum('thk,kc->thc', grad_b, lat_all, preferred_element_type=jnp.flo...  4.41 us
    all_to_all x1, waiting for transfers between devices, assemble(): return lax.all_to_all(spread, 'head', 0, 0, tiled=True)  3.87 us
  transfers between devices with their start and end apart: 10, of which 5 were waited for; matrix products, arithmetic and copies ran while one was open for 25% of the time, Pallas kernels for 0%

profile of v10, /device:TPU:6, one launch (start us, length us, event | category | flops | bytes accessed | tf_op | source)
XLA Modules:
  0.0 109.6 jit_solution(2528374310340948210)
XLA Ops:
  1.6 1.6 %fusion.30 = (bf16[1,128,576]{2,1,0:T(8,128)(2,1)S(1)}, bf16[128,576]{1,0:T(8,128)(2,1)}) fusion(bf16[128,64]{1,0:T(8,128)(2,1)S(1)} %copy.44, bf16[128,512]{1,0:T(8,128)(2,1)} %param.13), kind=kLoop, calls=%fused_computation.70 | loop fusion | flops 294912 | bytes 442368 | tf_op jit(solution)/shard_map/broadcast_in_dim | solution.py:80
  3.2 1.9 %collective-permute-start = (bf16[1,128,576]{2,1,0:T(8,128)(2,1)S(1)}, bf16[1,128,576]{2,1,0:T(8,128)(2,1)S(1)}, u32[]{:S(2)}, u32[]{:S(2)}) collective-permute-start(bf16[1,128,576]{2,1,0:T(8,128)(2,1)S(1)} %get-tuple-element.16), channel_id=1, source_target_pairs={{0,8},{8,16},{16,24},{24,32},{32,40},{40,48},{48,56},{56,64},{64,7... | collective-permute-start | bytes 442376 | tf_op jit(solution)/shard_map/ppermute | solution.py:14
  6.9 10.9 %collective-permute-done = bf16[1,128,576]{2,1,0:T(8,128)(2,1)S(1)} collective-permute-done((bf16[1,128,576]{2,1,0:T(8,128)(2,1)S(1)}, bf16[1,128,576]{2,1,0:T(8,128)(2,1)S(1)}, u32[]{:S(2)}, u32[]{:S(2)}) %collective-permute-start) | collective-permute-done | bytes 147488 | tf_op jit(solution)/shard_map/ppermute | solution.py:14
  18.5 1.9 %collective-permute-start.3 = (bf16[2,16,576]{2,1,0:T(8,128)(2,1)}, bf16[2,16,576]{2,1,0:T(8,128)(2,1)S(1)}, u32[]{:S(2)}, u32[]{:S(2)}) collective-permute-start(bf16[2,16,576]{2,1,0:T(8,128)(2,1)} %fusion.25), channel_id=1, source_target_pairs={{0,32},{8,40},{16,48},{24,56},{32,64},{40,72},{48,80},{56,88},{64,... | collective-permute-start | bytes 110600 | tf_op jit(solution)/shard_map/ppermute | solution.py:14
  20.4 3.0 %collective-permute-start.2 = (bf16[2,16,576]{2,1,0:T(8,128)(2,1)}, bf16[2,16,576]{2,1,0:T(8,128)(2,1)}, u32[]{:S(2)}, u32[]{:S(2)}) collective-permute-start(bf16[2,16,576]{2,1,0:T(8,128)(2,1)} %fusion.25), channel_id=1, source_target_pairs={{0,48},{8,56},{16,64},{24,72},{32,80},{40,88},{48,96},{56,104},{64... | collective-permute-start | bytes 110600 | tf_op jit(solution)/shard_map/ppermute | solution.py:14
  24.1 3.9 %collective-permute-start.1 = (bf16[2,128,576]{2,1,0:T(8,128)(2,1)}, bf16[2,128,576]{2,1,0:T(8,128)(2,1)}, u32[]{:S(2)}, u32[]{:S(2)}) collective-permute-start(bf16[2,128,576]{2,1,0:T(8,128)(2,1)} %pad_maximum_fusion.3), channel_id=1, source_target_pairs={{0,16},{8,24},{16,32},{24,40},{32,48},{40,56},{48,64},{56,72},{64,... | collective-permute-start | bytes 884744 | tf_op jit(solution)/shard_map/ppermute | solution.py:14
  28.1 1.6 %fusion.5 = f32[128,8]{1,0:T(8,128)S(1)} fusion(bf16[128,8,512]{2,1,0:T(8,128)(2,1)S(1)} %copy-done.4, bf16[128,8,512]{2,1,0:T(8,128)(2,1)} %param.10), kind=kLoop, calls=%fused_computation.9 | loop fusion | flops 2096128 | bytes 2101248
  31.8 1.7 %copy.62 = bf16[128,8,512]{0,2,1:T(8,128)(2,1)} copy(bf16[128,8,512]{2,1,0:T(8,128)(2,1)S(1)} %copy-done.5) | data formatting | bytes 2097152 | tf_op args[0]
  35.2 5.9 %all-to-all-start = ((bf16[8,4,16,576]{3,2,1,0:T(8,128)(2,1)}), bf16[8,4,16,576]{3,2,1,0:T(8,128)(2,1)S(1)}, u32[]{:S(2)}, u32[]{:S(2)}) async-start(bf16[8,4,16,576]{3,2,1,0:T(8,128)(2,1)} %broadcast_in_dim.56), calls=%async_computation | async-start | bytes 1310720 | tf_op jit(solution)/shard_map/all_to_all | solution.py:90
  43.7 1.7 %convolution_bitcast_fusion.2 = f32[512,512]{0,1:T(8,128)} fusion(bf16[128,8,512]{0,2,1:T(8,128)(2,1)S(1)} %copy.64, f32[128,8,512]{0,2,1:T(8,128)S(1)} %fusion.8), kind=kOutput, calls=%fused_computation.19 | convolution fusion | flops 537395200 | bytes 4194304 | tf_op jit(solution)/shard_map/thk,thc->kc/dot_general | solution.py:41
  46.2 3.9 %all-to-all-done = bf16[8,4,16,576]{3,2,1,0:T(8,128)(2,1)S(1)} async-done(((bf16[8,4,16,576]{3,2,1,0:T(8,128)(2,1)}), bf16[8,4,16,576]{3,2,1,0:T(8,128)(2,1)S(1)}, u32[]{:S(2)}, u32[]{:S(2)}) %all-to-all-start) | async-done | bytes 589856 | tf_op jit(solution)/shard_map/all_to_all | solution.py:90
  52.5 1.8 %fusion = bf16[128,8,512]{0,2,1:T(8,128)(2,1)S(1)} fusion(f32[128,8,512]{0,2,1:T(8,128)S(1)} %fusion.3, bf16[128,8,512]{0,2,1:T(8,128)(2,1)S(1)} %copy.64, f32[128,8]{0,1:T(8,128)S(1)} %copy.80, bf16[512,576]{1,0:T(8,128)(2,1)} %bitcast.121), kind=kOutput, calls=%fused_computation.1 | convolution fusion | flops 538443776 | bytes 4722688 | tf_op jit(solution)/shard_map/thc,kc->thk/dot_general | solution.py:33
  57.3 5.1 %all-to-all-start.1 = ((bf16[8,4,16,576]{3,2,1,0:T(8,128)(2,1)}), bf16[8,4,16,576]{3,2,1,0:T(8,128)(2,1)}, u32[]{:S(2)}, u32[]{:S(2)}) async-start(bf16[8,4,16,576]{3,2,1,0:T(8,128)(2,1)} %bitcast.28), calls=%async_computation.1 | async-start | bytes 1310720 | tf_op jit(solution)/shard_map/all_to_all | solution.py:77
  62.9 2.0 %fusion.12 = bf16[512,512]{0,1:T(8,128)(2,1)S(1)} fusion(f32[512,512]{0,1:T(8,128)} %convolution_bitcast_fusion.2, bf16[128,8,512]{0,2,1:T(8,128)(2,1)S(1)} %fusion.4, bf16[128,8,512]{0,2,1:T(8,128)(2,1)S(1)} %copy-done.8), kind=kOutput, calls=%fused_computation.22 | convolution fusion | flops 537657344 | bytes 3670016 | tf_op jit(solution)/shard_map/thk,thc->kc/dot_general | solution.py:39
  65.7 5.6 %all-to-all-done.1 = bf16[8,4,16,576]{3,2,1,0:T(8,128)(2,1)} async-done(((bf16[8,4,16,576]{3,2,1,0:T(8,128)(2,1)}), bf16[8,4,16,576]{3,2,1,0:T(8,128)(2,1)}, u32[]{:S(2)}, u32[]{:S(2)}) %all-to-all-start.1) | async-done | bytes 589856 | tf_op jit(solution)/shard_map/all_to_all | solution.py:77
  72.5 2.1 %copy.72 = bf16[512,576]{1,0:T(8,128)(2,1)} copy(bf16[512,576]{0,1:T(8,128)(2,1)} %pad_maximum_fusion) | data formatting | bytes 1179648 | tf_op jit(solution)/shard_map/convert_element_type | solution.py:76
  74.7 5.0 %all-to-all-start.2 = ((bf16[8,4,16,576]{3,2,1,0:T(8,128)(2,1)}), bf16[8,4,16,576]{3,2,1,0:T(8,128)(2,1)}, u32[]{:S(2)}, u32[]{:S(2)}) async-start(bf16[8,4,16,576]{3,2,1,0:T(8,128)(2,1)} %bitcast.133), calls=%async_computation.2 | async-start | bytes 1310720 | tf_op jit(solution)/shard_map/all_to_all | solution.py:77
  79.6 2.1 %fusion.21 = f32[128,8,512]{2,0,1:T(8,128)} fusion(bf16[128,8,512]{0,2,1:T(8,128)(2,1)S(1)} %fusion.4, bf16[512,576]{1,0:T(8,128)(2,1)S(1)} %bitcast.128), kind=kOutput, calls=%fused_computation.44 | convolution fusion | flops 536870912 | bytes 3670016 | tf_op jit(solution)/shard_map/thk,kc->thc/dot_general | solution.py:37
  81.7 4.7 %collective-permute-start.4 = (f32[4,16,576]{2,1,0:T(8,128)S(1)}, f32[4,16,576]{2,1,0:T(8,128)S(1)}, u32[]{:S(2)}, u32[]{:S(2)}) collective-permute-start(f32[4,16,576]{2,1,0:T(8,128)S(1)} %convert_reduce_fusion.1), channel_id=1, source_target_pairs={{32,0},{40,8},{48,16},{56,24},{64,32},{72,40},{80,48},{88,56},{96,... | collective-permute-start | bytes 442376 | tf_op jit(solution)/shard_map/ppermute | solution.py:14
  89.2 5.2 %collective-permute-done.4 = f32[4,16,576]{2,1,0:T(8,128)S(1)} collective-permute-done((f32[4,16,576]{2,1,0:T(8,128)S(1)}, f32[4,16,576]{2,1,0:T(8,128)S(1)}, u32[]{:S(2)}, u32[]{:S(2)}) %collective-permute-start.4) | collective-permute-done | bytes 147488 | tf_op jit(solution)/shard_map/ppermute | solution.py:14
  94.5 4.8 %collective-permute-start.5 = (f32[2,16,576]{2,1,0:T(8,128)S(1)}, f32[2,16,576]{2,1,0:T(8,128)S(1)}, u32[]{:S(2)}, u32[]{:S(2)}) collective-permute-start(f32[2,16,576]{2,1,0:T(8,128)S(1)} %slice.49), channel_id=1, source_target_pairs={{16,0},{24,8},{32,16},{40,24},{48,32},{56,40},{64,48},{72,56},{80,... | collective-permute-start | bytes 221192 | tf_op jit(solution)/shard_map/ppermute | solution.py:14
  99.3 2.3 %multiply_convert_fusion = bf16[128,8,512]{2,0,1:T(8,128)(2,1)S(1)} fusion(f32[128,8,512]{2,0,1:T(8,128)} %fusion.21, bf16[128,8,512]{0,2,1:T(8,128)(2,1)S(1)} %fusion, bf16[512,576]{1,0:T(8,128)(2,1)S(1)} %bitcast.122), kind=kOutput, calls=%fused_computation.14 | convolution fusion | flops 538443776 | bytes 4718592 | tf_op jit(solution)/shard_map/thk,kc->thc/dot_general | solution.py:37
  101.7 4.0 %collective-permute-start.6 = (f32[16,576]{1,0:T(8,128)S(1)}, f32[16,576]{1,0:T(8,128)S(1)}, u32[]{:S(2)}, u32[]{:S(2)}) collective-permute-start(f32[16,576]{1,0:T(8,128)S(1)} %slice_bitcast_fusion.14), channel_id=1, source_target_pairs={{8,0},{16,8},{24,16},{32,24},{40,32},{48,40},{56,48},{64,56},{72,6... | collective-permute-start | bytes 110600 | tf_op jit(solution)/shard_map/ppermute | solution.py:14
  106.8 1.5 %copy.73 = bf16[128,8,512]{2,1,0:T(8,128)(2,1)} copy(bf16[128,8,512]{2,0,1:T(8,128)(2,1)S(1)} %multiply_convert_fusion) | data formatting | bytes 2097152
  (70 shorter events, 24.3 us)
Async XLA Ops:
  0.6 27.4 %copy-start.4 = (bf16[128,8,512]{2,1,0:T(8,128)(2,1)S(1)}, bf16[128,8,512]{2,1,0:T(8,128)(2,1)}, u32[]{:S(2)}) copy-start(bf16[128,8,512]{2,1,0:T(8,128)(2,1)} %param.11) | copy-start | bytes 3145732
  3.2 14.7 %collective-permute-start = (bf16[1,128,576]{2,1,0:T(8,128)(2,1)S(1)}, bf16[1,128,576]{2,1,0:T(8,128)(2,1)S(1)}, u32[]{:S(2)}, u32[]{:S(2)}) collective-permute-start(bf16[1,128,576]{2,1,0:T(8,128)(2,1)S(1)} %get-tuple-element.16), channel_id=1, source_target_pairs={{0,8},{8,16},{16,24},{24,32},{32,40},{40,48},{48,56},{56,64},{64,7... | collective-permute-start | bytes 442376 | tf_op jit(solution)/shard_map/ppermute | solution.py:14
  18.5 15.0 %collective-permute-start.3 = (bf16[2,16,576]{2,1,0:T(8,128)(2,1)}, bf16[2,16,576]{2,1,0:T(8,128)(2,1)S(1)}, u32[]{:S(2)}, u32[]{:S(2)}) collective-permute-start(bf16[2,16,576]{2,1,0:T(8,128)(2,1)} %fusion.25), channel_id=1, source_target_pairs={{0,32},{8,40},{16,48},{24,56},{32,64},{40,72},{48,80},{56,88},{64,... | collective-permute-start | bytes 110600 | tf_op jit(solution)/shard_map/ppermute | solution.py:14
  20.4 13.1 %collective-permute-start.2 = (bf16[2,16,576]{2,1,0:T(8,128)(2,1)}, bf16[2,16,576]{2,1,0:T(8,128)(2,1)}, u32[]{:S(2)}, u32[]{:S(2)}) collective-permute-start(bf16[2,16,576]{2,1,0:T(8,128)(2,1)} %fusion.25), channel_id=1, source_target_pairs={{0,48},{8,56},{16,64},{24,72},{32,80},{40,88},{48,96},{56,104},{64... | collective-permute-start | bytes 110600 | tf_op jit(solution)/shard_map/ppermute | solution.py:14
  24.1 7.6 %copy-start.5 = (bf16[128,8,512]{2,1,0:T(8,128)(2,1)S(1)}, bf16[128,8,512]{2,1,0:T(8,128)(2,1)}, u32[]{:S(2)}) copy-start(bf16[128,8,512]{2,1,0:T(8,128)(2,1)} %param.8) | copy-start | bytes 3145732
  24.1 17.0 %collective-permute-start.1 = (bf16[2,128,576]{2,1,0:T(8,128)(2,1)}, bf16[2,128,576]{2,1,0:T(8,128)(2,1)}, u32[]{:S(2)}, u32[]{:S(2)}) collective-permute-start(bf16[2,128,576]{2,1,0:T(8,128)(2,1)} %pad_maximum_fusion.3), channel_id=1, source_target_pairs={{0,16},{8,24},{16,32},{24,40},{32,48},{40,56},{48,64},{56,72},{64,... | collective-permute-start | bytes 884744 | tf_op jit(solution)/shard_map/ppermute | solution.py:14
  31.8 9.4 %copy-start.9 = (bf16[128,576]{1,0:T(8,128)(2,1)S(1)}, bf16[128,576]{1,0:T(8,128)(2,1)}, u32[]{:S(2)}) copy-start(bf16[128,576]{1,0:T(8,128)(2,1)} %get-tuple-element.17) | copy-start | bytes 442372
  35.2 14.8 %all-to-all-start = ((bf16[8,4,16,576]{3,2,1,0:T(8,128)(2,1)}), bf16[8,4,16,576]{3,2,1,0:T(8,128)(2,1)S(1)}, u32[]{:S(2)}, u32[]{:S(2)}) async-start(bf16[8,4,16,576]{3,2,1,0:T(8,128)(2,1)} %broadcast_in_dim.56), calls=%async_computation | async-start | bytes 1310720 | tf_op jit(solution)/shard_map/all_to_all | solution.py:90
  41.1 1.6 %copy-start.6 = (bf16[128,8,512]{0,2,1:T(8,128)(2,1)S(1)}, bf16[128,8,512]{0,2,1:T(8,128)(2,1)}, u32[]{:S(2)}) copy-start(bf16[128,8,512]{0,2,1:T(8,128)(2,1)} %copy.62) | copy-start | bytes 3145732
  41.1 1.6 %copy-start.10 = (pred[128,512]{0,1:T(8,128)(4,1)S(1)}, pred[128,512]{0,1:T(8,128)(4,1)}, u32[]{:S(2)}) copy-start(pred[128,512]{0,1:T(8,128)(4,1)} %get-tuple-element.21) | copy-start | bytes 196612
  41.2 1.6 %copy-start.11 = (f32[128,8]{0,1:T(8,128)S(1)}, f32[128,8]{0,1:T(8,128)}, u32[]{:S(2)}) copy-start(f32[128,8]{0,1:T(8,128)} %param.12) | copy-start | bytes 12292
  42.3 3.1 %copy-start.2 = (bf16[4,8,16,576]{3,2,0,1:T(8,128)(2,1)}, bf16[4,8,16,576]{3,2,0,1:T(8,128)(2,1)S(1)}, u32[]{:S(2)}) copy-start(bf16[4,8,16,576]{3,2,0,1:T(8,128)(2,1)S(1)} %pad_maximum_fusion.1) | copy-start | bytes 1769476
  50.1 0.8 copy-start
  50.1 1.5 %copy-start.7 = (bf16[128,8,512]{0,2,1:T(8,128)(2,1)S(1)}, bf16[128,8,512]{0,2,1:T(8,128)(2,1)}, u32[]{:S(2)}) copy-start(bf16[128,8,512]{0,2,1:T(8,128)(2,1)} %copy.62) | copy-start | bytes 3145732
  57.3 5.6 %copy-start.8 = (bf16[128,8,512]{0,2,1:T(8,128)(2,1)S(1)}, bf16[128,8,512]{0,2,1:T(8,128)(2,1)}, u32[]{:S(2)}) copy-start(bf16[128,8,512]{0,2,1:T(8,128)(2,1)} %copy.62) | copy-start | bytes 3145732
  57.3 14.0 %all-to-all-start.1 = ((bf16[8,4,16,576]{3,2,1,0:T(8,128)(2,1)}), bf16[8,4,16,576]{3,2,1,0:T(8,128)(2,1)}, u32[]{:S(2)}, u32[]{:S(2)}) async-start(bf16[8,4,16,576]{3,2,1,0:T(8,128)(2,1)} %bitcast.28), calls=%async_computation.1 | async-start | bytes 1310720 | tf_op jit(solution)/shard_map/all_to_all | solution.py:77
  64.9 14.7 %copy-start.3 = (bf16[4,8,16,576]{3,2,0,1:T(8,128)(2,1)S(1)}, bf16[4,8,16,576]{3,2,0,1:T(8,128)(2,1)}, u32[]{:S(2)}) copy-start(bf16[4,8,16,576]{3,2,0,1:T(8,128)(2,1)} %copy-done.2) | copy-start | bytes 1769476
  74.7 13.4 %all-to-all-start.2 = ((bf16[8,4,16,576]{3,2,1,0:T(8,128)(2,1)}), bf16[8,4,16,576]{3,2,1,0:T(8,128)(2,1)}, u32[]{:S(2)}, u32[]{:S(2)}) async-start(bf16[8,4,16,576]{3,2,1,0:T(8,128)(2,1)} %bitcast.133), calls=%async_computation.2 | async-start | bytes 1310720 | tf_op jit(solution)/shard_map/all_to_all | solution.py:77
  81.7 17.6 %copy-start.1 = (bf16[8,4,16,576]{3,2,1,0:T(8,128)(2,1)S(1)}, bf16[8,4,16,576]{3,2,1,0:T(8,128)(2,1)}, u32[]{:S(2)}) copy-start(bf16[8,4,16,576]{3,2,1,0:T(8,128)(2,1)} %copy-done) | copy-start | bytes 1769476
  81.7 12.8 %collective-permute-start.4 = (f32[4,16,576]{2,1,0:T(8,128)S(1)}, f32[4,16,576]{2,1,0:T(8,128)S(1)}, u32[]{:S(2)}, u32[]{:S(2)}) collective-permute-start(f32[4,16,576]{2,1,0:T(8,128)S(1)} %convert_reduce_fusion.1), channel_id=1, source_target_pairs={{32,0},{40,8},{48,16},{56,24},{64,32},{72,40},{80,48},{88,56},{96,... | collective-permute-start | bytes 442376 | tf_op jit(solution)/shard_map/ppermute | solution.py:14
  94.5 7.1 %collective-permute-start.5 = (f32[2,16,576]{2,1,0:T(8,128)S(1)}, f32[2,16,576]{2,1,0:T(8,128)S(1)}, u32[]{:S(2)}, u32[]{:S(2)}) collective-permute-start(f32[2,16,576]{2,1,0:T(8,128)S(1)} %slice.49), channel_id=1, source_target_pairs={{16,0},{24,8},{32,16},{40,24},{48,32},{56,40},{64,48},{72,56},{80,... | collective-permute-start | bytes 221192 | tf_op jit(solution)/shard_map/ppermute | solution.py:14
  101.7 6.7 %collective-permute-start.6 = (f32[16,576]{1,0:T(8,128)S(1)}, f32[16,576]{1,0:T(8,128)S(1)}, u32[]{:S(2)}, u32[]{:S(2)}) collective-permute-start(f32[16,576]{1,0:T(8,128)S(1)} %slice_bitcast_fusion.14), channel_id=1, source_target_pairs={{8,0},{16,8},{24,16},{32,24},{40,32},{48,40},{56,48},{64,56},{72,6... | collective-permute-start | bytes 110600 | tf_op jit(solution)/shard_map/ppermute | solution.py:14

commit v11 on v10

--- a/solution.py
+++ b/solution.py
@@ -97,9 +97,7 @@
     grad_qlat = softmax_scale * (near_qlat + far_qlat)
     grad_qrot = softmax_scale * (near_qrot + far_qrot)
 
-    far_sum = group_sum(far_part)
-    near_part, far_sum = lax.optimization_barrier((near_part, far_sum))
-    far_sum = shifted(far_sum, "ctx", -half_span)
+    far_sum = shifted(group_sum(far_part), "ctx", -half_span)
     part = group_sum(near_part) + far_sum
     width = half_span
     while width > 2:

time: 111 us -> 109 us (0.982)
  waiting for transfers between devices: 25.9 us -> 23.8 us
    all_to_all x2, waiting for transfers between devices: 5.89 us -> 3.43 us  [group_sum(): got = lax.all_to_all(part, 'head', 0, 0, tiled=True)]
    concatenate x1 -> x2, local copies, waits for them, and re-layouts: 1.08 us -> 3.26 us  [window_terms(): return (grad_qlat, grad_qrot, jnp.concatenate([grad_lat, grad_rot], axis=1))]
    convert_element_type x1 -> x0, local copies, waits for them, and re-layouts: 2.14 us -> none  [group_sum(): part = part.astype(jnp.bfloat16)]
  transfers between devices with their start and end apart: 10 -> 10, of which waited for: 5 -> 4; matrix products, arithmetic and copies ran while one was open for 25% -> 29% of each run, Pallas kernels for 0% -> 0%
where the time goes in v11:
time: 109 us; the launch traced here: 108 us
  starting transfers between devices  40.5 us (37%)
  waiting for transfers between devices  23.8 us (22%)
  matrix products  17.3 us (16%)
  other arithmetic  12.7 us (12%)
  local copies, waits for them, and re-layouts  12.5 us (11%)
    ppermute x7, starting transfers between devices, shifted(): return lax.ppermute(x, axis, pairs)  24.4 us
    ppermute x7, waiting for transfers between devices, shifted(): return lax.ppermute(x, axis, pairs)  16.5 us
    all_to_all x2, starting transfers between devices, group_sum(): got = lax.all_to_all(part, 'head', 0, 0, tiled=True)  10.1 us
    unnamed x30, local copies, waits for them, and re-layouts  8.06 us
    all_to_all x1, starting transfers between devices, assemble(): return lax.all_to_all(spread, 'head', 0, 0, tiled=True)  5.93 us
    dot_general x2, matrix products, window_terms(): jnp.einsum('thk,kc->thc', grad_b, lat_all, preferred_element_type=jnp.flo...  4.41 us
    all_to_all x1, waiting for transfers between devices, assemble(): return lax.all_to_all(spread, 'head', 0, 0, tiled=True)  3.87 us
    all_to_all x2, waiting for transfers between devices, group_sum(): got = lax.all_to_all(part, 'head', 0, 0, tiled=True)  3.43 us
  transfers between devices with their start and end apart: 10, of which 4 were waited for; matrix products, arithmetic and copies ran while one was open for 29% of the time, Pallas kernels for 0%

profile of v11, /device:TPU:6, one launch (start us, length us, event | category | flops | bytes accessed | tf_op | source)
XLA Modules:
  0.0 107.7 jit_solution(14186351394516468579)
XLA Ops:
  1.6 1.6 %fusion.32 = (bf16[1,128,576]{2,1,0:T(8,128)(2,1)S(1)}, bf16[128,576]{1,0:T(8,128)(2,1)}) fusion(bf16[128,64]{1,0:T(8,128)(2,1)S(1)} %copy.44, bf16[128,512]{1,0:T(8,128)(2,1)} %param.13), kind=kLoop, calls=%fused_computation.72 | loop fusion | flops 294912 | bytes 442368 | tf_op jit(solution)/shard_map/broadcast_in_dim | solution.py:80
  3.2 1.9 %collective-permute-start = (bf16[1,128,576]{2,1,0:T(8,128)(2,1)S(1)}, bf16[1,128,576]{2,1,0:T(8,128)(2,1)S(1)}, u32[]{:S(2)}, u32[]{:S(2)}) collective-permute-start(bf16[1,128,576]{2,1,0:T(8,128)(2,1)S(1)} %get-tuple-element.12), channel_id=1, source_target_pairs={{0,8},{8,16},{16,24},{24,32},{32,40},{40,48},{48,56},{56,64},{64,7... | collective-permute-start | bytes 442376 | tf_op jit(solution)/shard_map/ppermute | solution.py:14
  6.9 10.9 %collective-permute-done = bf16[1,128,576]{2,1,0:T(8,128)(2,1)S(1)} collective-permute-done((bf16[1,128,576]{2,1,0:T(8,128)(2,1)S(1)}, bf16[1,128,576]{2,1,0:T(8,128)(2,1)S(1)}, u32[]{:S(2)}, u32[]{:S(2)}) %collective-permute-start) | collective-permute-done | bytes 147488 | tf_op jit(solution)/shard_map/ppermute | solution.py:14
  18.5 1.9 %collective-permute-start.3 = (bf16[2,16,576]{2,1,0:T(8,128)(2,1)}, bf16[2,16,576]{2,1,0:T(8,128)(2,1)S(1)}, u32[]{:S(2)}, u32[]{:S(2)}) collective-permute-start(bf16[2,16,576]{2,1,0:T(8,128)(2,1)} %fusion.27), channel_id=1, source_target_pairs={{0,32},{8,40},{16,48},{24,56},{32,64},{40,72},{48,80},{56,88},{64,... | collective-permute-start | bytes 110600 | tf_op jit(solution)/shard_map/ppermute | solution.py:14
  20.4 3.0 %collective-permute-start.2 = (bf16[2,16,576]{2,1,0:T(8,128)(2,1)}, bf16[2,16,576]{2,1,0:T(8,128)(2,1)}, u32[]{:S(2)}, u32[]{:S(2)}) collective-permute-start(bf16[2,16,576]{2,1,0:T(8,128)(2,1)} %fusion.27), channel_id=1, source_target_pairs={{0,48},{8,56},{16,64},{24,72},{32,80},{40,88},{48,96},{56,104},{64... | collective-permute-start | bytes 110600 | tf_op jit(solution)/shard_map/ppermute | solution.py:14
  24.1 3.9 %collective-permute-start.1 = (bf16[2,128,576]{2,1,0:T(8,128)(2,1)}, bf16[2,128,576]{2,1,0:T(8,128)(2,1)}, u32[]{:S(2)}, u32[]{:S(2)}) collective-permute-start(bf16[2,128,576]{2,1,0:T(8,128)(2,1)} %pad_maximum_fusion.3), channel_id=1, source_target_pairs={{0,16},{8,24},{16,32},{24,40},{32,48},{40,56},{48,64},{56,72},{64,... | collective-permute-start | bytes 884744 | tf_op jit(solution)/shard_map/ppermute | solution.py:14
  28.1 1.6 %fusion.5 = f32[128,8]{1,0:T(8,128)S(1)} fusion(bf16[128,8,512]{2,1,0:T(8,128)(2,1)S(1)} %copy-done.4, bf16[128,8,512]{2,1,0:T(8,128)(2,1)} %param.10), kind=kLoop, calls=%fused_computation.9 | loop fusion | flops 2096128 | bytes 2101248
  31.8 1.7 %copy.62 = bf16[128,8,512]{0,2,1:T(8,128)(2,1)} copy(bf16[128,8,512]{2,1,0:T(8,128)(2,1)S(1)} %copy-done.5) | data formatting | bytes 2097152 | tf_op args[0]
  35.2 5.9 %all-to-all-start = ((bf16[8,4,16,576]{3,2,1,0:T(8,128)(2,1)}), bf16[8,4,16,576]{3,2,1,0:T(8,128)(2,1)S(1)}, u32[]{:S(2)}, u32[]{:S(2)}) async-start(bf16[8,4,16,576]{3,2,1,0:T(8,128)(2,1)} %broadcast_in_dim.56), calls=%async_computation | async-start | bytes 1310720 | tf_op jit(solution)/shard_map/all_to_all | solution.py:90
  43.7 1.7 %convolution_bitcast_fusion.2 = f32[512,512]{0,1:T(8,128)} fusion(bf16[128,8,512]{0,2,1:T(8,128)(2,1)S(1)} %copy.64, f32[128,8,512]{0,2,1:T(8,128)S(1)} %fusion.8), kind=kOutput, calls=%fused_computation.19 | convolution fusion | flops 537395200 | bytes 4194304 | tf_op jit(solution)/shard_map/thk,thc->kc/dot_general | solution.py:41
  46.2 3.9 %all-to-all-done = bf16[8,4,16,576]{3,2,1,0:T(8,128)(2,1)S(1)} async-done(((bf16[8,4,16,576]{3,2,1,0:T(8,128)(2,1)}), bf16[8,4,16,576]{3,2,1,0:T(8,128)(2,1)S(1)}, u32[]{:S(2)}, u32[]{:S(2)}) %all-to-all-start) | async-done | bytes 589856 | tf_op jit(solution)/shard_map/all_to_all | solution.py:90
  52.5 1.8 %fusion = bf16[128,8,512]{0,2,1:T(8,128)(2,1)S(1)} fusion(f32[128,8,512]{0,2,1:T(8,128)S(1)} %fusion.3, bf16[128,8,512]{0,2,1:T(8,128)(2,1)S(1)} %copy.64, f32[128,8]{0,1:T(8,128)S(1)} %copy.80, bf16[512,576]{1,0:T(8,128)(2,1)} %bitcast.125), kind=kOutput, calls=%fused_computation.1 | convolution fusion | flops 538443776 | bytes 4722688 | tf_op jit(solution)/shard_map/thc,kc->thk/dot_general | solution.py:33
  57.4 5.1 %all-to-all-start.2 = ((bf16[8,4,16,576]{3,2,1,0:T(8,128)(2,1)}), bf16[8,4,16,576]{3,2,1,0:T(8,128)(2,1)}, u32[]{:S(2)}, u32[]{:S(2)}) async-start(bf16[8,4,16,576]{3,2,1,0:T(8,128)(2,1)} %bitcast.29), calls=%async_computation.2 | async-start | bytes 1310720 | tf_op jit(solution)/shard_map/all_to_all | solution.py:77
  62.9 2.0 %fusion.13 = bf16[512,512]{0,1:T(8,128)(2,1)S(1)} fusion(f32[512,512]{0,1:T(8,128)} %convolution_bitcast_fusion.2, bf16[128,8,512]{0,2,1:T(8,128)(2,1)S(1)} %fusion.4, bf16[128,8,512]{0,2,1:T(8,128)(2,1)S(1)} %copy-done.8), kind=kOutput, calls=%fused_computation.25 | convolution fusion | flops 537657344 | bytes 3670016 | tf_op jit(solution)/shard_map/thk,thc->kc/dot_general | solution.py:39
  65.8 2.1 %copy.66 = bf16[512,576]{1,0:T(8,128)(2,1)} copy(bf16[512,576]{0,1:T(8,128)(2,1)} %pad_maximum_fusion.1) | data formatting | bytes 1179648 | tf_op jit(solution)/shard_map/concatenate | solution.py:45
  67.9 3.4 %all-to-all-done.2 = bf16[8,4,16,576]{3,2,1,0:T(8,128)(2,1)} async-done(((bf16[8,4,16,576]{3,2,1,0:T(8,128)(2,1)}), bf16[8,4,16,576]{3,2,1,0:T(8,128)(2,1)}, u32[]{:S(2)}, u32[]{:S(2)}) %all-to-all-start.2) | async-done | bytes 589856 | tf_op jit(solution)/shard_map/all_to_all | solution.py:77
  71.3 5.0 %all-to-all-start.1 = ((bf16[8,4,16,576]{3,2,1,0:T(8,128)(2,1)}), bf16[8,4,16,576]{3,2,1,0:T(8,128)(2,1)}, u32[]{:S(2)}, u32[]{:S(2)}) async-start(bf16[8,4,16,576]{3,2,1,0:T(8,128)(2,1)} %bitcast.137), calls=%async_computation.1 | async-start | bytes 1310720 | tf_op jit(solution)/shard_map/all_to_all | solution.py:77
  76.3 2.1 %fusion.23 = f32[128,8,512]{2,0,1:T(8,128)} fusion(bf16[128,8,512]{0,2,1:T(8,128)(2,1)S(1)} %fusion.4, bf16[512,576]{1,0:T(8,128)(2,1)S(1)} %bitcast.132), kind=kOutput, calls=%fused_computation.46 | convolution fusion | flops 536870912 | bytes 3670016 | tf_op jit(solution)/shard_map/thk,kc->thc/dot_general | solution.py:37
  79.7 4.6 %collective-permute-start.4 = (f32[4,16,576]{2,1,0:T(8,128)S(1)}, f32[4,16,576]{2,1,0:T(8,128)S(1)}, u32[]{:S(2)}, u32[]{:S(2)}) collective-permute-start(f32[4,16,576]{2,1,0:T(8,128)S(1)} %convert_reduce_fusion), channel_id=1, source_target_pairs={{32,0},{40,8},{48,16},{56,24},{64,32},{72,40},{80,48},{88,56},{96,... | collective-permute-start | bytes 442376 | tf_op jit(solution)/shard_map/ppermute | solution.py:14
  86.7 5.6 %collective-permute-done.4 = f32[4,16,576]{2,1,0:T(8,128)S(1)} collective-permute-done((f32[4,16,576]{2,1,0:T(8,128)S(1)}, f32[4,16,576]{2,1,0:T(8,128)S(1)}, u32[]{:S(2)}, u32[]{:S(2)}) %collective-permute-start.4) | collective-permute-done | bytes 147488 | tf_op jit(solution)/shard_map/ppermute | solution.py:14
  92.3 4.8 %collective-permute-start.5 = (f32[2,16,576]{2,1,0:T(8,128)S(1)}, f32[2,16,576]{2,1,0:T(8,128)S(1)}, u32[]{:S(2)}, u32[]{:S(2)}) collective-permute-start(f32[2,16,576]{2,1,0:T(8,128)S(1)} %slice.49), channel_id=1, source_target_pairs={{16,0},{24,8},{32,16},{40,24},{48,32},{56,40},{64,48},{72,56},{80,... | collective-permute-start | bytes 221192 | tf_op jit(solution)/shard_map/ppermute | solution.py:14
  97.1 2.3 %multiply_convert_fusion = bf16[128,8,512]{2,0,1:T(8,128)(2,1)S(1)} fusion(f32[128,8,512]{2,0,1:T(8,128)} %fusion.23, bf16[128,8,512]{0,2,1:T(8,128)(2,1)S(1)} %fusion, bf16[512,576]{1,0:T(8,128)(2,1)S(1)} %bitcast.126), kind=kOutput, calls=%fused_computation.14 | convolution fusion | flops 538443776 | bytes 4718592 | tf_op jit(solution)/shard_map/thk,kc->thc/dot_general | solution.py:37
  99.5 4.3 %collective-permute-start.6 = (f32[16,576]{1,0:T(8,128)S(1)}, f32[16,576]{1,0:T(8,128)S(1)}, u32[]{:S(2)}, u32[]{:S(2)}) collective-permute-start(f32[16,576]{1,0:T(8,128)S(1)} %slice_bitcast_fusion.14), channel_id=1, source_target_pairs={{8,0},{16,8},{24,16},{32,24},{40,32},{48,40},{56,48},{64,56},{72,6... | collective-permute-start | bytes 110600 | tf_op jit(solution)/shard_map/ppermute | solution.py:14
  105.0 1.5 %copy.73 = bf16[128,8,512]{2,1,0:T(8,128)(2,1)} copy(bf16[128,8,512]{2,0,1:T(8,128)(2,1)S(1)} %multiply_convert_fusion) | data formatting | bytes 2097152
  (70 shorter events, 24.0 us)
Async XLA Ops:
  0.6 27.4 %copy-start.4 = (bf16[128,8,512]{2,1,0:T(8,128)(2,1)S(1)}, bf16[128,8,512]{2,1,0:T(8,128)(2,1)}, u32[]{:S(2)}) copy-start(bf16[128,8,512]{2,1,0:T(8,128)(2,1)} %param.11) | copy-start | bytes 3145732
  3.2 14.7 %collective-permute-start = (bf16[1,128,576]{2,1,0:T(8,128)(2,1)S(1)}, bf16[1,128,576]{2,1,0:T(8,128)(2,1)S(1)}, u32[]{:S(2)}, u32[]{:S(2)}) collective-permute-start(bf16[1,128,576]{2,1,0:T(8,128)(2,1)S(1)} %get-tuple-element.12), channel_id=1, source_target_pairs={{0,8},{8,16},{16,24},{24,32},{32,40},{40,48},{48,56},{56,64},{64,7... | collective-permute-start | bytes 442376 | tf_op jit(solution)/shard_map/ppermute | solution.py:14
  18.5 15.0 %collective-permute-start.3 = (bf16[2,16,576]{2,1,0:T(8,128)(2,1)}, bf16[2,16,576]{2,1,0:T(8,128)(2,1)S(1)}, u32[]{:S(2)}, u32[]{:S(2)}) collective-permute-start(bf16[2,16,576]{2,1,0:T(8,128)(2,1)} %fusion.27), channel_id=1, source_target_pairs={{0,32},{8,40},{16,48},{24,56},{32,64},{40,72},{48,80},{56,88},{64,... | collective-permute-start | bytes 110600 | tf_op jit(solution)/shard_map/ppermute | solution.py:14
  20.4 13.1 %collective-permute-start.2 = (bf16[2,16,576]{2,1,0:T(8,128)(2,1)}, bf16[2,16,576]{2,1,0:T(8,128)(2,1)}, u32[]{:S(2)}, u32[]{:S(2)}) collective-permute-start(bf16[2,16,576]{2,1,0:T(8,128)(2,1)} %fusion.27), channel_id=1, source_target_pairs={{0,48},{8,56},{16,64},{24,72},{32,80},{40,88},{48,96},{56,104},{64... | collective-permute-start | bytes 110600 | tf_op jit(solution)/shard_map/ppermute | solution.py:14
  24.1 7.6 %copy-start.5 = (bf16[128,8,512]{2,1,0:T(8,128)(2,1)S(1)}, bf16[128,8,512]{2,1,0:T(8,128)(2,1)}, u32[]{:S(2)}) copy-start(bf16[128,8,512]{2,1,0:T(8,128)(2,1)} %param.8) | copy-start | bytes 3145732
  24.1 17.0 %collective-permute-start.1 = (bf16[2,128,576]{2,1,0:T(8,128)(2,1)}, bf16[2,128,576]{2,1,0:T(8,128)(2,1)}, u32[]{:S(2)}, u32[]{:S(2)}) collective-permute-start(bf16[2,128,576]{2,1,0:T(8,128)(2,1)} %pad_maximum_fusion.3), channel_id=1, source_target_pairs={{0,16},{8,24},{16,32},{24,40},{32,48},{40,56},{48,64},{56,72},{64,... | collective-permute-start | bytes 884744 | tf_op jit(solution)/shard_map/ppermute | solution.py:14
  31.8 9.4 %copy-start.9 = (bf16[128,576]{1,0:T(8,128)(2,1)S(1)}, bf16[128,576]{1,0:T(8,128)(2,1)}, u32[]{:S(2)}) copy-start(bf16[128,576]{1,0:T(8,128)(2,1)} %get-tuple-element.13) | copy-start | bytes 442372
  35.2 14.8 %all-to-all-start = ((bf16[8,4,16,576]{3,2,1,0:T(8,128)(2,1)}), bf16[8,4,16,576]{3,2,1,0:T(8,128)(2,1)S(1)}, u32[]{:S(2)}, u32[]{:S(2)}) async-start(bf16[8,4,16,576]{3,2,1,0:T(8,128)(2,1)} %broadcast_in_dim.56), calls=%async_computation | async-start | bytes 1310720 | tf_op jit(solution)/shard_map/all_to_all | solution.py:90
  41.1 1.6 %copy-start.6 = (bf16[128,8,512]{0,2,1:T(8,128)(2,1)S(1)}, bf16[128,8,512]{0,2,1:T(8,128)(2,1)}, u32[]{:S(2)}) copy-start(bf16[128,8,512]{0,2,1:T(8,128)(2,1)} %copy.62) | copy-start | bytes 3145732
  41.1 1.6 %copy-start.10 = (pred[128,512]{0,1:T(8,128)(4,1)S(1)}, pred[128,512]{0,1:T(8,128)(4,1)}, u32[]{:S(2)}) copy-start(pred[128,512]{0,1:T(8,128)(4,1)} %get-tuple-element.17) | copy-start | bytes 196612
  41.2 1.6 %copy-start.11 = (f32[128,8]{0,1:T(8,128)S(1)}, f32[128,8]{0,1:T(8,128)}, u32[]{:S(2)}) copy-start(f32[128,8]{0,1:T(8,128)} %param.12) | copy-start | bytes 12292
  42.3 3.1 %copy-start.2 = (bf16[4,8,16,576]{3,2,0,1:T(8,128)(2,1)}, bf16[4,8,16,576]{3,2,0,1:T(8,128)(2,1)S(1)}, u32[]{:S(2)}) copy-start(bf16[4,8,16,576]{3,2,0,1:T(8,128)(2,1)S(1)} %pad_maximum_fusion) | copy-start | bytes 1769476
  50.1 0.8 copy-start
  50.1 1.5 %copy-start.7 = (bf16[128,8,512]{0,2,1:T(8,128)(2,1)S(1)}, bf16[128,8,512]{0,2,1:T(8,128)(2,1)}, u32[]{:S(2)}) copy-start(bf16[128,8,512]{0,2,1:T(8,128)(2,1)} %copy.62) | copy-start | bytes 3145732
  57.4 5.6 %copy-start.8 = (bf16[128,8,512]{0,2,1:T(8,128)(2,1)S(1)}, bf16[128,8,512]{0,2,1:T(8,128)(2,1)}, u32[]{:S(2)}) copy-start(bf16[128,8,512]{0,2,1:T(8,128)(2,1)} %copy.62) | copy-start | bytes 3145732
  57.4 14.0 %all-to-all-start.2 = ((bf16[8,4,16,576]{3,2,1,0:T(8,128)(2,1)}), bf16[8,4,16,576]{3,2,1,0:T(8,128)(2,1)}, u32[]{:S(2)}, u32[]{:S(2)}) async-start(bf16[8,4,16,576]{3,2,1,0:T(8,128)(2,1)} %bitcast.29), calls=%async_computation.2 | async-start | bytes 1310720 | tf_op jit(solution)/shard_map/all_to_all | solution.py:77
  64.9 11.4 %copy-start.3 = (bf16[4,8,16,576]{3,2,0,1:T(8,128)(2,1)S(1)}, bf16[4,8,16,576]{3,2,0,1:T(8,128)(2,1)}, u32[]{:S(2)}) copy-start(bf16[4,8,16,576]{3,2,0,1:T(8,128)(2,1)} %copy-done.2) | copy-start | bytes 1769476
  71.3 14.2 %all-to-all-start.1 = ((bf16[8,4,16,576]{3,2,1,0:T(8,128)(2,1)}), bf16[8,4,16,576]{3,2,1,0:T(8,128)(2,1)}, u32[]{:S(2)}, u32[]{:S(2)}) async-start(bf16[8,4,16,576]{3,2,1,0:T(8,128)(2,1)} %bitcast.137), calls=%async_computation.1 | async-start | bytes 1310720 | tf_op jit(solution)/shard_map/all_to_all | solution.py:77
  78.4 18.7 %copy-start.1 = (bf16[8,4,16,576]{3,2,1,0:T(8,128)(2,1)S(1)}, bf16[8,4,16,576]{3,2,1,0:T(8,128)(2,1)}, u32[]{:S(2)}) copy-start(bf16[8,4,16,576]{3,2,1,0:T(8,128)(2,1)} %copy-done) | copy-start | bytes 1769476
  79.7 12.6 %collective-permute-start.4 = (f32[4,16,576]{2,1,0:T(8,128)S(1)}, f32[4,16,576]{2,1,0:T(8,128)S(1)}, u32[]{:S(2)}, u32[]{:S(2)}) collective-permute-start(f32[4,16,576]{2,1,0:T(8,128)S(1)} %convert_reduce_fusion), channel_id=1, source_target_pairs={{32,0},{40,8},{48,16},{56,24},{64,32},{72,40},{80,48},{88,56},{96,... | collective-permute-start | bytes 442376 | tf_op jit(solution)/shard_map/ppermute | solution.py:14
  92.3 7.1 %collective-permute-start.5 = (f32[2,16,576]{2,1,0:T(8,128)S(1)}, f32[2,16,576]{2,1,0:T(8,128)S(1)}, u32[]{:S(2)}, u32[]{:S(2)}) collective-permute-start(f32[2,16,576]{2,1,0:T(8,128)S(1)} %slice.49), channel_id=1, source_target_pairs={{16,0},{24,8},{32,16},{40,24},{48,32},{56,40},{64,48},{72,56},{80,... | collective-permute-start | bytes 221192 | tf_op jit(solution)/shard_map/ppermute | solution.py:14
  99.5 7.0 %collective-permute-start.6 = (f32[16,576]{1,0:T(8,128)S(1)}, f32[16,576]{1,0:T(8,128)S(1)}, u32[]{:S(2)}, u32[]{:S(2)}) collective-permute-start(f32[16,576]{1,0:T(8,128)S(1)} %slice_bitcast_fusion.14), channel_id=1, source_target_pairs={{8,0},{16,8},{24,16},{32,24},{40,32},{48,40},{56,48},{64,56},{72,6... | collective-permute-start | bytes 110600 | tf_op jit(solution)/shard_map/ppermute | solution.py:14
